TPU v7x, 1024 devices: a whole 8x8x8 slice. The times are simulated.
1024 devices in a mesh: calls: 32 (over y_hi, z, core), ctx: 32 (over x, y_lo).
Axes of the slice: x: 8, y: 8 (y_hi: 2, y_lo: 4; y = y_hi * 4 + y_lo), z: 8, core: 2. Of those that a mesh axis runs over, the one named last changes fastest.
Arguments:
- frames_in: bfloat16 [32, 4096, 1024], P('calls', 'ctx'), may hold values from -12 to 12
- w_qkv: bfloat16 [1024, 1536], replicated, may hold values from -1 to 1
- out_grad: bfloat16 [32, 4096, 512], P('calls', 'ctx'), may hold values from -6 to 6
- lengths: int32 [32], P('calls'), may hold values from 2048 to 4096, as said below
Outputs:
- context: bfloat16 [32, 4096, 512], P('calls', 'ctx')
- in_grad: bfloat16 [32, 4096, 1024], P('calls', 'ctx')
- weight_grad: float32 [1024, 1536], P('calls', 'ctx')
Inputs may be any that keep to these rules, and one draw needn't show every extreme that they name: Frames at and beyond lengths[c] are padding of call c; some call has all 4096 frames valid.
All inputs are finite; a program needn't handle non-finite values.
Results may differ from a plain program's by a relative error of at most 0.012.
The roundings to bfloat16 on the way count: a program that leaves them out, or rounds other values in their place, can miss the bound.
Values may be sent and summed in bfloat16 or wider, within the bound.
No kernel may reach another device: no remote copies, remote signals or barrier semaphores. Data moves between devices by JAX's collectives and lax.ppermute only.
A program may use at most 64 MiB of HBM per device.

v0:
```python
import math

import jax
import jax.numpy as jnp
from jax import lax
from jax.sharding import PartitionSpec as P

HEADS = 4
WIN = 128


def with_halo(cells, sides, width):
    for axis, dim in sides:
        count = lax.axis_size(axis)
        ends = count - 1
        head = lax.slice_in_dim(cells, 0, width, axis=dim)
        tail = lax.slice_in_dim(cells, cells.shape[dim] - width, cells.shape[dim], axis=dim)
        cells = jnp.concatenate(
            [
                lax.ppermute(tail, axis, [(i, (i + 1) % count) for i in range(ends)]),
                cells,
                lax.ppermute(head, axis, [((i + 1) % count, i) for i in range(ends)]),
            ],
            axis=dim,
        )
    return cells


def band_mask(query_pos, key_pos, length_now):
    gap = jnp.abs(query_pos[:, None] - key_pos[None, :])
    inside = (gap <= WIN) & (key_pos[None, :] >= 0) & (key_pos[None, :] < length_now)
    return inside | (query_pos[:, None] == key_pos[None, :])


def attend(queries, key_value, cotangent, allowed, living):
    frame_count, inner_width = queries.shape
    head_size = inner_width // HEADS
    key_span = key_value.shape[0]
    factor = 1.0 / math.sqrt(head_size)
    query_heads = queries.reshape(frame_count, HEADS, head_size)
    key_heads = key_value[:, :inner_width].reshape(key_span, HEADS, head_size)
    value_heads = key_value[:, inner_width:].reshape(key_span, HEADS, head_size)
    cot_heads = cotangent.reshape(frame_count, HEADS, head_size)
    scores = (
        jnp.einsum("fhd,shd->hfs", query_heads, key_heads, preferred_element_type=jnp.float32)
        * factor
    )
    scores = jnp.where(allowed[None], scores, -jnp.inf)
    maxima = jnp.max(scores, axis=-1, keepdims=True)
    shifted = jnp.exp(scores - maxima)
    totals = jnp.sum(shifted, axis=-1, keepdims=True)
    weights = shifted / totals
    rounded = weights.astype(jnp.bfloat16)
    context = jnp.einsum("hfs,shd->fhd", rounded, value_heads, preferred_element_type=jnp.float32)
    context = (
        (context * living[:, None, None]).reshape(frame_count, inner_width).astype(jnp.bfloat16)
    )
    grad_probs = jnp.einsum(
        "fhd,shd->hfs", cot_heads, value_heads, preferred_element_type=jnp.float32
    )
    centre_term = jnp.sum(grad_probs * weights, axis=-1, keepdims=True)
    grad_scores = (weights * (grad_probs - centre_term) * factor).astype(jnp.bfloat16)
    grad_query = jnp.einsum(
        "hfs,shd->fhd", grad_scores, key_heads, preferred_element_type=jnp.float32
    )
    grad_key = jnp.einsum(
        "hfs,fhd->shd", grad_scores, query_heads, preferred_element_type=jnp.float32
    )
    grad_value = jnp.einsum("hfs,fhd->shd", rounded, cot_heads, preferred_element_type=jnp.float32)
    grad_query = grad_query.reshape(frame_count, inner_width).astype(jnp.bfloat16)
    grad_terms = jnp.concatenate(
        [grad_key.reshape(key_span, inner_width), grad_value.reshape(key_span, inner_width)], axis=1
    )
    return (context, grad_query, grad_terms)


def body(frames_in, w_qkv, out_grad, lengths):
    frame_rows = frames_in[0]
    frame_count, model_width = frame_rows.shape
    inner_width = w_qkv.shape[1] // 3
    window = WIN
    offset = lax.axis_index("ctx") * frame_count
    length_now = lengths[0]
    qkv = jnp.dot(frame_rows, w_qkv, preferred_element_type=jnp.float32).astype(jnp.bfloat16)
    queries = qkv[:, :inner_width]
    key_value = with_halo(qkv[:, inner_width:], (("ctx", 0),), window)
    query_pos = offset + jnp.arange(frame_count, dtype=jnp.int32)
    key_pos = offset - window + jnp.arange(frame_count + 2 * window, dtype=jnp.int32)
    allowed = band_mask(query_pos, key_pos, length_now)
    live_rows = query_pos < length_now
    living = live_rows.astype(jnp.float32)
    cotangent = jnp.where(live_rows[:, None], out_grad[0], jnp.zeros_like(out_grad[0]))
    context, grad_query, grad_terms = attend(queries, key_value, cotangent, allowed, living)
    own_part = grad_terms[window : window + frame_count]
    rim_part = jnp.concatenate(
        [grad_terms[:window], grad_terms[window + frame_count :]], axis=0
    ).astype(jnp.bfloat16)
    returned = with_halo(rim_part, (("ctx", 0),), window)
    from_left = returned[:window].astype(jnp.float32)
    from_right = returned[3 * window :].astype(jnp.float32)
    summed = own_part + from_left
    summed = summed + from_right
    grad_kv = summed.astype(jnp.bfloat16)
    grad_all = jnp.concatenate([grad_query, grad_kv], axis=1)
    in_grad = lax.dot_general(
        grad_all, w_qkv, (((1,), (1,)), ((), ())), preferred_element_type=jnp.float32
    ).astype(jnp.bfloat16)
    term = lax.dot_general(
        frame_rows, grad_all, (((0,), (0,)), ((), ())), preferred_element_type=jnp.float32
    )
    partial_grad = lax.psum_scatter(term, "calls", scatter_dimension=0, tiled=True)
    weight_grad = lax.psum_scatter(partial_grad, "ctx", scatter_dimension=1, tiled=True)
    return (context[None], in_grad[None], weight_grad)


def solution(mesh):
    in_specs = (P("calls", "ctx", None), P(), P("calls", "ctx", None), P("calls"))
    out_specs = (P("calls", "ctx", None), P("calls", "ctx", None), P("calls", "ctx"))
    return jax.shard_map(body, mesh=mesh, in_specs=in_specs, out_specs=out_specs, check_vma=False)
```

profile of v0, /device:TPU:118, one launch (start us, length us, event | category | flops | bytes accessed | tf_op | source)
XLA Modules:
  0.0 432.8 jit_solution(9018198243197125222)
XLA Ops:
  7.2 1.8 copy-done
  9.1 1.5 convolution_convert_fusion
  11.3 3.1 collective-permute-start.1
  14.5 6.6 %collective-permute-start = (bf16[128,1024]{1,0:T(8,128)(2,1)}, bf16[128,1024]{1,0:T(8,128)(2,1)}, u32[]{:S(2)}, u32[]{:S(2)}) collective-permute-start(bf16[128,1024]{1,0:T(8,128)(2,1)} %slice.32), channel_id=1, source_target_pairs={{0,1},{1,2},{2,3},{3,4},{4,5},{5,6},{6,7},{7,8},{8,9},{9,10},{10,1... | collective-permute-start | bytes 786440 | tf_op jit(solution)/shard_map/ppermute | solution.py:20
  23.5 1.7 copy.28
  25.2 1.7 copy.31
  28.3 1.8 collective-permute-done
  33.0 2.3 fusion.22
  35.3 2.3 fusion.54
  37.7 2.6 fusion.30
  40.3 5.4 %fusion.12 = f32[4,128,384]{2,1,0:T(8,128)} fusion(bf16[128,4,128]{0,2,1:T(8,128)(2,1)S(1)} %bitcast.60, f32[4,128,384]{2,1,0:T(8,128)} %fusion.22, f32[4,128,384]{2,1,0:T(8,128)} %get-tuple-element.16, f32[4,128]{1,0:T(4,128)S(1)} %get-tuple-element.15), kind=kOutput, calls=%fused_computation.21 | convolution fusion | flops 51708800 | bytes 2492416 | tf_op jit(solution)/shard_map/hfs,fhd->shd/dot_general | solution.py:66
  45.7 1.5 fusion.2
  47.9 4.9 %collective-permute-start.2 = (bf16[128,1024]{0,1:T(8,128)(2,1)}, bf16[128,1024]{0,1:T(8,128)(2,1)S(1)}, u32[]{:S(2)}, u32[]{:S(2)}) collective-permute-start(bf16[128,1024]{0,1:T(8,128)(2,1)} %get-tuple-element.11), channel_id=1, source_target_pairs={{0,1},{1,2},{2,3},{3,4},{4,5},{5,6},{6,7},{7,8},{8,9},{9,10},{10,1... | collective-permute-start | bytes 786440 | tf_op jit(solution)/shard_map/ppermute | solution.py:20
  52.8 1.9 collective-permute-start.3
  54.8 4.5 %convolution_convert_fusion.2 = bf16[4,128,128]{2,1,0:T(8,128)(2,1)S(1)} fusion(bf16[384,4,128]{0,2,1:T(8,128)(2,1)} %bitcast.55, f32[4,128,384]{2,1,0:T(8,128)} %fusion.22, f32[4,128,384]{2,1,0:T(8,128)} %get-tuple-element.16, f32[4,128]{1,0:T(4,128)S(1)} %get-tuple-element.15), kind=kOutput, calls=%fused_computation.20 | convolution fusion | flops 51774336 | bytes 2099200 | tf_op jit(solution)/shard_map/hfs,shd->fhd/dot_general | solution.py:63
  60.0 5.5 %collective-permute-done.3 = bf16[128,1024]{0,1:T(8,128)(2,1)} collective-permute-done((bf16[128,1024]{0,1:T(8,128)(2,1)}, bf16[128,1024]{0,1:T(8,128)(2,1)}, u32[]{:S(2)}, u32[]{:S(2)}) %collective-permute-start.3) | collective-permute-done | bytes 262176 | tf_op jit(solution)/shard_map/ppermute | solution.py:22
  66.8 4.6 %convolution_bitcast_fusion = f32[1024,1536]{0,1:T(8,128)} fusion(bf16[1,128,1024]{2,1,0:T(8,128)(2,1)} %param.4, bf16[128,1024]{0,1:T(8,128)(2,1)S(1)} %fusion.20, bf16[128,512]{0,1:T(8,128)(2,1)S(1)} %bitcast.49), kind=kOutput, calls=%fused_computation.2 | convolution fusion | flops 403439616 | bytes 6946816 | tf_op jit(solution)/shard_map/dot_general | solution.py:108
  71.4 6.6 %copy.29 = f32[1024,1536]{1,0:T(8,128)} copy(f32[1024,1536]{0,1:T(8,128)} %convolution_bitcast_fusion) | data formatting | bytes 12582912
  78.1 181.5 %reduce-scatter.7.cloned.1.call-done = f32[32,1536]{1,0:T(8,128)} async-done(((f32[1024,1536]{1,0:T(8,128)}), f32[32,1536]{1,0:T(8,128)}) %reduce-scatter.7.cloned.1.call-update) | async-done | bytes 196624
  259.5 2.1 copy.30
  261.6 2.5 fusion.11
  264.2 1.7 copy.25
  265.8 1.9 fusion.10
  267.7 156.8 %reduce-scatter.5.cloned.1.call-done = f32[32,48]{0,1:T(8,128)} async-done(((f32[32,1536]{0,1:T(8,128)}), f32[32,48]{0,1:T(8,128)}) %reduce-scatter.5.cloned.1.call-update) | async-done | bytes 6160 | tf_op jit(solution)/shard_map/reduce_scatter | solution.py:112
  (26 shorter events, 11.2 us)
Async XLA Ops:
  7.2 1.9 copy-start
  7.2 252.4 %reduce-scatter.7.cloned.1.call-start = ((), (), s32[]{:S(2)}) async-start(), calls=%async_computation.3 | async-start | bytes 6488064
  11.3 16.9 %collective-permute-start.1 = (bf16[128,1024]{1,0:T(8,128)(2,1)}, bf16[128,1024]{1,0:T(8,128)(2,1)}, u32[]{:S(2)}, u32[]{:S(2)}) collective-permute-start(bf16[128,1024]{1,0:T(8,128)(2,1)} %slice.32), channel_id=1, source_target_pairs={{1,0},{2,1},{3,2},{4,3},{5,4},{6,5},{7,6},{8,7},{9,8},{10,9},{11,1... | collective-permute-start | bytes 786440 | tf_op jit(solution)/shard_map/ppermute | solution.py:22
  14.5 15.6 %collective-permute-start = (bf16[128,1024]{1,0:T(8,128)(2,1)}, bf16[128,1024]{1,0:T(8,128)(2,1)}, u32[]{:S(2)}, u32[]{:S(2)}) collective-permute-start(bf16[128,1024]{1,0:T(8,128)(2,1)} %slice.32), channel_id=1, source_target_pairs={{0,1},{1,2},{2,3},{3,4},{4,5},{5,6},{6,7},{7,8},{8,9},{9,10},{10,1... | collective-permute-start | bytes 786440 | tf_op jit(solution)/shard_map/ppermute | solution.py:20
  33.0 7.3 %copy-start.2 = (bf16[128,512]{0,1:T(8,128)(2,1)S(1)}, bf16[128,512]{0,1:T(8,128)(2,1)}, u32[]{:S(2)}) copy-start(bf16[128,512]{0,1:T(8,128)(2,1)} %copy.31) | copy-start | bytes 393220
  47.9 11.4 %collective-permute-start.2 = (bf16[128,1024]{0,1:T(8,128)(2,1)}, bf16[128,1024]{0,1:T(8,128)(2,1)S(1)}, u32[]{:S(2)}, u32[]{:S(2)}) collective-permute-start(bf16[128,1024]{0,1:T(8,128)(2,1)} %get-tuple-element.11), channel_id=1, source_target_pairs={{0,1},{1,2},{2,3},{3,4},{4,5},{5,6},{6,7},{7,8},{8,9},{9,10},{10,1... | collective-permute-start | bytes 786440 | tf_op jit(solution)/shard_map/ppermute | solution.py:20
  52.8 12.7 %collective-permute-start.3 = (bf16[128,1024]{0,1:T(8,128)(2,1)}, bf16[128,1024]{0,1:T(8,128)(2,1)}, u32[]{:S(2)}, u32[]{:S(2)}) collective-permute-start(bf16[128,1024]{0,1:T(8,128)(2,1)} %get-tuple-element.12), channel_id=1, source_target_pairs={{1,0},{2,1},{3,2},{4,3},{5,4},{6,5},{7,6},{8,7},{9,8},{10,9},{11,1... | collective-permute-start | bytes 786440 | tf_op jit(solution)/shard_map/ppermute | solution.py:22
  59.3 0.7 copy-start.1
  78.0 183.6 %copy-start.3 = (f32[128]{0:T(128)S(1)}, f32[128]{0:T(128)}, u32[]{:S(2)}) copy-start(f32[128]{0:T(128)} %get-tuple-element.9) | copy-start | bytes 1540
  78.0 346.5 %reduce-scatter.5.cloned.1.call-start = ((), (), s32[]{:S(2)}) async-start(), calls=%async_computation.2 | async-start | bytes 811008 | tf_op jit(solution)/shard_map/reduce_scatter | solution.py:112
Sparse Core Ops, SparseCore 0:
  78.1 181.3 reduce-scatter.6
  262.9 161.5 reduce-scatter.4
where the time goes:
time: 434 us; the launch traced here: 433 us
  waiting for transfers between devices  346 us (80%)
  matrix products  27.7 us (6%)
  local copies, waits for them, and re-layouts  21.6 us (5%)
  starting transfers between devices  16.6 us (4%)
  between operations  14.8 us (3%)
  other arithmetic  6.44 us (1%)
    unnamed x3, waiting for transfers between devices  181 us
    reduce_scatter x1, waiting for transfers between devices, body(): lax.psum_scatter(partial_grad, 'ctx', scatter_dimension=1, tiled=True)  157 us
    unnamed x12, local copies, waits for them, and re-layouts  14.3 us
    ppermute x2, starting transfers between devices, with_halo(): lax.ppermute(tail, axis, [(i, (i + 1) % count) for i in range(ends)])  11.5 us
  transfers between devices with their start and end apart: 6, of which 4 were waited for; matrix products, arithmetic and copies ran while one was open for 4% of the time, Pallas kernels for 0%

commit v1 on v0

--- a/solution.py
+++ b/solution.py
@@ -105,11 +105,18 @@
     in_grad = lax.dot_general(
         grad_all, w_qkv, (((1,), (1,)), ((), ())), preferred_element_type=jnp.float32
     ).astype(jnp.bfloat16)
-    term = lax.dot_general(
-        frame_rows, grad_all, (((0,), (0,)), ((), ())), preferred_element_type=jnp.float32
-    )
-    partial_grad = lax.psum_scatter(term, "calls", scatter_dimension=0, tiled=True)
-    weight_grad = lax.psum_scatter(partial_grad, "ctx", scatter_dimension=1, tiled=True)
+    row_blocks = lax.axis_size("calls")
+    col_blocks = lax.axis_size("ctx")
+    row_width = model_width // row_blocks
+    col_width = grad_all.shape[1] // col_blocks
+    term = jnp.einsum(
+        "fas,fbt->abst",
+        frame_rows.reshape(frame_count, row_blocks, row_width),
+        grad_all.reshape(frame_count, col_blocks, col_width),
+        preferred_element_type=jnp.float32,
+    ).reshape(row_blocks * col_blocks, row_width * col_width)
+    weight_grad = lax.psum_scatter(term, ("calls", "ctx"), scatter_dimension=0, tiled=True)
+    weight_grad = weight_grad.reshape(row_width, col_width)
     return (context[None], in_grad[None], weight_grad)
 
 

time: 434 us -> 419 us (0.965)
  the two profiles are of different devices: /device:TPU:118 before, /device:TPU:1 now
where the time goes in v1:
time: 419 us; the launch traced here: 418 us
  waiting for transfers between devices  321 us (77%)
  local copies, waits for them, and re-layouts  37.4 us (9%)
  matrix products  25.5 us (6%)
  between operations  14.8 us (4%)
  starting transfers between devices  13.2 us (3%)
  other arithmetic  6.45 us (2%)
    unnamed x2, waiting for transfers between devices  320 us
    reshape x1, local copies, waits for them, and re-layouts, body(): term = jnp.einsum('fas,fbt->abst', frame_rows.reshape(frame_count, row_bl...  16.7 us
    ppermute x2, starting transfers between devices, with_halo(): lax.ppermute(tail, axis, [(i, (i + 1) % count) for i in range(ends)])  10.6 us
  transfers between devices with their start and end apart: 5, of which 2 were waited for; matrix products, arithmetic and copies ran while one was open for 4% of the time, Pallas kernels for 0%

profile of v1, /device:TPU:1, one launch (start us, length us, event | category | flops | bytes accessed | tf_op | source)
XLA Modules:
  0.0 418.4 jit_solution(10845476376976914627)
XLA Ops:
  7.2 1.8 copy-done
  9.1 1.5 convolution_convert_fusion
  11.3 1.3 collective-permute-start.1
  12.6 5.5 %collective-permute-start = (bf16[128,1024]{1,0:T(8,128)(2,1)}, bf16[128,1024]{1,0:T(8,128)(2,1)}, u32[]{:S(2)}, u32[]{:S(2)}) collective-permute-start(bf16[128,1024]{1,0:T(8,128)(2,1)} %slice.32), channel_id=1, source_target_pairs={{0,1},{1,2},{2,3},{3,4},{4,5},{5,6},{6,7},{7,8},{8,9},{9,10},{10,1... | collective-permute-start | bytes 786440 | tf_op jit(solution)/shard_map/ppermute | solution.py:20
  20.5 1.7 copy.42
  22.1 1.7 copy.41
  23.8 1.4 fusion.34
  25.2 1.4 collective-permute-done
  29.6 2.4 fusion.51
  31.9 2.3 fusion.22
  34.2 2.6 fusion.29
  36.9 5.4 %fusion.12 = f32[4,128,384]{2,1,0:T(8,128)} fusion(bf16[128,4,128]{0,2,1:T(8,128)(2,1)S(1)} %bitcast.71, f32[4,128,384]{2,1,0:T(8,128)} %fusion.22, f32[4,128,384]{2,1,0:T(8,128)} %get-tuple-element.19, f32[4,128]{1,0:T(4,128)S(1)} %get-tuple-element.18), kind=kOutput, calls=%fused_computation.21 | convolution fusion | flops 51708800 | bytes 2492416 | tf_op jit(solution)/shard_map/hfs,fhd->shd/dot_general | solution.py:66
  42.2 1.5 fusion.2
  44.5 1.3 collective-permute-start.3
  45.8 5.2 %collective-permute-start.2 = (bf16[128,1024]{0,1:T(8,128)(2,1)}, bf16[128,1024]{0,1:T(8,128)(2,1)}, u32[]{:S(2)}, u32[]{:S(2)}) collective-permute-start(bf16[128,1024]{0,1:T(8,128)(2,1)} %get-tuple-element.14), channel_id=1, source_target_pairs={{0,1},{1,2},{2,3},{3,4},{4,5},{5,6},{6,7},{7,8},{8,9},{9,10},{10,1... | collective-permute-start | bytes 786440 | tf_op jit(solution)/shard_map/ppermute | solution.py:20
  51.8 4.5 %convolution_convert_fusion.2 = bf16[4,128,128]{2,1,0:T(8,128)(2,1)S(1)} fusion(bf16[384,4,128]{0,2,1:T(8,128)(2,1)} %bitcast.66, f32[4,128,384]{2,1,0:T(8,128)} %fusion.22, f32[4,128,384]{2,1,0:T(8,128)} %get-tuple-element.19, f32[4,128]{1,0:T(4,128)S(1)} %get-tuple-element.18), kind=kOutput, calls=%fused_computation.20 | convolution fusion | flops 51774336 | bytes 2099200 | tf_op jit(solution)/shard_map/hfs,shd->fhd/dot_general | solution.py:63
  56.4 1.3 fusion.20
  57.8 2.4 convolution_bitcast_fusion
  60.1 7.0 %copy.37 = f32[32,32,32,48]{3,2,1,0:T(8,128)} copy(f32[32,32,32,48]{3,2,0,1:T(8,128)S(1)} %convolution_bitcast_fusion) | data formatting | bytes 12582912 | tf_op jit(solution)/shard_map/fas,fbt->abst/transpose | solution.py:112
  67.1 16.7 %reshape.172 = f32[1024,1536]{1,0:T(8,128)} reshape(f32[32,32,32,48]{3,2,1,0:T(8,128)} %copy.37) | data formatting | bytes 12582912 | tf_op jit(solution)/shard_map/reshape | solution.py:117
  84.4 2.5 fusion.11
  86.9 1.7 copy.38
  88.6 1.9 fusion.10
  90.4 319.6 %all-reduce.3.cloned.1.call-done = f32[1024,1536]{1,0:T(8,128)} async-done(((f32[1024,1536]{1,0:T(8,128)}), f32[1024,1536]{1,0:T(8,128)}) %all-reduce.3.cloned.1.call-update) | async-done | bytes 6291472
  (28 shorter events, 9.3 us)
Async XLA Ops:
  7.2 1.9 copy-start
  7.2 402.9 %all-reduce.3.cloned.1.call-start = ((), (), s32[]{:S(2)}) async-start(), calls=%async_computation | async-start | bytes 12582912
  11.3 13.9 %collective-permute-start.1 = (bf16[128,1024]{1,0:T(8,128)(2,1)}, bf16[128,1024]{1,0:T(8,128)(2,1)}, u32[]{:S(2)}, u32[]{:S(2)}) collective-permute-start(bf16[128,1024]{1,0:T(8,128)(2,1)} %slice.32), channel_id=1, source_target_pairs={{1,0},{2,1},{3,2},{4,3},{5,4},{6,5},{7,6},{8,7},{9,8},{10,9},{11,1... | collective-permute-start | bytes 786440 | tf_op jit(solution)/shard_map/ppermute | solution.py:22
  12.6 14.0 %collective-permute-start = (bf16[128,1024]{1,0:T(8,128)(2,1)}, bf16[128,1024]{1,0:T(8,128)(2,1)}, u32[]{:S(2)}, u32[]{:S(2)}) collective-permute-start(bf16[128,1024]{1,0:T(8,128)(2,1)} %slice.32), channel_id=1, source_target_pairs={{0,1},{1,2},{2,3},{3,4},{4,5},{5,6},{6,7},{7,8},{8,9},{9,10},{10,1... | collective-permute-start | bytes 786440 | tf_op jit(solution)/shard_map/ppermute | solution.py:20
  29.6 7.3 %copy-start.3 = (bf16[128,512]{0,1:T(8,128)(2,1)S(1)}, bf16[128,512]{0,1:T(8,128)(2,1)}, u32[]{:S(2)}) copy-start(bf16[128,512]{0,1:T(8,128)(2,1)} %copy.42) | copy-start | bytes 393220
  36.9 14.1 %copy-start.2 = (bf16[1,128,1024]{2,1,0:T(8,128)(2,1)S(1)}, bf16[1,128,1024]{2,1,0:T(8,128)(2,1)}, u32[]{:S(2)}) copy-start(bf16[1,128,1024]{2,1,0:T(8,128)(2,1)} %param.4) | copy-start | bytes 786436
  44.5 11.8 %collective-permute-start.3 = (bf16[128,1024]{0,1:T(8,128)(2,1)}, bf16[128,1024]{0,1:T(8,128)(2,1)}, u32[]{:S(2)}, u32[]{:S(2)}) collective-permute-start(bf16[128,1024]{0,1:T(8,128)(2,1)} %get-tuple-element.15), channel_id=1, source_target_pairs={{1,0},{2,1},{3,2},{4,3},{5,4},{6,5},{7,6},{8,7},{9,8},{10,9},{11,1... | collective-permute-start | bytes 786440 | tf_op jit(solution)/shard_map/ppermute | solution.py:22
  45.8 10.6 %collective-permute-start.2 = (bf16[128,1024]{0,1:T(8,128)(2,1)}, bf16[128,1024]{0,1:T(8,128)(2,1)}, u32[]{:S(2)}, u32[]{:S(2)}) collective-permute-start(bf16[128,1024]{0,1:T(8,128)(2,1)} %get-tuple-element.14), channel_id=1, source_target_pairs={{0,1},{1,2},{2,3},{3,4},{4,5},{5,6},{6,7},{7,8},{8,9},{9,10},{10,1... | collective-permute-start | bytes 786440 | tf_op jit(solution)/shard_map/ppermute | solution.py:20
  56.4 1.4 copy-start.1
  83.8 0.6 copy-start.4
Sparse Core Ops, SparseCore 0:
  83.9 326.1 all-reduce.2

commit v2 on v0

--- a/solution.py
+++ b/solution.py
@@ -74,6 +74,40 @@
     return (context, grad_query, grad_terms)
 
 
+def weight_gradient(frame_rows, grad_all):
+    frame_count, model_width = frame_rows.shape
+    grad_width = grad_all.shape[1]
+    calls = lax.axis_size("calls")
+    ctx = lax.axis_size("ctx")
+    row_parts = 4
+    col_parts = ctx // row_parts
+    tile_rows = model_width // row_parts
+    tile_cols = grad_width // col_parts
+    block_rows = model_width // calls
+    block_cols = grad_width // ctx
+    rows_per_tile = tile_rows // block_rows
+    cols_per_tile = tile_cols // block_cols
+    row_factor = frame_rows.reshape(frame_count, row_parts, 1, tile_rows).transpose(1, 2, 0, 3)
+    col_factor = grad_all.reshape(frame_count, 1, col_parts, tile_cols).transpose(1, 2, 0, 3)
+    row_factor = jnp.broadcast_to(row_factor, (row_parts, col_parts, frame_count, tile_rows))
+    col_factor = jnp.broadcast_to(col_factor, (row_parts, col_parts, frame_count, tile_cols))
+    sent = jnp.concatenate([row_factor, col_factor], axis=3).reshape(ctx, frame_count, -1)
+    got = lax.all_to_all(sent, "ctx", 0, 0, tiled=True)
+    tile = jnp.einsum(
+        "sfa,sfb->ab", got[..., :tile_rows], got[..., tile_rows:], preferred_element_type=jnp.float32
+    )
+    pieces = tile.reshape(rows_per_tile, block_rows, cols_per_tile, block_cols).transpose(0, 2, 1, 3)
+    pieces = pieces.reshape(calls, block_rows, block_cols)
+    summed = jnp.sum(lax.all_to_all(pieces, "calls", 0, 0, tiled=True), axis=0)
+    pairs = []
+    for piece in range(calls):
+        for owner in range(ctx):
+            row_block = (owner // col_parts) * rows_per_tile + piece // cols_per_tile
+            col_block = (owner % col_parts) * cols_per_tile + piece % cols_per_tile
+            pairs.append((piece * ctx + owner, row_block * ctx + col_block))
+    return lax.ppermute(summed, ("calls", "ctx"), pairs)
+
+
 def body(frames_in, w_qkv, out_grad, lengths):
     frame_rows = frames_in[0]
     frame_count, model_width = frame_rows.shape
@@ -105,11 +139,7 @@
     in_grad = lax.dot_general(
         grad_all, w_qkv, (((1,), (1,)), ((), ())), preferred_element_type=jnp.float32
     ).astype(jnp.bfloat16)
-    term = lax.dot_general(
-        frame_rows, grad_all, (((0,), (0,)), ((), ())), preferred_element_type=jnp.float32
-    )
-    partial_grad = lax.psum_scatter(term, "calls", scatter_dimension=0, tiled=True)
-    weight_grad = lax.psum_scatter(partial_grad, "ctx", scatter_dimension=1, tiled=True)
+    weight_grad = weight_gradient(frame_rows, grad_all)
     return (context[None], in_grad[None], weight_grad)
 
 

time: 434 us -> 219 us (0.50)
  the two profiles are of different devices: /device:TPU:118 before, /device:TPU:192 now
where the time goes in v2:
time: 219 us; the launch traced here: 218 us
  blocking collectives  96.3 us (44%)
  starting transfers between devices  40.1 us (18%)
  matrix products  24.5 us (11%)
  local copies, waits for them, and re-layouts  22.9 us (10%)
  waiting for transfers between devices  22.1 us (10%)
  other arithmetic  10.5 us (5%)
    all_to_all x1, blocking collectives, weight_gradient(): got = lax.all_to_all(sent, 'ctx', 0, 0, tiled=True)  96.3 us
    all_to_all x1, starting transfers between devices, weight_gradient(): summed = jnp.sum(lax.all_to_all(pieces, 'calls', 0, 0, tiled=True), axis=0)  20.4 us
    ppermute x2, starting transfers between devices, with_halo(): lax.ppermute(tail, axis, [(i, (i + 1) % count) for i in range(ends)])  11 us
    ppermute x1, waiting for transfers between devices, weight_gradient(): return lax.ppermute(summed, ('calls', 'ctx'), pairs)  10.3 us
    unnamed x12, local copies, waits for them, and re-layouts  8.35 us
    ppermute x2, waiting for transfers between devices, with_halo(): lax.ppermute(tail, axis, [(i, (i + 1) % count) for i in range(ends)])  6.22 us
    ppermute x1, starting transfers between devices, weight_gradient(): return lax.ppermute(summed, ('calls', 'ctx'), pairs)  6.12 us
    all_to_all x1, waiting for transfers between devices, weight_gradient(): summed = jnp.sum(lax.all_to_all(pieces, 'calls', 0, 0, tiled=True), axis=0)  5.6 us
  transfers between devices with their start and end apart: 6, of which 4 were waited for; matrix products, arithmetic and copies ran while one was open for 9% of the time, Pallas kernels for 0%

profile of v2, /device:TPU:192, one launch (start us, length us, event | category | flops | bytes accessed | tf_op | source)
XLA Modules:
  0.0 217.8 jit_solution(15546515807677047105)
XLA Ops:
  0.6 1.9 copy-done
  6.1 5.3 %collective-permute-start = (bf16[128,1024]{1,0:T(8,128)(2,1)}, bf16[128,1024]{1,0:T(8,128)(2,1)}, u32[]{:S(2)}, u32[]{:S(2)}) collective-permute-start(bf16[128,1024]{1,0:T(8,128)(2,1)} %slice.40), channel_id=1, source_target_pairs={{0,1},{1,2},{2,3},{3,4},{4,5},{5,6},{6,7},{7,8},{8,9},{9,10},{10,1... | collective-permute-start | bytes 786440 | tf_op jit(solution)/shard_map/ppermute | solution.py:20
  15.4 1.7 copy.34
  18.5 1.8 collective-permute-done
  23.2 2.4 %fusion.59 = (f32[4,128]{1,0:T(4,128)S(1)}, f32[4,128,384]{2,1,0:T(8,128)}) fusion(bf16[128,4,128]{0,2,1:T(8,128)(2,1)} %bitcast.70, bf16[384,4,128]{0,2,1:T(8,128)(2,1)} %bitcast.66, pred[128,384]{1,0:T(8,128)(4,1)} %fusion.42), kind=kOutput, calls=%fused_computation.72 | convolution fusion | flops 51118464 | bytes 1361920 | tf_op jit(solution)/shard_map/sub | solution.py:50
  25.6 2.3 %fusion.30 = f32[4,128,384]{2,1,0:T(8,128)} fusion(bf16[48,4,8,128]{3,2,1,0:T(8,128)(2,1)} %get-tuple-element.14, bf16[128,4,128]{0,2,1:T(8,128)(2,1)} %bitcast.62, pred[128]{0:T(512)(128)(4,1)S(1)} %get-tuple-element.10), kind=kOutput, calls=%fused_computation.35 | convolution fusion | flops 50397184 | bytes 1310848 | tf_op jit(solution)/shard_map/fhd,shd->hfs/dot_general | solution.py:58
  27.9 2.6 %fusion.37 = f32[4,128,384]{2,1,0:T(8,128)} fusion(bf16[128,4,128]{0,2,1:T(8,128)(2,1)} %bitcast.63, pred[128]{0:T(512)(128)(4,1)S(1)} %get-tuple-element.10, f32[4,128]{1,0:T(4,128)S(1)} %get-tuple-element.15, bf16[128,4,128]{0,2,1:T(8,128)(2,1)} %bitcast.71, bf16[384,4,128]{0,2,1:T(8,128)(2,1)} %bitcast.67, pred[128,384]{1,0:T(8,128)(4,1)} %fusion.42), kind=kOutput, calls=%fused_computation.45 | convolution fusion | flops 101712768 | bytes 1493120 | tf_op jit(solution)/shard_map/hfs,fhd->shd/dot_general | solution.py:69
  30.5 5.3 %fusion.20 = f32[4,128,384]{2,1,0:T(8,128)} fusion(bf16[128,4,128]{0,2,1:T(8,128)(2,1)S(1)} %bitcast.73, f32[4,128,384]{2,1,0:T(8,128)} %fusion.30, f32[4,128,384]{2,1,0:T(8,128)} %get-tuple-element.16, f32[4,128]{1,0:T(4,128)S(1)} %get-tuple-element.15), kind=kOutput, calls=%fused_computation.25 | convolution fusion | flops 51708800 | bytes 2492416 | tf_op jit(solution)/shard_map/hfs,fhd->shd/dot_general | solution.py:66
  39.4 5.7 %collective-permute-start.2 = (bf16[128,1024]{0,1:T(8,128)(2,1)}, bf16[128,1024]{0,1:T(8,128)(2,1)}, u32[]{:S(2)}, u32[]{:S(2)}) collective-permute-start(bf16[128,1024]{0,1:T(8,128)(2,1)} %get-tuple-element.11), channel_id=1, source_target_pairs={{0,1},{1,2},{2,3},{3,4},{4,5},{5,6},{6,7},{7,8},{8,9},{9,10},{10,1... | collective-permute-start | bytes 786440 | tf_op jit(solution)/shard_map/ppermute | solution.py:20
  47.2 4.5 %convolution_convert_fusion.2 = bf16[4,128,128]{2,1,0:T(8,128)(2,1)S(1)} fusion(bf16[384,4,128]{0,2,1:T(8,128)(2,1)} %bitcast.68, f32[4,128,384]{2,1,0:T(8,128)} %fusion.30, f32[4,128,384]{2,1,0:T(8,128)} %get-tuple-element.16, f32[4,128]{1,0:T(4,128)S(1)} %get-tuple-element.15), kind=kOutput, calls=%fused_computation.24 | convolution fusion | flops 51774336 | bytes 2099200 | tf_op jit(solution)/shard_map/hfs,shd->fhd/dot_general | solution.py:63
  51.7 4.4 %collective-permute-done.2 = bf16[128,1024]{0,1:T(8,128)(2,1)} collective-permute-done((bf16[128,1024]{0,1:T(8,128)(2,1)}, bf16[128,1024]{0,1:T(8,128)(2,1)}, u32[]{:S(2)}, u32[]{:S(2)}) %collective-permute-start.2) | collective-permute-done | bytes 262176 | tf_op jit(solution)/shard_map/ppermute | solution.py:20
  58.6 96.3 %all_to_all.10 = bf16[32,128,448]{1,2,0:T(8,128)(2,1)S(1)} all-to-all(bf16[32,128,448]{1,2,0:T(8,128)(2,1)S(1)} %bitcast.53), channel_id=1, replica_groups=mesh['calls'=32,'ctx'=32] {'ctx'}, dimensions={0} | all-to-all | bytes 7340032 | tf_op jit(solution)/shard_map/all_to_all | solution.py:95
  156.3 2.0 reshape.176
  158.3 1.9 copy.29
  160.2 2.2 %reshape.179 = f32[32,1,1536]{2,1,0:T(1,128)} reshape(f32[32,32,48]{2,1,0:T(8,128)} %bitcast.59) | data formatting | bytes 393216
  162.5 20.4 %all-to-all-start.1 = ((f32[32,1,1536]{2,1,0:T(1,128)}), f32[32,1,1536]{2,1,0:T(1,128)}, u32[]{:S(2)}, u32[]{:S(2)}) async-start(f32[32,1,1536]{2,1,0:T(1,128)} %reshape.179), calls=%async_computation.1 | async-start | bytes 393216 | tf_op jit(solution)/shard_map/all_to_all | solution.py:101
  182.9 2.5 %fusion.19 = bf16[4,128,128]{2,1,0:T(8,128)(2,1)} fusion(bf16[48,4,8,128]{3,2,1,0:T(8,128)(2,1)} %get-tuple-element.14, f32[128]{0:T(128)S(1)} %copy-done.3, f32[4,128]{1,0:T(4,128)S(1)} %get-tuple-element.15, bf16[128,4,128]{0,2,1:T(8,128)(2,1)} %bitcast.72, bf16[384,4,128]{0,2,1:T(8,128)(2,1)} %bitcast.69, pred[128,384]{1,0:T(8,128)(4,1)} %fusion.42), kind=kOutput, calls=%fused_computation.23 | convolution fusion | flops 101778304 | bytes 1100288 | tf_op jit(solution)/shard_map/hfs,shd->fhd/dot_general | solution.py:54
  185.4 1.7 copy.30
  187.1 5.6 %all-to-all-done.1 = f32[32,1,1536]{2,1,0:T(1,128)} async-done(((f32[32,1,1536]{2,1,0:T(1,128)}), f32[32,1,1536]{2,1,0:T(1,128)}, u32[]{:S(2)}, u32[]{:S(2)}) %all-to-all-start.1) | async-done | bytes 196640 | tf_op jit(solution)/shard_map/all_to_all | solution.py:101
  193.2 2.7 %reduce = f32[32,1536]{1,0:T(8,128)} reduce(f32[32,1,1536]{2,1,0:T(1,128)} %all-to-all-done.1, f32[]{:T(128)} %broadcast.137), dimensions={1}, to_apply=%all_to_all.7.reduce_sub_computation | reduce | bytes 393220 | tf_op jit(solution)/shard_map/all_to_all | solution.py:101
  195.9 2.0 reshape.180
  199.0 6.1 %collective-permute-start.4 = (f32[32,48]{1,0:T(8,128)S(1)}, f32[32,48]{1,0:T(8,128)S(1)}, u32[]{:S(2)}, u32[]{:S(2)}) collective-permute-start(f32[32,48]{1,0:T(8,128)S(1)} %reduce_sum.29), channel_id=1, source_target_pairs={{0,0},{1,4},{2,8},{3,12},{4,16},{5,20},{6,24},{7,28},{8,256},{9,26... | collective-permute-start | bytes 18440 | tf_op jit(solution)/shard_map/ppermute | solution.py:108
  205.1 1.9 fusion.13
  207.0 10.3 %collective-permute-done.4 = f32[32,48]{1,0:T(8,128)S(1)} collective-permute-done((f32[32,48]{1,0:T(8,128)S(1)}, f32[32,48]{1,0:T(8,128)S(1)}, u32[]{:S(2)}, u32[]{:S(2)}) %collective-permute-start.4) | collective-permute-done | bytes 6176 | tf_op jit(solution)/shard_map/ppermute | solution.py:108
  (36 shorter events, 22.9 us)
Async XLA Ops:
  0.6 1.9 copy-start
  4.8 13.7 %collective-permute-start.1 = (bf16[128,1024]{1,0:T(8,128)(2,1)}, bf16[128,1024]{1,0:T(8,128)(2,1)}, u32[]{:S(2)}, u32[]{:S(2)}) collective-permute-start(bf16[128,1024]{1,0:T(8,128)(2,1)} %slice.40), channel_id=1, source_target_pairs={{1,0},{2,1},{3,2},{4,3},{5,4},{6,5},{7,6},{8,7},{9,8},{10,9},{11,1... | collective-permute-start | bytes 786440 | tf_op jit(solution)/shard_map/ppermute | solution.py:22
  6.1 14.2 %collective-permute-start = (bf16[128,1024]{1,0:T(8,128)(2,1)}, bf16[128,1024]{1,0:T(8,128)(2,1)}, u32[]{:S(2)}, u32[]{:S(2)}) collective-permute-start(bf16[128,1024]{1,0:T(8,128)(2,1)} %slice.40), channel_id=1, source_target_pairs={{0,1},{1,2},{2,3},{3,4},{4,5},{5,6},{6,7},{7,8},{8,9},{9,10},{10,1... | collective-permute-start | bytes 786440 | tf_op jit(solution)/shard_map/ppermute | solution.py:20
  23.2 7.3 %copy-start.2 = (bf16[128,512]{0,1:T(8,128)(2,1)S(1)}, bf16[128,512]{0,1:T(8,128)(2,1)}, u32[]{:S(2)}) copy-start(bf16[128,512]{0,1:T(8,128)(2,1)} %copy.36) | copy-start | bytes 393220
  38.1 13.6 %collective-permute-start.3 = (bf16[128,1024]{0,1:T(8,128)(2,1)}, bf16[128,1024]{0,1:T(8,128)(2,1)}, u32[]{:S(2)}, u32[]{:S(2)}) collective-permute-start(bf16[128,1024]{0,1:T(8,128)(2,1)} %get-tuple-element.12), channel_id=1, source_target_pairs={{1,0},{2,1},{3,2},{4,3},{5,4},{6,5},{7,6},{8,7},{9,8},{10,9},{11,1... | collective-permute-start | bytes 786440 | tf_op jit(solution)/shard_map/ppermute | solution.py:22
  39.4 16.7 %collective-permute-start.2 = (bf16[128,1024]{0,1:T(8,128)(2,1)}, bf16[128,1024]{0,1:T(8,128)(2,1)}, u32[]{:S(2)}, u32[]{:S(2)}) collective-permute-start(bf16[128,1024]{0,1:T(8,128)(2,1)} %get-tuple-element.11), channel_id=1, source_target_pairs={{0,1},{1,2},{2,3},{3,4},{4,5},{5,6},{6,7},{7,8},{8,9},{9,10},{10,1... | collective-permute-start | bytes 786440 | tf_op jit(solution)/shard_map/ppermute | solution.py:20
  51.7 6.1 %copy-start.1 = (bf16[4,128,256]{1,2,0:T(8,128)(2,1)S(1)}, bf16[4,128,256]{1,2,0:T(8,128)(2,1)}, u32[]{:S(2)}) copy-start(bf16[4,128,256]{1,2,0:T(8,128)(2,1)} %copy.26) | copy-start | bytes 786436
  154.9 28.0 %copy-start.3 = (f32[128]{0:T(128)S(1)}, f32[128]{0:T(128)}, u32[]{:S(2)}) copy-start(f32[128]{0:T(128)} %get-tuple-element.9) | copy-start | bytes 1540
  162.5 30.2 %all-to-all-start.1 = ((f32[32,1,1536]{2,1,0:T(1,128)}), f32[32,1,1536]{2,1,0:T(1,128)}, u32[]{:S(2)}, u32[]{:S(2)}) async-start(f32[32,1,1536]{2,1,0:T(1,128)} %reshape.179), calls=%async_computation.1 | async-start | bytes 393216 | tf_op jit(solution)/shard_map/all_to_all | solution.py:101
  199.0 18.3 %collective-permute-start.4 = (f32[32,48]{1,0:T(8,128)S(1)}, f32[32,48]{1,0:T(8,128)S(1)}, u32[]{:S(2)}, u32[]{:S(2)}) collective-permute-start(f32[32,48]{1,0:T(8,128)S(1)} %reduce_sum.29), channel_id=1, source_target_pairs={{0,0},{1,4},{2,8},{3,12},{4,16},{5,20},{6,24},{7,28},{8,256},{9,26... | collective-permute-start | bytes 18440 | tf_op jit(solution)/shard_map/ppermute | solution.py:108

commit v3 on v2

--- a/solution.py
+++ b/solution.py
@@ -91,11 +91,10 @@
     col_factor = grad_all.reshape(frame_count, 1, col_parts, tile_cols).transpose(1, 2, 0, 3)
     row_factor = jnp.broadcast_to(row_factor, (row_parts, col_parts, frame_count, tile_rows))
     col_factor = jnp.broadcast_to(col_factor, (row_parts, col_parts, frame_count, tile_cols))
-    sent = jnp.concatenate([row_factor, col_factor], axis=3).reshape(ctx, frame_count, -1)
-    got = lax.all_to_all(sent, "ctx", 0, 0, tiled=True)
-    tile = jnp.einsum(
-        "sfa,sfb->ab", got[..., :tile_rows], got[..., tile_rows:], preferred_element_type=jnp.float32
-    )
+    got_rows = lax.all_to_all(row_factor.reshape(ctx, 2 * frame_count, -1), "ctx", 0, 0, tiled=True)
+    got_cols = lax.all_to_all(col_factor.reshape(ctx, frame_count, -1), "ctx", 0, 0, tiled=True)
+    got_rows = got_rows.reshape(ctx, frame_count, tile_rows)
+    tile = jnp.einsum("sfa,sfb->ab", got_rows, got_cols, preferred_element_type=jnp.float32)
     pieces = tile.reshape(rows_per_tile, block_rows, cols_per_tile, block_cols).transpose(0, 2, 1, 3)
     pieces = pieces.reshape(calls, block_rows, block_cols)
     summed = jnp.sum(lax.all_to_all(pieces, "calls", 0, 0, tiled=True), axis=0)

time: 219 us -> 228 us (1.041)
  the two profiles are of different devices: /device:TPU:192 before, /device:TPU:224 now
where the time goes in v3:
time: 228 us; the launch traced here: 226 us
  waiting for transfers between devices  93.9 us (41%)
  starting transfers between devices  59.4 us (26%)
  local copies, waits for them, and re-layouts  34.3 us (15%)
  matrix products  26.4 us (12%)
  other arithmetic  11 us (5%)
    ppermute x2, waiting for transfers between devices, with_halo(): lax.ppermute(head, axis, [((i + 1) % count, i) for i in range(ends)])  35.1 us
    all_to_all x1, waiting for transfers between devices, weight_gradient(): lax.all_to_all(col_factor.reshape(ctx, frame_count, -1), 'ctx', 0, 0, til...  34.1 us
    all_to_all x1, starting transfers between devices, weight_gradient(): summed = jnp.sum(lax.all_to_all(pieces, 'calls', 0, 0, tiled=True), axis=0)  20.4 us
    all_to_all x1, starting transfers between devices, weight_gradient(): lax.all_to_all(col_factor.reshape(ctx, frame_count, -1), 'ctx', 0, 0, til...  12.4 us
    ppermute x1, waiting for transfers between devices, weight_gradient(): return lax.ppermute(summed, ('calls', 'ctx'), pairs)  10.3 us
    all_to_all x1, starting transfers between devices, weight_gradient(): lax.all_to_all(row_factor.reshape(ctx, 2 * frame_count, -1), 'ctx', 0, 0,...  9.56 us
    ppermute x2, waiting for transfers between devices, with_halo(): lax.ppermute(tail, axis, [(i, (i + 1) % count) for i in range(ends)])  8.88 us
    ppermute x2, starting transfers between devices, with_halo(): lax.ppermute(tail, axis, [(i, (i + 1) % count) for i in range(ends)])  7.3 us
  transfers between devices with their start and end apart: 8, of which 6 were waited for; matrix products, arithmetic and copies ran while one was open for 19% of the time, Pallas kernels for 0%

profile of v3, /device:TPU:224, one launch (start us, length us, event | category | flops | bytes accessed | tf_op | source)
XLA Modules:
  0.0 226.5 jit_solution(16778936475463489071)
XLA Ops:
  3.6 4.1 %reshape.182 = bf16[32,256,128]{2,1,0:T(8,128)(2,1)} reshape(bf16[4,8,128,256]{3,2,1,0:T(8,128)(2,1)} %broadcast_in_dim.61) | data formatting | bytes 4194304 | tf_op jit(solution)/shard_map/reshape | solution.py:94
  7.6 9.6 %all-to-all-start.1 = ((bf16[32,256,128]{2,1,0:T(8,128)(2,1)}), bf16[32,256,128]{2,1,0:T(8,128)(2,1)}, u32[]{:S(2)}, u32[]{:S(2)}) async-start(bf16[32,256,128]{2,1,0:T(8,128)(2,1)} %reshape.182), calls=%async_computation.1 | async-start | bytes 4194304 | tf_op jit(solution)/shard_map/all_to_all | solution.py:94
  19.5 2.5 %collective-permute-start.1 = (bf16[128,1024]{1,0:T(8,128)(2,1)}, bf16[128,1024]{1,0:T(8,128)(2,1)}, u32[]{:S(2)}, u32[]{:S(2)}) collective-permute-start(bf16[128,1024]{1,0:T(8,128)(2,1)} %slice.32), channel_id=1, source_target_pairs={{1,0},{2,1},{3,2},{4,3},{5,4},{6,5},{7,6},{8,7},{9,8},{10,9},{11,1... | collective-permute-start | bytes 786440 | tf_op jit(solution)/shard_map/ppermute | solution.py:22
  22.0 3.4 %collective-permute-start = (bf16[128,1024]{1,0:T(8,128)(2,1)}, bf16[128,1024]{1,0:T(8,128)(2,1)}, u32[]{:S(2)}, u32[]{:S(2)}) collective-permute-start(bf16[128,1024]{1,0:T(8,128)(2,1)} %slice.32), channel_id=1, source_target_pairs={{0,1},{1,2},{2,3},{3,4},{4,5},{5,6},{6,7},{7,8},{8,9},{9,10},{10,1... | collective-permute-start | bytes 786440 | tf_op jit(solution)/shard_map/ppermute | solution.py:20
  32.5 35.1 %collective-permute-done.1 = bf16[128,1024]{1,0:T(8,128)(2,1)} collective-permute-done((bf16[128,1024]{1,0:T(8,128)(2,1)}, bf16[128,1024]{1,0:T(8,128)(2,1)}, u32[]{:S(2)}, u32[]{:S(2)}) %collective-permute-start.1) | collective-permute-done | bytes 262176 | tf_op jit(solution)/shard_map/ppermute | solution.py:22
  67.6 6.6 %collective-permute-done = bf16[128,1024]{1,0:T(8,128)(2,1)} collective-permute-done((bf16[128,1024]{1,0:T(8,128)(2,1)}, bf16[128,1024]{1,0:T(8,128)(2,1)}, u32[]{:S(2)}, u32[]{:S(2)}) %collective-permute-start) | collective-permute-done | bytes 262176 | tf_op jit(solution)/shard_map/ppermute | solution.py:20
  77.1 2.3 %fusion.22 = f32[4,128,384]{2,1,0:T(8,128)} fusion(bf16[48,4,8,128]{3,2,1,0:T(8,128)(2,1)} %get-tuple-element.14, bf16[128,4,128]{0,2,1:T(8,128)(2,1)} %bitcast.68, pred[128]{0:T(512)(128)(4,1)S(1)} %get-tuple-element.10), kind=kOutput, calls=%fused_computation.31 | convolution fusion | flops 50397184 | bytes 1310848 | tf_op jit(solution)/shard_map/fhd,shd->hfs/dot_general | solution.py:58
  79.4 2.3 %fusion.51 = (f32[4,128]{1,0:T(4,128)S(1)}, f32[4,128,384]{2,1,0:T(8,128)}) fusion(bf16[128,4,128]{0,2,1:T(8,128)(2,1)} %bitcast.76, bf16[384,4,128]{0,2,1:T(8,128)(2,1)} %bitcast.72, pred[128,384]{1,0:T(8,128)(4,1)} %fusion.34), kind=kOutput, calls=%fused_computation.68 | convolution fusion | flops 51118464 | bytes 1361920 | tf_op jit(solution)/shard_map/sub | solution.py:50
  81.8 5.4 %fusion.12 = f32[4,128,384]{2,1,0:T(8,128)} fusion(bf16[128,4,128]{0,2,1:T(8,128)(2,1)S(1)} %bitcast.78, f32[4,128,384]{2,1,0:T(8,128)} %fusion.22, f32[4,128,384]{2,1,0:T(8,128)} %get-tuple-element.16, f32[4,128]{1,0:T(4,128)S(1)} %get-tuple-element.15), kind=kOutput, calls=%fused_computation.21 | convolution fusion | flops 51708800 | bytes 2492416 | tf_op jit(solution)/shard_map/hfs,fhd->shd/dot_general | solution.py:66
  87.2 2.5 %fusion.29 = f32[4,128,384]{2,1,0:T(8,128)} fusion(bf16[128,4,128]{0,2,1:T(8,128)(2,1)S(1)} %bitcast.69, pred[128]{0:T(512)(128)(4,1)S(1)} %get-tuple-element.10, f32[4,128]{1,0:T(4,128)S(1)} %get-tuple-element.15, bf16[128,4,128]{0,2,1:T(8,128)(2,1)S(1)} %bitcast.79, bf16[384,4,128]{0,2,1:T(8,128)(2,1)} %bitcast.73, pred[128,384]{1,0:T(8,128)(4,1)} %fusion.34), kind=kOutput, calls=%fused_computation.41 | convolution fusion | flops 101712768 | bytes 1493120 | tf_op jit(solution)/shard_map/hfs,fhd->shd/dot_general | solution.py:69
  93.9 3.9 %collective-permute-start.2 = (bf16[128,1024]{0,1:T(8,128)(2,1)}, bf16[128,1024]{0,1:T(8,128)(2,1)}, u32[]{:S(2)}, u32[]{:S(2)}) collective-permute-start(bf16[128,1024]{0,1:T(8,128)(2,1)} %get-tuple-element.11), channel_id=1, source_target_pairs={{0,1},{1,2},{2,3},{3,4},{4,5},{5,6},{6,7},{7,8},{8,9},{9,10},{10,1... | collective-permute-start | bytes 786440 | tf_op jit(solution)/shard_map/ppermute | solution.py:20
  97.8 4.6 %convolution_convert_fusion.2 = bf16[4,128,128]{2,1,0:T(8,128)(2,1)S(1)} fusion(bf16[384,4,128]{0,2,1:T(8,128)(2,1)} %bitcast.74, f32[4,128,384]{2,1,0:T(8,128)} %fusion.22, f32[4,128,384]{2,1,0:T(8,128)} %get-tuple-element.16, f32[4,128]{1,0:T(4,128)S(1)} %get-tuple-element.15), kind=kOutput, calls=%fused_computation.19 | convolution fusion | flops 51774336 | bytes 2099200 | tf_op jit(solution)/shard_map/hfs,shd->fhd/dot_general | solution.py:63
  103.1 2.3 collective-permute-done.2
  107.5 2.6 %broadcast_in_dim.59 = bf16[4,8,128,192]{2,3,1,0:T(8,128)(2,1)} broadcast(bf16[8,128,192]{1,2,0:T(8,128)(2,1)} %bitcast.66), dimensions={1,2,3} | broadcast | bytes 1966080 | tf_op jit(solution)/shard_map/broadcast_in_dim | solution.py:93
  110.0 12.4 %all-to-all-start = ((bf16[32,128,192]{1,2,0:T(8,128)(2,1)}), bf16[32,128,192]{1,2,0:T(8,128)(2,1)}, u32[]{:S(2)}, u32[]{:S(2)}) async-start(bf16[32,128,192]{1,2,0:T(8,128)(2,1)} %bitcast.59), calls=%async_computation | async-start | bytes 3145728 | tf_op jit(solution)/shard_map/all_to_all | solution.py:95
  122.4 4.1 %reshape.183 = bf16[32,128,256]{2,1,0:T(8,128)(2,1)} reshape(bf16[32,256,128]{2,1,0:T(8,128)(2,1)} %all-to-all-done.1) | data formatting | bytes 4194304 | tf_op jit(solution)/shard_map/reshape | solution.py:96
  126.5 34.1 %all-to-all-done = bf16[32,128,192]{1,2,0:T(8,128)(2,1)} async-done(((bf16[32,128,192]{1,2,0:T(8,128)(2,1)}), bf16[32,128,192]{1,2,0:T(8,128)(2,1)}, u32[]{:S(2)}, u32[]{:S(2)}) %all-to-all-start) | async-done | bytes 1572896 | tf_op jit(solution)/shard_map/all_to_all | solution.py:95
  160.6 3.3 %convolution_bitcast_fusion = f32[256,192]{0,1:T(8,128)} fusion(bf16[32,128,192]{1,2,0:T(8,128)(2,1)} %all-to-all-done, bf16[32,128,256]{2,1,0:T(8,128)(2,1)} %reshape.183), kind=kOutput, calls=%fused_computation.20 | convolution fusion | flops 402653184 | bytes 3866624 | tf_op jit(solution)/shard_map/sfa,sfb->ab/dot_general | solution.py:97
  171.9 20.4 %all-to-all-start.2 = ((f32[32,1,1536]{2,1,0:T(1,128)}), f32[32,1,1536]{2,1,0:T(1,128)}, u32[]{:S(2)}, u32[]{:S(2)}) async-start(f32[32,1,1536]{2,1,0:T(1,128)} %reshape.187), calls=%async_computation.2 | async-start | bytes 393216 | tf_op jit(solution)/shard_map/all_to_all | solution.py:100
  192.3 2.5 %fusion.11 = bf16[4,128,128]{2,1,0:T(8,128)(2,1)} fusion(bf16[48,4,8,128]{3,2,1,0:T(8,128)(2,1)} %get-tuple-element.14, f32[128]{0:T(128)S(1)} %copy-done.4, f32[4,128]{1,0:T(4,128)S(1)} %get-tuple-element.15, bf16[128,4,128]{0,2,1:T(8,128)(2,1)} %bitcast.77, bf16[384,4,128]{0,2,1:T(8,128)(2,1)} %bitcast.75, pred[128,384]{1,0:T(8,128)(4,1)} %fusion.34), kind=kOutput, calls=%fused_computation.18 | convolution fusion | flops 101778304 | bytes 1100288 | tf_op jit(solution)/shard_map/hfs,shd->fhd/dot_general | solution.py:54
  196.5 5.6 %all-to-all-done.2 = f32[32,1,1536]{2,1,0:T(1,128)} async-done(((f32[32,1,1536]{2,1,0:T(1,128)}), f32[32,1,1536]{2,1,0:T(1,128)}, u32[]{:S(2)}, u32[]{:S(2)}) %all-to-all-start.2) | async-done | bytes 196640 | tf_op jit(solution)/shard_map/all_to_all | solution.py:100
  202.6 2.7 %reduce = f32[32,1536]{1,0:T(8,128)} reduce(f32[32,1,1536]{2,1,0:T(1,128)} %all-to-all-done.2, f32[]{:T(128)} %broadcast.137), dimensions={1}, to_apply=%all_to_all.11.reduce_sub_computation | reduce | bytes 393220 | tf_op jit(solution)/shard_map/all_to_all | solution.py:100
  208.3 5.4 %collective-permute-start.4 = (f32[32,48]{1,0:T(8,128)S(1)}, f32[32,48]{1,0:T(8,128)S(1)}, u32[]{:S(2)}, u32[]{:S(2)}) collective-permute-start(f32[32,48]{1,0:T(8,128)S(1)} %reduce_sum.29), channel_id=1, source_target_pairs={{0,0},{1,4},{2,8},{3,12},{4,16},{5,20},{6,24},{7,28},{8,256},{9,26... | collective-permute-start | bytes 18440 | tf_op jit(solution)/shard_map/ppermute | solution.py:107
  215.6 10.3 %collective-permute-done.4 = f32[32,48]{1,0:T(8,128)S(1)} collective-permute-done((f32[32,48]{1,0:T(8,128)S(1)}, f32[32,48]{1,0:T(8,128)S(1)}, u32[]{:S(2)}, u32[]{:S(2)}) %collective-permute-start.4) | collective-permute-done | bytes 6176 | tf_op jit(solution)/shard_map/ppermute | solution.py:107
  (43 shorter events, 37.2 us)
Async XLA Ops:
  0.6 16.6 %copy-start = (bf16[1024,1536]{1,0:T(8,128)(2,1)S(1)}, bf16[1024,1536]{1,0:T(8,128)(2,1)}, u32[]{:S(2)}) copy-start(bf16[1024,1536]{1,0:T(8,128)(2,1)} %param.5) | copy-start | bytes 9437188
  7.6 99.8 %all-to-all-start.1 = ((bf16[32,256,128]{2,1,0:T(8,128)(2,1)}), bf16[32,256,128]{2,1,0:T(8,128)(2,1)}, u32[]{:S(2)}, u32[]{:S(2)}) async-start(bf16[32,256,128]{2,1,0:T(8,128)(2,1)} %reshape.182), calls=%async_computation.1 | async-start | bytes 4194304 | tf_op jit(solution)/shard_map/all_to_all | solution.py:94
  19.5 48.1 %collective-permute-start.1 = (bf16[128,1024]{1,0:T(8,128)(2,1)}, bf16[128,1024]{1,0:T(8,128)(2,1)}, u32[]{:S(2)}, u32[]{:S(2)}) collective-permute-start(bf16[128,1024]{1,0:T(8,128)(2,1)} %slice.32), channel_id=1, source_target_pairs={{1,0},{2,1},{3,2},{4,3},{5,4},{6,5},{7,6},{8,7},{9,8},{10,9},{11,1... | collective-permute-start | bytes 786440 | tf_op jit(solution)/shard_map/ppermute | solution.py:22
  22.0 52.3 %collective-permute-start = (bf16[128,1024]{1,0:T(8,128)(2,1)}, bf16[128,1024]{1,0:T(8,128)(2,1)}, u32[]{:S(2)}, u32[]{:S(2)}) collective-permute-start(bf16[128,1024]{1,0:T(8,128)(2,1)} %slice.32), channel_id=1, source_target_pairs={{0,1},{1,2},{2,3},{3,4},{4,5},{5,6},{6,7},{7,8},{8,9},{9,10},{10,1... | collective-permute-start | bytes 786440 | tf_op jit(solution)/shard_map/ppermute | solution.py:20
  77.1 4.7 %copy-start.3 = (bf16[128,512]{0,1:T(8,128)(2,1)S(1)}, bf16[128,512]{0,1:T(8,128)(2,1)}, u32[]{:S(2)}) copy-start(bf16[128,512]{0,1:T(8,128)(2,1)} %copy.31) | copy-start | bytes 393220
  81.8 5.4 %copy-start.1 = (bf16[1,128,512]{1,2,0:T(8,128)(2,1)S(1)}, bf16[1,128,512]{1,2,0:T(8,128)(2,1)}, u32[]{:S(2)}) copy-start(bf16[1,128,512]{1,2,0:T(8,128)(2,1)} %copy.30) | copy-start | bytes 393220
  92.0 10.5 %collective-permute-start.3 = (bf16[128,1024]{0,1:T(8,128)(2,1)}, bf16[128,1024]{0,1:T(8,128)(2,1)S(1)}, u32[]{:S(2)}, u32[]{:S(2)}) collective-permute-start(bf16[128,1024]{0,1:T(8,128)(2,1)} %get-tuple-element.12), channel_id=1, source_target_pairs={{1,0},{2,1},{3,2},{4,3},{5,4},{6,5},{7,6},{8,7},{9,8},{10,9},{11,1... | collective-permute-start | bytes 786440 | tf_op jit(solution)/shard_map/ppermute | solution.py:22
  93.9 11.5 %collective-permute-start.2 = (bf16[128,1024]{0,1:T(8,128)(2,1)}, bf16[128,1024]{0,1:T(8,128)(2,1)}, u32[]{:S(2)}, u32[]{:S(2)}) collective-permute-start(bf16[128,1024]{0,1:T(8,128)(2,1)} %get-tuple-element.11), channel_id=1, source_target_pairs={{0,1},{1,2},{2,3},{3,4},{4,5},{5,6},{6,7},{7,8},{8,9},{9,10},{10,1... | collective-permute-start | bytes 786440 | tf_op jit(solution)/shard_map/ppermute | solution.py:20
  102.4 0.7 copy-start.2
  110.0 50.6 %all-to-all-start = ((bf16[32,128,192]{1,2,0:T(8,128)(2,1)}), bf16[32,128,192]{1,2,0:T(8,128)(2,1)}, u32[]{:S(2)}, u32[]{:S(2)}) async-start(bf16[32,128,192]{1,2,0:T(8,128)(2,1)} %bitcast.59), calls=%async_computation | async-start | bytes 3145728 | tf_op jit(solution)/shard_map/all_to_all | solution.py:95
  165.7 26.6 %copy-start.4 = (f32[128]{0:T(128)S(1)}, f32[128]{0:T(128)}, u32[]{:S(2)}) copy-start(f32[128]{0:T(128)} %get-tuple-element.9) | copy-start | bytes 1540
  171.9 30.2 %all-to-all-start.2 = ((f32[32,1,1536]{2,1,0:T(1,128)}), f32[32,1,1536]{2,1,0:T(1,128)}, u32[]{:S(2)}, u32[]{:S(2)}) async-start(f32[32,1,1536]{2,1,0:T(1,128)} %reshape.187), calls=%async_computation.2 | async-start | bytes 393216 | tf_op jit(solution)/shard_map/all_to_all | solution.py:100
  208.3 17.5 %collective-permute-start.4 = (f32[32,48]{1,0:T(8,128)S(1)}, f32[32,48]{1,0:T(8,128)S(1)}, u32[]{:S(2)}, u32[]{:S(2)}) collective-permute-start(f32[32,48]{1,0:T(8,128)S(1)} %reduce_sum.29), channel_id=1, source_target_pairs={{0,0},{1,4},{2,8},{3,12},{4,16},{5,20},{6,24},{7,28},{8,256},{9,26... | collective-permute-start | bytes 18440 | tf_op jit(solution)/shard_map/ppermute | solution.py:107

commit v4 on v2

--- a/solution.py
+++ b/solution.py
@@ -93,12 +93,21 @@
     col_factor = jnp.broadcast_to(col_factor, (row_parts, col_parts, frame_count, tile_cols))
     sent = jnp.concatenate([row_factor, col_factor], axis=3).reshape(ctx, frame_count, -1)
     got = lax.all_to_all(sent, "ctx", 0, 0, tiled=True)
-    tile = jnp.einsum(
-        "sfa,sfb->ab", got[..., :tile_rows], got[..., tile_rows:], preferred_element_type=jnp.float32
-    )
-    pieces = tile.reshape(rows_per_tile, block_rows, cols_per_tile, block_cols).transpose(0, 2, 1, 3)
-    pieces = pieces.reshape(calls, block_rows, block_cols)
-    summed = jnp.sum(lax.all_to_all(pieces, "calls", 0, 0, tiled=True), axis=0)
+    row_pieces = got[..., :tile_rows].reshape(ctx, frame_count, rows_per_tile, block_rows)
+    col_pieces = got[..., tile_rows:].reshape(ctx, frame_count, cols_per_tile, block_cols)
+    pieces = jnp.einsum("sfia,sfjb->ijab", row_pieces, col_pieces, preferred_element_type=jnp.float32)
+    pieces = pieces.reshape((2,) * (calls.bit_length() - 1) + (block_rows, block_cols))
+    index = lax.axis_index("calls")
+    for bit in range(calls.bit_length() - 1):
+        axis = pieces.ndim - 3
+        mine = (index >> bit) & 1
+        low = lax.index_in_dim(pieces, 0, axis, keepdims=False)
+        high = lax.index_in_dim(pieces, 1, axis, keepdims=False)
+        keep = jnp.where(mine == 0, low, high)
+        send = jnp.where(mine == 0, high, low)
+        pairs = [(i, i ^ (1 << bit)) for i in range(calls)]
+        pieces = keep + lax.ppermute(send, "calls", pairs)
+    summed = pieces
     pairs = []
     for piece in range(calls):
         for owner in range(ctx):

time: 219 us -> 242 us (1.11)
  the two profiles are of different devices: /device:TPU:192 before, /device:TPU:246 now
where the time goes in v4:
time: 242 us; the launch traced here: 241 us
  waiting for transfers between devices  123 us (51%)
  starting transfers between devices  61.3 us (25%)
  matrix products  24.3 us (10%)
  local copies, waits for them, and re-layouts  19 us (8%)
  other arithmetic  11.5 us (5%)
    all_to_all x1, waiting for transfers between devices, weight_gradient(): got = lax.all_to_all(sent, 'ctx', 0, 0, tiled=True)  95.5 us
    ppermute x5, starting transfers between devices, weight_gradient(): pieces = keep + lax.ppermute(send, 'calls', pairs)  30.2 us
    ppermute x2, starting transfers between devices, with_halo(): lax.ppermute(tail, axis, [(i, (i + 1) % count) for i in range(ends)])  13.2 us
    ppermute x1, waiting for transfers between devices, weight_gradient(): return lax.ppermute(summed, ('calls', 'ctx'), pairs)  12.1 us
    ppermute x5, waiting for transfers between devices, weight_gradient(): pieces = keep + lax.ppermute(send, 'calls', pairs)  11.4 us
    all_to_all x1, starting transfers between devices, weight_gradient(): got = lax.all_to_all(sent, 'ctx', 0, 0, tiled=True)  9.71 us
    ppermute x2, starting transfers between devices, with_halo(): lax.ppermute(head, axis, [((i + 1) % count, i) for i in range(ends)])  6.26 us
    unnamed x26, local copies, waits for them, and re-layouts  5.62 us
  transfers between devices with their start and end apart: 11, of which 8 were waited for; matrix products, arithmetic and copies ran while one was open for 8% of the time, Pallas kernels for 0%

profile of v4, /device:TPU:246, one launch (start us, length us, event | category | flops | bytes accessed | tf_op | source)
XLA Modules:
  0.0 240.7 jit_solution(14936262503468577418)
XLA Ops:
  0.6 1.9 copy-done
  4.8 3.1 %collective-permute-start.1 = (bf16[128,1024]{1,0:T(8,128)(2,1)}, bf16[128,1024]{1,0:T(8,128)(2,1)}, u32[]{:S(2)}, u32[]{:S(2)}) collective-permute-start(bf16[128,1024]{1,0:T(8,128)(2,1)} %slice.80), channel_id=1, source_target_pairs={{1,0},{2,1},{3,2},{4,3},{5,4},{6,5},{7,6},{8,7},{9,8},{10,9},{11,1... | collective-permute-start | bytes 786440 | tf_op jit(solution)/shard_map/ppermute | solution.py:22
  7.9 6.6 %collective-permute-start = (bf16[128,1024]{1,0:T(8,128)(2,1)}, bf16[128,1024]{1,0:T(8,128)(2,1)}, u32[]{:S(2)}, u32[]{:S(2)}) collective-permute-start(bf16[128,1024]{1,0:T(8,128)(2,1)} %slice.80), channel_id=1, source_target_pairs={{0,1},{1,2},{2,3},{3,4},{4,5},{5,6},{6,7},{7,8},{8,9},{9,10},{10,1... | collective-permute-start | bytes 786440 | tf_op jit(solution)/shard_map/ppermute | solution.py:20
  26.4 2.4 fusion.56
  28.8 2.3 fusion.26
  31.1 2.5 %fusion.33 = f32[4,128,384]{2,1,0:T(8,128)} fusion(bf16[128,4,128]{0,2,1:T(8,128)(2,1)S(1)} %bitcast.92, pred[128]{0:T(512)(128)(4,1)S(1)} %get-tuple-element.10, f32[4,128]{1,0:T(4,128)S(1)} %get-tuple-element.17, bf16[128,4,128]{0,2,1:T(8,128)(2,1)S(1)} %bitcast.102, bf16[384,4,128]{0,2,1:T(8,128)(2,1)} %bitcast.97, pred[128,384]{1,0:T(8,128)(4,1)} %fusion.38), kind=kOutput, calls=%fused_computation.47 | convolution fusion | flops 101712768 | bytes 1493120 | tf_op jit(solution)/shard_map/hfs,fhd->shd/dot_general | solution.py:69
  33.6 5.3 %fusion.16 = f32[4,128,384]{2,1,0:T(8,128)} fusion(bf16[128,4,128]{0,2,1:T(8,128)(2,1)S(1)} %bitcast.103, f32[4,128,384]{2,1,0:T(8,128)} %fusion.26, f32[4,128,384]{2,1,0:T(8,128)} %get-tuple-element.18, f32[4,128]{1,0:T(4,128)S(1)} %get-tuple-element.17), kind=kOutput, calls=%fused_computation.25 | convolution fusion | flops 51708800 | bytes 2492416 | tf_op jit(solution)/shard_map/hfs,fhd->shd/dot_general | solution.py:66
  41.3 3.1 %collective-permute-start.3 = (bf16[128,1024]{0,1:T(8,128)(2,1)}, bf16[128,1024]{0,1:T(8,128)(2,1)}, u32[]{:S(2)}, u32[]{:S(2)}) collective-permute-start(bf16[128,1024]{0,1:T(8,128)(2,1)} %get-tuple-element.12), channel_id=1, source_target_pairs={{1,0},{2,1},{3,2},{4,3},{5,4},{6,5},{7,6},{8,7},{9,8},{10,9},{11,1... | collective-permute-start | bytes 786440 | tf_op jit(solution)/shard_map/ppermute | solution.py:22
  44.4 6.6 %collective-permute-start.2 = (bf16[128,1024]{0,1:T(8,128)(2,1)}, bf16[128,1024]{0,1:T(8,128)(2,1)}, u32[]{:S(2)}, u32[]{:S(2)}) collective-permute-start(bf16[128,1024]{0,1:T(8,128)(2,1)} %get-tuple-element.11), channel_id=1, source_target_pairs={{0,1},{1,2},{2,3},{3,4},{4,5},{5,6},{6,7},{7,8},{8,9},{9,10},{10,1... | collective-permute-start | bytes 786440 | tf_op jit(solution)/shard_map/ppermute | solution.py:20
  53.1 4.5 %convolution_convert_fusion.2 = bf16[4,128,128]{2,1,0:T(8,128)(2,1)S(1)} fusion(bf16[384,4,128]{0,2,1:T(8,128)(2,1)} %bitcast.98, f32[4,128,384]{2,1,0:T(8,128)} %fusion.26, f32[4,128,384]{2,1,0:T(8,128)} %get-tuple-element.18, f32[4,128]{1,0:T(4,128)S(1)} %get-tuple-element.17), kind=kOutput, calls=%fused_computation.24 | convolution fusion | flops 51774336 | bytes 2099200 | tf_op jit(solution)/shard_map/hfs,shd->fhd/dot_general | solution.py:63
  57.6 2.1 collective-permute-done.2
  62.6 2.1 pad_maximum_fusion
  64.7 9.7 %all-to-all-start = ((bf16[32,128,448]{1,2,0:T(8,128)(2,1)}), bf16[32,128,448]{1,2,0:T(8,128)(2,1)}, u32[]{:S(2)}, u32[]{:S(2)}) async-start(bf16[32,128,448]{1,2,0:T(8,128)(2,1)} %bitcast.82), calls=%async_computation | async-start | bytes 7340032 | tf_op jit(solution)/shard_map/all_to_all | solution.py:95
  74.5 95.5 %all-to-all-done = bf16[32,128,448]{1,2,0:T(8,128)(2,1)} async-done(((bf16[32,128,448]{1,2,0:T(8,128)(2,1)}), bf16[32,128,448]{1,2,0:T(8,128)(2,1)}, u32[]{:S(2)}, u32[]{:S(2)}) %all-to-all-start) | async-done | bytes 3670048 | tf_op jit(solution)/shard_map/all_to_all | solution.py:95
  175.3 1.9 collective-permute-start.4
  180.1 1.9 collective-permute-start.5
  182.0 5.6 %collective-permute-done.5 = f32[2,2,2,32,48]{4,3,0,1,2:T(8,128)} collective-permute-done((f32[2,2,2,32,48]{4,3,0,1,2:T(8,128)S(1)}, f32[2,2,2,32,48]{4,3,0,1,2:T(8,128)}, u32[]{:S(2)}, u32[]{:S(2)}) %collective-permute-start.5) | collective-permute-done | bytes 49184 | tf_op jit(solution)/shard_map/ppermute | solution.py:109
  188.6 7.9 %collective-permute-start.6 = (f32[2,2,32,48]{3,2,0,1:T(8,128)S(1)}, f32[2,2,32,48]{3,2,0,1:T(8,128)S(1)}, u32[]{:S(2)}, u32[]{:S(2)}) collective-permute-start(f32[2,2,32,48]{3,2,0,1:T(8,128)S(1)} %select_bitcast_fusion.2), channel_id=1, source_target_pairs={{0,128},{32,160},{64,192},{96,224},{128,0},{160,32},{192,64},{224,... | collective-permute-start | bytes 73736 | tf_op jit(solution)/shard_map/ppermute | solution.py:109
  196.5 2.2 collective-permute-done.6
  198.8 11.9 %collective-permute-start.7 = (f32[2,32,48]{2,1,0:T(8,128)S(1)}, f32[2,32,48]{2,1,0:T(8,128)S(1)}, u32[]{:S(2)}, u32[]{:S(2)}) collective-permute-start(f32[2,32,48]{2,1,0:T(8,128)S(1)} %select_bitcast_fusion.3), channel_id=1, source_target_pairs={{0,256},{32,288},{64,320},{96,352},{128,384},{160,416},{192,448},{... | collective-permute-start | bytes 36872 | tf_op jit(solution)/shard_map/ppermute | solution.py:109
  212.6 6.6 %collective-permute-start.8 = (f32[32,48]{1,0:T(8,128)S(1)}, f32[32,48]{1,0:T(8,128)}, u32[]{:S(2)}, u32[]{:S(2)}) collective-permute-start(f32[32,48]{1,0:T(8,128)S(1)} %select_bitcast_fusion.4), channel_id=1, source_target_pairs={{0,512},{32,544},{64,576},{96,608},{128,640},{160,672},{192,704},{... | collective-permute-start | bytes 18440 | tf_op jit(solution)/shard_map/ppermute | solution.py:109
  219.2 2.6 %fusion.15 = bf16[4,128,128]{2,1,0:T(8,128)(2,1)} fusion(bf16[48,4,8,128]{3,2,1,0:T(8,128)(2,1)} %get-tuple-element.14, f32[128]{0:T(128)} %get-tuple-element.9, f32[4,128]{1,0:T(4,128)} %copy-done.11, bf16[128,4,128]{0,2,1:T(8,128)(2,1)} %bitcast.101, bf16[384,4,128]{0,2,1:T(8,128)(2,1)} %bitcast.99, pred[128,384]{1,0:T(8,128)(4,1)} %fusion.38), kind=kOutput, calls=%fused_computation.23 | convolution fusion | flops 101778304 | bytes 1100288 | tf_op jit(solution)/shard_map/hfs,shd->fhd/dot_general | solution.py:54
  224.2 1.9 collective-permute-start.9
  228.0 12.1 %collective-permute-done.9 = f32[32,48]{1,0:T(8,128)S(1)} collective-permute-done((f32[32,48]{1,0:T(8,128)S(1)}, f32[32,48]{1,0:T(8,128)S(1)}, u32[]{:S(2)}, u32[]{:S(2)}) %collective-permute-start.9) | collective-permute-done | bytes 6176 | tf_op jit(solution)/shard_map/ppermute | solution.py:117
  (67 shorter events, 36.6 us)
Async XLA Ops:
  0.6 1.9 copy-start
  4.8 16.9 %collective-permute-start.1 = (bf16[128,1024]{1,0:T(8,128)(2,1)}, bf16[128,1024]{1,0:T(8,128)(2,1)}, u32[]{:S(2)}, u32[]{:S(2)}) collective-permute-start(bf16[128,1024]{1,0:T(8,128)(2,1)} %slice.80), channel_id=1, source_target_pairs={{1,0},{2,1},{3,2},{4,3},{5,4},{6,5},{7,6},{8,7},{9,8},{10,9},{11,1... | collective-permute-start | bytes 786440 | tf_op jit(solution)/shard_map/ppermute | solution.py:22
  7.9 15.6 %collective-permute-start = (bf16[128,1024]{1,0:T(8,128)(2,1)}, bf16[128,1024]{1,0:T(8,128)(2,1)}, u32[]{:S(2)}, u32[]{:S(2)}) collective-permute-start(bf16[128,1024]{1,0:T(8,128)(2,1)} %slice.80), channel_id=1, source_target_pairs={{0,1},{1,2},{2,3},{3,4},{4,5},{5,6},{6,7},{7,8},{8,9},{9,10},{10,1... | collective-permute-start | bytes 786440 | tf_op jit(solution)/shard_map/ppermute | solution.py:20
  26.4 4.7 %copy-start.6 = (bf16[1,128,512]{1,2,0:T(8,128)(2,1)S(1)}, bf16[1,128,512]{1,2,0:T(8,128)(2,1)}, u32[]{:S(2)}) copy-start(bf16[1,128,512]{1,2,0:T(8,128)(2,1)} %copy.37) | copy-start | bytes 393220
  26.4 4.7 %copy-start.10 = (bf16[128,512]{0,1:T(8,128)(2,1)S(1)}, bf16[128,512]{0,1:T(8,128)(2,1)}, u32[]{:S(2)}) copy-start(bf16[128,512]{0,1:T(8,128)(2,1)} %copy.42) | copy-start | bytes 393220
  28.8 24.3 %copy-start.11 = (f32[4,128]{1,0:T(4,128)}, f32[4,128]{1,0:T(4,128)S(1)}, u32[]{:S(2)}) copy-start(f32[4,128]{1,0:T(4,128)S(1)} %get-tuple-element.17) | copy-start | bytes 6148
  38.9 12.1 %copy-start.5 = (bf16[1,128,1024]{2,1,0:T(8,128)(2,1)S(1)}, bf16[1,128,1024]{2,1,0:T(8,128)(2,1)}, u32[]{:S(2)}) copy-start(bf16[1,128,1024]{2,1,0:T(8,128)(2,1)} %param.4) | copy-start | bytes 786436
  41.3 16.3 %collective-permute-start.3 = (bf16[128,1024]{0,1:T(8,128)(2,1)}, bf16[128,1024]{0,1:T(8,128)(2,1)}, u32[]{:S(2)}, u32[]{:S(2)}) collective-permute-start(bf16[128,1024]{0,1:T(8,128)(2,1)} %get-tuple-element.12), channel_id=1, source_target_pairs={{1,0},{2,1},{3,2},{4,3},{5,4},{6,5},{7,6},{8,7},{9,8},{10,9},{11,1... | collective-permute-start | bytes 786440 | tf_op jit(solution)/shard_map/ppermute | solution.py:22
  44.4 15.3 %collective-permute-start.2 = (bf16[128,1024]{0,1:T(8,128)(2,1)}, bf16[128,1024]{0,1:T(8,128)(2,1)}, u32[]{:S(2)}, u32[]{:S(2)}) collective-permute-start(bf16[128,1024]{0,1:T(8,128)(2,1)} %get-tuple-element.11), channel_id=1, source_target_pairs={{0,1},{1,2},{2,3},{3,4},{4,5},{5,6},{6,7},{7,8},{8,9},{9,10},{10,1... | collective-permute-start | bytes 786440 | tf_op jit(solution)/shard_map/ppermute | solution.py:20
  57.6 4.5 %copy-start.7 = (bf16[4,128,128]{2,1,0:T(8,128)(2,1)}, bf16[4,128,128]{2,1,0:T(8,128)(2,1)S(1)}, u32[]{:S(2)}) copy-start(bf16[4,128,128]{2,1,0:T(8,128)(2,1)S(1)} %convolution_convert_fusion.2) | copy-start | bytes 393220
  61.0 0.7 copy-start.3
  64.7 105.2 %all-to-all-start = ((bf16[32,128,448]{1,2,0:T(8,128)(2,1)}), bf16[32,128,448]{1,2,0:T(8,128)(2,1)}, u32[]{:S(2)}, u32[]{:S(2)}) async-start(bf16[32,128,448]{1,2,0:T(8,128)(2,1)} %bitcast.82), calls=%async_computation | async-start | bytes 7340032 | tf_op jit(solution)/shard_map/all_to_all | solution.py:95
  174.5 0.7 copy-start.1
  174.5 0.8 copy-start.2
  175.3 3.5 %collective-permute-start.4 = (f32[2,2,2,2,32,48]{5,4,0,1,2,3:T(8,128)S(1)}, f32[2,2,2,2,32,48]{5,4,0,1,2,3:T(8,128)}, u32[]{:S(2)}, u32[]{:S(2)}) collective-permute-start(f32[2,2,2,2,32,48]{5,4,0,1,2,3:T(8,128)S(1)} %select_bitcast_fusion), channel_id=1, source_target_pairs={{0,32},{32,0},{64,96},{96,64},{128,160},{160,128},{192,224},{224,1... | collective-permute-start | bytes 294920 | tf_op jit(solution)/shard_map/ppermute | solution.py:109
  180.1 7.5 %collective-permute-start.5 = (f32[2,2,2,32,48]{4,3,0,1,2:T(8,128)S(1)}, f32[2,2,2,32,48]{4,3,0,1,2:T(8,128)}, u32[]{:S(2)}, u32[]{:S(2)}) collective-permute-start(f32[2,2,2,32,48]{4,3,0,1,2:T(8,128)S(1)} %select_bitcast_fusion.1), channel_id=1, source_target_pairs={{0,64},{32,96},{64,0},{96,32},{128,192},{160,224},{192,128},{224,1... | collective-permute-start | bytes 147464 | tf_op jit(solution)/shard_map/ppermute | solution.py:109
  188.6 10.2 %collective-permute-start.6 = (f32[2,2,32,48]{3,2,0,1:T(8,128)S(1)}, f32[2,2,32,48]{3,2,0,1:T(8,128)S(1)}, u32[]{:S(2)}, u32[]{:S(2)}) collective-permute-start(f32[2,2,32,48]{3,2,0,1:T(8,128)S(1)} %select_bitcast_fusion.2), channel_id=1, source_target_pairs={{0,128},{32,160},{64,192},{96,224},{128,0},{160,32},{192,64},{224,... | collective-permute-start | bytes 73736 | tf_op jit(solution)/shard_map/ppermute | solution.py:109
  198.8 13.7 %collective-permute-start.7 = (f32[2,32,48]{2,1,0:T(8,128)S(1)}, f32[2,32,48]{2,1,0:T(8,128)S(1)}, u32[]{:S(2)}, u32[]{:S(2)}) collective-permute-start(f32[2,32,48]{2,1,0:T(8,128)S(1)} %select_bitcast_fusion.3), channel_id=1, source_target_pairs={{0,256},{32,288},{64,320},{96,352},{128,384},{160,416},{192,448},{... | collective-permute-start | bytes 36872 | tf_op jit(solution)/shard_map/ppermute | solution.py:109
  212.6 6.6 %copy-start.9 = (f32[2,32,48]{2,1,0:T(8,128)}, f32[2,32,48]{2,1,0:T(8,128)S(1)}, u32[]{:S(2)}) copy-start(f32[2,32,48]{2,1,0:T(8,128)S(1)} %bitcast_add_fusion.3) | copy-start | bytes 36868
  212.6 10.8 %collective-permute-start.8 = (f32[32,48]{1,0:T(8,128)S(1)}, f32[32,48]{1,0:T(8,128)}, u32[]{:S(2)}, u32[]{:S(2)}) collective-permute-start(f32[32,48]{1,0:T(8,128)S(1)} %select_bitcast_fusion.4), channel_id=1, source_target_pairs={{0,512},{32,544},{64,576},{96,608},{128,640},{160,672},{192,704},{... | collective-permute-start | bytes 18440 | tf_op jit(solution)/shard_map/ppermute | solution.py:109
  219.2 6.9 %copy-start.4 = (bf16[128,1024]{0,1:T(8,128)(2,1)S(1)}, bf16[128,1024]{0,1:T(8,128)(2,1)}, u32[]{:S(2)}) copy-start(bf16[128,1024]{0,1:T(8,128)(2,1)} %copy-done.3) | copy-start | bytes 786436
  219.2 6.9 %copy-start.8 = (bf16[4,128,128]{2,1,0:T(8,128)(2,1)S(1)}, bf16[4,128,128]{2,1,0:T(8,128)(2,1)}, u32[]{:S(2)}) copy-start(bf16[4,128,128]{2,1,0:T(8,128)(2,1)} %copy-done.7) | copy-start | bytes 393220
  224.2 15.9 %collective-permute-start.9 = (f32[32,48]{1,0:T(8,128)S(1)}, f32[32,48]{1,0:T(8,128)S(1)}, u32[]{:S(2)}, u32[]{:S(2)}) collective-permute-start(f32[32,48]{1,0:T(8,128)S(1)} %bitcast_add_fusion.4), channel_id=1, source_target_pairs={{0,0},{1,4},{2,8},{3,12},{4,16},{5,20},{6,24},{7,28},{8,256},{9,26... | collective-permute-start | bytes 18440 | tf_op jit(solution)/shard_map/ppermute | solution.py:117

commit v5 on v2

--- a/solution.py
+++ b/solution.py
@@ -93,11 +93,11 @@
     col_factor = jnp.broadcast_to(col_factor, (row_parts, col_parts, frame_count, tile_cols))
     sent = jnp.concatenate([row_factor, col_factor], axis=3).reshape(ctx, frame_count, -1)
     got = lax.all_to_all(sent, "ctx", 0, 0, tiled=True)
-    tile = jnp.einsum(
-        "sfa,sfb->ab", got[..., :tile_rows], got[..., tile_rows:], preferred_element_type=jnp.float32
-    )
-    pieces = tile.reshape(rows_per_tile, block_rows, cols_per_tile, block_cols).transpose(0, 2, 1, 3)
-    pieces = pieces.reshape(calls, block_rows, block_cols)
+    row_pieces = got[..., :tile_rows].reshape(ctx, frame_count, rows_per_tile, 1, block_rows)
+    col_pieces = got[..., tile_rows:].reshape(ctx, frame_count, 1, cols_per_tile, block_cols)
+    pieces = jnp.einsum(
+        "sfiza,sfzjb->ijab", row_pieces, col_pieces, preferred_element_type=jnp.float32
+    ).reshape(calls, block_rows, block_cols)
     summed = jnp.sum(lax.all_to_all(pieces, "calls", 0, 0, tiled=True), axis=0)
     pairs = []
     for piece in range(calls):

time: 219 us -> 216 us (0.986)
  local copies, waits for them, and re-layouts: 22.9 us -> 20.1 us
    unnamed x12 -> x14, local copies, waits for them, and re-layouts: 8.35 us -> 8.35 us
where the time goes in v5:
time: 216 us; the launch traced here: 215 us
  blocking collectives  96.3 us (45%)
  starting transfers between devices  40.1 us (19%)
  matrix products  24.2 us (11%)
  waiting for transfers between devices  22.1 us (10%)
  local copies, waits for them, and re-layouts  20.1 us (9%)
  other arithmetic  10.5 us (5%)
    all_to_all x1, blocking collectives, weight_gradient(): got = lax.all_to_all(sent, 'ctx', 0, 0, tiled=True)  96.3 us
    all_to_all x1, starting transfers between devices, weight_gradient(): summed = jnp.sum(lax.all_to_all(pieces, 'calls', 0, 0, tiled=True), axis=0)  20.4 us
    ppermute x2, starting transfers between devices, with_halo(): lax.ppermute(tail, axis, [(i, (i + 1) % count) for i in range(ends)])  11 us
    ppermute x1, waiting for transfers between devices, weight_gradient(): return lax.ppermute(summed, ('calls', 'ctx'), pairs)  10.2 us
    unnamed x14, local copies, waits for them, and re-layouts  8.35 us
    ppermute x2, waiting for transfers between devices, with_halo(): lax.ppermute(tail, axis, [(i, (i + 1) % count) for i in range(ends)])  6.22 us
    ppermute x1, starting transfers between devices, weight_gradient(): return lax.ppermute(summed, ('calls', 'ctx'), pairs)  6.13 us
    all_to_all x1, waiting for transfers between devices, weight_gradient(): summed = jnp.sum(lax.all_to_all(pieces, 'calls', 0, 0, tiled=True), axis=0)  5.6 us
  transfers between devices with their start and end apart: 6, of which 4 were waited for; matrix products, arithmetic and copies ran while one was open for 9% of the time, Pallas kernels for 0%

profile of v5, /device:TPU:192, one launch (start us, length us, event | category | flops | bytes accessed | tf_op | source)
XLA Modules:
  0.0 214.7 jit_solution(12631521019347647703)
XLA Ops:
  0.6 1.9 copy-done
  2.5 1.5 convolution_convert_fusion
  6.1 5.3 %collective-permute-start = (bf16[128,1024]{1,0:T(8,128)(2,1)}, bf16[128,1024]{1,0:T(8,128)(2,1)}, u32[]{:S(2)}, u32[]{:S(2)}) collective-permute-start(bf16[128,1024]{1,0:T(8,128)(2,1)} %slice.40), channel_id=1, source_target_pairs={{0,1},{1,2},{2,3},{3,4},{4,5},{5,6},{6,7},{7,8},{8,9},{9,10},{10,1... | collective-permute-start | bytes 786440 | tf_op jit(solution)/shard_map/ppermute | solution.py:20
  13.7 1.7 copy.37
  15.4 1.7 copy.34
  18.5 1.8 collective-permute-done
  23.2 2.4 %fusion.60 = (f32[4,128]{1,0:T(4,128)S(1)}, f32[4,128,384]{2,1,0:T(8,128)}) fusion(bf16[128,4,128]{0,2,1:T(8,128)(2,1)} %bitcast.82, bf16[384,4,128]{0,2,1:T(8,128)(2,1)} %bitcast.78, pred[128,384]{1,0:T(8,128)(4,1)} %fusion.43), kind=kOutput, calls=%fused_computation.73 | convolution fusion | flops 51118464 | bytes 1361920 | tf_op jit(solution)/shard_map/sub | solution.py:50
  25.6 2.3 %fusion.31 = f32[4,128,384]{2,1,0:T(8,128)} fusion(bf16[48,4,8,128]{3,2,1,0:T(8,128)(2,1)} %get-tuple-element.14, bf16[128,4,128]{0,2,1:T(8,128)(2,1)} %bitcast.74, pred[128]{0:T(512)(128)(4,1)S(1)} %get-tuple-element.10), kind=kOutput, calls=%fused_computation.36 | convolution fusion | flops 50397184 | bytes 1310848 | tf_op jit(solution)/shard_map/fhd,shd->hfs/dot_general | solution.py:58
  27.9 2.5 %fusion.38 = f32[4,128,384]{2,1,0:T(8,128)} fusion(bf16[128,4,128]{0,2,1:T(8,128)(2,1)S(1)} %bitcast.75, pred[128]{0:T(512)(128)(4,1)S(1)} %get-tuple-element.10, f32[4,128]{1,0:T(4,128)S(1)} %get-tuple-element.15, bf16[128,4,128]{0,2,1:T(8,128)(2,1)S(1)} %bitcast.84, bf16[384,4,128]{0,2,1:T(8,128)(2,1)} %bitcast.79, pred[128,384]{1,0:T(8,128)(4,1)} %fusion.43), kind=kOutput, calls=%fused_computation.46 | convolution fusion | flops 101712768 | bytes 1493120 | tf_op jit(solution)/shard_map/hfs,fhd->shd/dot_general | solution.py:69
  30.4 5.3 %fusion.21 = f32[4,128,384]{2,1,0:T(8,128)} fusion(bf16[128,4,128]{0,2,1:T(8,128)(2,1)S(1)} %bitcast.85, f32[4,128,384]{2,1,0:T(8,128)} %fusion.31, f32[4,128,384]{2,1,0:T(8,128)} %get-tuple-element.16, f32[4,128]{1,0:T(4,128)S(1)} %get-tuple-element.15), kind=kOutput, calls=%fused_computation.26 | convolution fusion | flops 51708800 | bytes 2492416 | tf_op jit(solution)/shard_map/hfs,fhd->shd/dot_general | solution.py:66
  39.3 5.7 %collective-permute-start.2 = (bf16[128,1024]{0,1:T(8,128)(2,1)}, bf16[128,1024]{0,1:T(8,128)(2,1)}, u32[]{:S(2)}, u32[]{:S(2)}) collective-permute-start(bf16[128,1024]{0,1:T(8,128)(2,1)} %get-tuple-element.11), channel_id=1, source_target_pairs={{0,1},{1,2},{2,3},{3,4},{4,5},{5,6},{6,7},{7,8},{8,9},{9,10},{10,1... | collective-permute-start | bytes 786440 | tf_op jit(solution)/shard_map/ppermute | solution.py:20
  47.0 4.5 %convolution_convert_fusion.2 = bf16[4,128,128]{2,1,0:T(8,128)(2,1)S(1)} fusion(bf16[384,4,128]{0,2,1:T(8,128)(2,1)} %bitcast.80, f32[4,128,384]{2,1,0:T(8,128)} %fusion.31, f32[4,128,384]{2,1,0:T(8,128)} %get-tuple-element.16, f32[4,128]{1,0:T(4,128)S(1)} %get-tuple-element.15), kind=kOutput, calls=%fused_computation.25 | convolution fusion | flops 51774336 | bytes 2099200 | tf_op jit(solution)/shard_map/hfs,shd->fhd/dot_general | solution.py:63
  51.6 4.4 %collective-permute-done.2 = bf16[128,1024]{0,1:T(8,128)(2,1)} collective-permute-done((bf16[128,1024]{0,1:T(8,128)(2,1)}, bf16[128,1024]{0,1:T(8,128)(2,1)}, u32[]{:S(2)}, u32[]{:S(2)}) %collective-permute-start.2) | collective-permute-done | bytes 262176 | tf_op jit(solution)/shard_map/ppermute | solution.py:20
  58.5 96.3 %all_to_all.10 = bf16[32,128,448]{1,2,0:T(8,128)(2,1)S(1)} all-to-all(bf16[32,128,448]{1,2,0:T(8,128)(2,1)S(1)} %bitcast.64), channel_id=1, replica_groups=mesh['calls'=32,'ctx'=32] {'ctx'}, dimensions={0} | all-to-all | bytes 7340032 | tf_op jit(solution)/shard_map/all_to_all | solution.py:95
  157.1 2.2 %reshape.189 = f32[32,1,1536]{2,1,0:T(1,128)} reshape(f32[32,32,48]{2,1,0:T(8,128)} %bitcast.70) | data formatting | bytes 393216
  159.3 20.4 %all-to-all-start.1 = ((f32[32,1,1536]{2,1,0:T(1,128)}), f32[32,1,1536]{2,1,0:T(1,128)}, u32[]{:S(2)}, u32[]{:S(2)}) async-start(f32[32,1,1536]{2,1,0:T(1,128)} %reshape.189), calls=%async_computation.1 | async-start | bytes 393216 | tf_op jit(solution)/shard_map/all_to_all | solution.py:101
  179.8 2.5 %fusion.20 = bf16[4,128,128]{2,1,0:T(8,128)(2,1)} fusion(bf16[48,4,8,128]{3,2,1,0:T(8,128)(2,1)} %get-tuple-element.14, f32[128]{0:T(128)S(1)} %copy-done.4, f32[4,128]{1,0:T(4,128)S(1)} %get-tuple-element.15, bf16[128,4,128]{0,2,1:T(8,128)(2,1)} %bitcast.83, bf16[384,4,128]{0,2,1:T(8,128)(2,1)} %bitcast.81, pred[128,384]{1,0:T(8,128)(4,1)} %fusion.43), kind=kOutput, calls=%fused_computation.24 | convolution fusion | flops 101778304 | bytes 1100288 | tf_op jit(solution)/shard_map/hfs,shd->fhd/dot_general | solution.py:54
  182.3 1.7 copy.30
  184.0 5.6 %all-to-all-done.1 = f32[32,1,1536]{2,1,0:T(1,128)} async-done(((f32[32,1,1536]{2,1,0:T(1,128)}), f32[32,1,1536]{2,1,0:T(1,128)}, u32[]{:S(2)}, u32[]{:S(2)}) %all-to-all-start.1) | async-done | bytes 196640 | tf_op jit(solution)/shard_map/all_to_all | solution.py:101
  190.1 2.7 %reduce = f32[32,1536]{1,0:T(8,128)} reduce(f32[32,1,1536]{2,1,0:T(1,128)} %all-to-all-done.1, f32[]{:T(128)} %broadcast.137), dimensions={1}, to_apply=%all_to_all.7.reduce_sub_computation | reduce | bytes 393220 | tf_op jit(solution)/shard_map/all_to_all | solution.py:101
  192.8 2.0 reshape.190
  195.8 6.1 %collective-permute-start.4 = (f32[32,48]{1,0:T(8,128)S(1)}, f32[32,48]{1,0:T(8,128)S(1)}, u32[]{:S(2)}, u32[]{:S(2)}) collective-permute-start(f32[32,48]{1,0:T(8,128)S(1)} %reduce_sum.29), channel_id=1, source_target_pairs={{0,0},{1,4},{2,8},{3,12},{4,16},{5,20},{6,24},{7,28},{8,256},{9,26... | collective-permute-start | bytes 18440 | tf_op jit(solution)/shard_map/ppermute | solution.py:108
  202.0 1.9 fusion.19
  203.9 10.2 %collective-permute-done.4 = f32[32,48]{1,0:T(8,128)S(1)} collective-permute-done((f32[32,48]{1,0:T(8,128)S(1)}, f32[32,48]{1,0:T(8,128)S(1)}, u32[]{:S(2)}, u32[]{:S(2)}) %collective-permute-start.4) | collective-permute-done | bytes 6176 | tf_op jit(solution)/shard_map/ppermute | solution.py:108
  (39 shorter events, 20.7 us)
Async XLA Ops:
  0.6 1.9 copy-start
  4.8 13.7 %collective-permute-start.1 = (bf16[128,1024]{1,0:T(8,128)(2,1)}, bf16[128,1024]{1,0:T(8,128)(2,1)}, u32[]{:S(2)}, u32[]{:S(2)}) collective-permute-start(bf16[128,1024]{1,0:T(8,128)(2,1)} %slice.40), channel_id=1, source_target_pairs={{1,0},{2,1},{3,2},{4,3},{5,4},{6,5},{7,6},{8,7},{9,8},{10,9},{11,1... | collective-permute-start | bytes 786440 | tf_op jit(solution)/shard_map/ppermute | solution.py:22
  6.1 14.2 %collective-permute-start = (bf16[128,1024]{1,0:T(8,128)(2,1)}, bf16[128,1024]{1,0:T(8,128)(2,1)}, u32[]{:S(2)}, u32[]{:S(2)}) collective-permute-start(bf16[128,1024]{1,0:T(8,128)(2,1)} %slice.40), channel_id=1, source_target_pairs={{0,1},{1,2},{2,3},{3,4},{4,5},{5,6},{6,7},{7,8},{8,9},{9,10},{10,1... | collective-permute-start | bytes 786440 | tf_op jit(solution)/shard_map/ppermute | solution.py:20
  23.2 4.7 %copy-start.2 = (bf16[1,128,512]{1,2,0:T(8,128)(2,1)S(1)}, bf16[1,128,512]{1,2,0:T(8,128)(2,1)}, u32[]{:S(2)}) copy-start(bf16[1,128,512]{1,2,0:T(8,128)(2,1)} %copy.34) | copy-start | bytes 393220
  23.2 4.7 %copy-start.3 = (bf16[128,512]{0,1:T(8,128)(2,1)S(1)}, bf16[128,512]{0,1:T(8,128)(2,1)}, u32[]{:S(2)}) copy-start(bf16[128,512]{0,1:T(8,128)(2,1)} %copy.37) | copy-start | bytes 393220
  38.0 13.6 %collective-permute-start.3 = (bf16[128,1024]{0,1:T(8,128)(2,1)}, bf16[128,1024]{0,1:T(8,128)(2,1)}, u32[]{:S(2)}, u32[]{:S(2)}) collective-permute-start(bf16[128,1024]{0,1:T(8,128)(2,1)} %get-tuple-element.12), channel_id=1, source_target_pairs={{1,0},{2,1},{3,2},{4,3},{5,4},{6,5},{7,6},{8,7},{9,8},{10,9},{11,1... | collective-permute-start | bytes 786440 | tf_op jit(solution)/shard_map/ppermute | solution.py:22
  39.3 16.7 %collective-permute-start.2 = (bf16[128,1024]{0,1:T(8,128)(2,1)}, bf16[128,1024]{0,1:T(8,128)(2,1)}, u32[]{:S(2)}, u32[]{:S(2)}) collective-permute-start(bf16[128,1024]{0,1:T(8,128)(2,1)} %get-tuple-element.11), channel_id=1, source_target_pairs={{0,1},{1,2},{2,3},{3,4},{4,5},{5,6},{6,7},{7,8},{8,9},{9,10},{10,1... | collective-permute-start | bytes 786440 | tf_op jit(solution)/shard_map/ppermute | solution.py:20
  51.6 6.1 %copy-start.1 = (bf16[4,128,256]{1,2,0:T(8,128)(2,1)S(1)}, bf16[4,128,256]{1,2,0:T(8,128)(2,1)}, u32[]{:S(2)}) copy-start(bf16[4,128,256]{1,2,0:T(8,128)(2,1)} %copy.26) | copy-start | bytes 786436
  156.3 23.5 %copy-start.4 = (f32[128]{0:T(128)S(1)}, f32[128]{0:T(128)}, u32[]{:S(2)}) copy-start(f32[128]{0:T(128)} %get-tuple-element.9) | copy-start | bytes 1540
  159.3 30.2 %all-to-all-start.1 = ((f32[32,1,1536]{2,1,0:T(1,128)}), f32[32,1,1536]{2,1,0:T(1,128)}, u32[]{:S(2)}, u32[]{:S(2)}) async-start(f32[32,1,1536]{2,1,0:T(1,128)} %reshape.189), calls=%async_computation.1 | async-start | bytes 393216 | tf_op jit(solution)/shard_map/all_to_all | solution.py:101
  195.8 18.3 %collective-permute-start.4 = (f32[32,48]{1,0:T(8,128)S(1)}, f32[32,48]{1,0:T(8,128)S(1)}, u32[]{:S(2)}, u32[]{:S(2)}) collective-permute-start(f32[32,48]{1,0:T(8,128)S(1)} %reduce_sum.29), channel_id=1, source_target_pairs={{0,0},{1,4},{2,8},{3,12},{4,16},{5,20},{6,24},{7,28},{8,256},{9,26... | collective-permute-start | bytes 18440 | tf_op jit(solution)/shard_map/ppermute | solution.py:108

commit v6 on v0

--- a/solution.py
+++ b/solution.py
@@ -3,10 +3,11 @@
 import jax
 import jax.numpy as jnp
 from jax import lax
-from jax.sharding import PartitionSpec as P
+from jax.sharding import Mesh, PartitionSpec as P
 
 HEADS = 4
 WIN = 128
+CTX = ("cx", "cy")
 
 
 def with_halo(cells, sides, width):
@@ -74,16 +75,54 @@
     return (context, grad_query, grad_terms)
 
 
+def weight_gradient(frame_rows, grad_all):
+    frame_count, model_width = frame_rows.shape
+    grad_width = grad_all.shape[1]
+    calls = lax.axis_size("calls")
+    ring = lax.axis_size("cx")
+    group = lax.axis_size("cy")
+    ctx = ring * group
+    block_rows = model_width // calls
+    block_cols = grad_width // ctx
+    tile_rows = model_width // 2
+    tile_cols = grad_width // (group // 2)
+    row_factor = frame_rows.reshape(frame_count, 2, 1, tile_rows).transpose(1, 2, 0, 3)
+    col_factor = grad_all.reshape(frame_count, 1, group // 2, tile_cols).transpose(1, 2, 0, 3)
+    row_factor = jnp.broadcast_to(row_factor, (2, group // 2, frame_count, tile_rows))
+    col_factor = jnp.broadcast_to(col_factor, (2, group // 2, frame_count, tile_cols))
+    sent = jnp.concatenate([row_factor, col_factor], axis=3).reshape(group, frame_count, -1)
+    got = lax.all_to_all(sent, "cy", 0, 0, tiled=True)
+    pair_rows = tile_rows // (ring * block_rows)
+    row_pieces = got[..., :tile_rows].reshape(group, frame_count, ring, pair_rows, 1, block_rows)
+    col_pieces = got[..., tile_rows:].reshape(group, frame_count, 1, 1, -1, block_cols)
+    parts = jnp.einsum(
+        "sfpiza,sfzwjb->pijab", row_pieces, col_pieces, preferred_element_type=jnp.float32
+    ).reshape(ring, calls, block_rows * block_cols)
+    part = jnp.sum(lax.all_to_all(parts, "cx", 0, 0, tiled=True), axis=0)
+    summed = jnp.sum(lax.all_to_all(part, "calls", 0, 0, tiled=True), axis=0)
+    summed = summed.reshape(block_rows, block_cols)
+    col_pieces_per_tile = tile_cols // block_cols
+    pairs = []
+    for piece in range(calls):
+        for x in range(ring):
+            for y in range(group):
+                row_block = (y // (group // 2)) * (tile_rows // block_rows)
+                row_block += x * pair_rows + piece // col_pieces_per_tile
+                col_block = (y % (group // 2)) * col_pieces_per_tile + piece % col_pieces_per_tile
+                pairs.append(((piece * ring + x) * group + y, row_block * ctx + col_block))
+    return lax.ppermute(summed, ("calls", "cx", "cy"), pairs)
+
+
 def body(frames_in, w_qkv, out_grad, lengths):
     frame_rows = frames_in[0]
     frame_count, model_width = frame_rows.shape
     inner_width = w_qkv.shape[1] // 3
     window = WIN
-    offset = lax.axis_index("ctx") * frame_count
+    offset = lax.axis_index(CTX) * frame_count
     length_now = lengths[0]
     qkv = jnp.dot(frame_rows, w_qkv, preferred_element_type=jnp.float32).astype(jnp.bfloat16)
     queries = qkv[:, :inner_width]
-    key_value = with_halo(qkv[:, inner_width:], (("ctx", 0),), window)
+    key_value = with_halo(qkv[:, inner_width:], ((CTX, 0),), window)
     query_pos = offset + jnp.arange(frame_count, dtype=jnp.int32)
     key_pos = offset - window + jnp.arange(frame_count + 2 * window, dtype=jnp.int32)
     allowed = band_mask(query_pos, key_pos, length_now)
@@ -95,7 +134,7 @@
     rim_part = jnp.concatenate(
         [grad_terms[:window], grad_terms[window + frame_count :]], axis=0
     ).astype(jnp.bfloat16)
-    returned = with_halo(rim_part, (("ctx", 0),), window)
+    returned = with_halo(rim_part, ((CTX, 0),), window)
     from_left = returned[:window].astype(jnp.float32)
     from_right = returned[3 * window :].astype(jnp.float32)
     summed = own_part + from_left
@@ -105,15 +144,15 @@
     in_grad = lax.dot_general(
         grad_all, w_qkv, (((1,), (1,)), ((), ())), preferred_element_type=jnp.float32
     ).astype(jnp.bfloat16)
-    term = lax.dot_general(
-        frame_rows, grad_all, (((0,), (0,)), ((), ())), preferred_element_type=jnp.float32
-    )
-    partial_grad = lax.psum_scatter(term, "calls", scatter_dimension=0, tiled=True)
-    weight_grad = lax.psum_scatter(partial_grad, "ctx", scatter_dimension=1, tiled=True)
+    weight_grad = weight_gradient(frame_rows, grad_all)
     return (context[None], in_grad[None], weight_grad)
 
 
 def solution(mesh):
-    in_specs = (P("calls", "ctx", None), P(), P("calls", "ctx", None), P("calls"))
-    out_specs = (P("calls", "ctx", None), P("calls", "ctx", None), P("calls", "ctx"))
-    return jax.shard_map(body, mesh=mesh, in_specs=in_specs, out_specs=out_specs, check_vma=False)
+    calls, ctx = mesh.devices.shape
+    group = 4
+    fine = Mesh(mesh.devices.reshape(calls, ctx // group, group), ("calls",) + CTX)
+    frames = P("calls", CTX, None)
+    in_specs = (frames, P(), frames, P("calls"))
+    out_specs = (frames, frames, P("calls", CTX))
+    return jax.shard_map(body, mesh=fine, in_specs=in_specs, out_specs=out_specs, check_vma=False)

time: 434 us -> 206 us (0.47)
  the two profiles are of different devices: /device:TPU:118 before, /device:TPU:5 now
where the time goes in v6:
time: 206 us; the launch traced here: 205 us
  blocking collectives  76.5 us (37%)
  starting transfers between devices  45.8 us (22%)
  local copies, waits for them, and re-layouts  24.2 us (12%)
  matrix products  24.2 us (12%)
  waiting for transfers between devices  23.4 us (11%)
  other arithmetic  9.8 us (5%)
    all_to_all x1, blocking collectives, weight_gradient(): part = jnp.sum(lax.all_to_all(parts, 'cx', 0, 0, tiled=True), axis=0)  43.2 us
    all_to_all x1, blocking collectives, weight_gradient(): got = lax.all_to_all(sent, 'cy', 0, 0, tiled=True)  33.3 us
    all_to_all x1, starting transfers between devices, weight_gradient(): summed = jnp.sum(lax.all_to_all(part, 'calls', 0, 0, tiled=True), axis=0)  23.4 us
    ppermute x2, starting transfers between devices, with_halo(): lax.ppermute(head, axis, [((i + 1) % count, i) for i in range(ends)])  9.4 us
    all_to_all x1, waiting for transfers between devices, weight_gradient(): summed = jnp.sum(lax.all_to_all(part, 'calls', 0, 0, tiled=True), axis=0)  8.42 us
    ppermute x1, waiting for transfers between devices, weight_gradient(): return lax.ppermute(summed, ('calls', 'cx', 'cy'), pairs)  7.05 us
    ppermute x1, starting transfers between devices, weight_gradient(): return lax.ppermute(summed, ('calls', 'cx', 'cy'), pairs)  7 us
    ppermute x2, starting transfers between devices, with_halo(): lax.ppermute(tail, axis, [(i, (i + 1) % count) for i in range(ends)])  6.03 us
  transfers between devices with their start and end apart: 6, of which 4 were waited for; matrix products, arithmetic and copies ran while one was open for 9% of the time, Pallas kernels for 0%

profile of v6, /device:TPU:5, one launch (start us, length us, event | category | flops | bytes accessed | tf_op | source)
XLA Modules:
  0.0 205.4 jit_solution(7881297804102578813)
XLA Ops:
  0.6 1.9 copy-done
  4.8 5.5 %collective-permute-start.1 = (bf16[128,1024]{1,0:T(8,128)(2,1)}, bf16[128,1024]{1,0:T(8,128)(2,1)}, u32[]{:S(2)}, u32[]{:S(2)}) collective-permute-start(bf16[128,1024]{1,0:T(8,128)(2,1)} %slice.40), channel_id=1, source_target_pairs={{1,0},{2,1},{3,2},{4,3},{5,4},{6,5},{7,6},{8,7},{9,8},{10,9},{11,1... | collective-permute-start | bytes 786440 | tf_op jit(solution)/shard_map/ppermute | solution.py:23
  10.3 1.9 collective-permute-start
  19.5 3.8 %collective-permute-done = bf16[128,1024]{1,0:T(8,128)(2,1)} collective-permute-done((bf16[128,1024]{1,0:T(8,128)(2,1)}, bf16[128,1024]{1,0:T(8,128)(2,1)}, u32[]{:S(2)}, u32[]{:S(2)}) %collective-permute-start) | collective-permute-done | bytes 262176 | tf_op jit(solution)/shard_map/ppermute | solution.py:21
  26.1 2.3 %fusion.25 = f32[4,128,384]{2,1,0:T(8,128)} fusion(bf16[48,4,8,128]{3,2,1,0:T(8,128)(2,1)} %get-tuple-element.17, bf16[128,4,128]{0,2,1:T(8,128)(2,1)} %bitcast.71, pred[128]{0:T(512)(128)(4,1)S(1)} %get-tuple-element.13), kind=kOutput, calls=%fused_computation.35 | convolution fusion | flops 50397184 | bytes 1310848 | tf_op jit(solution)/shard_map/fhd,shd->hfs/dot_general | solution.py:59
  28.5 2.3 %fusion.54 = (f32[4,128]{1,0:T(4,128)S(1)}, f32[4,128,384]{2,1,0:T(8,128)}) fusion(bf16[128,4,128]{0,2,1:T(8,128)(2,1)} %bitcast.80, bf16[384,4,128]{0,2,1:T(8,128)(2,1)} %bitcast.76, pred[128,384]{1,0:T(8,128)(4,1)} %fusion.37), kind=kOutput, calls=%fused_computation.72 | convolution fusion | flops 51118464 | bytes 1361920 | tf_op jit(solution)/shard_map/sub | solution.py:51
  30.8 2.5 %fusion.32 = f32[4,128,384]{2,1,0:T(8,128)} fusion(bf16[128,4,128]{0,2,1:T(8,128)(2,1)S(1)} %bitcast.72, pred[128]{0:T(512)(128)(4,1)S(1)} %get-tuple-element.13, f32[4,128]{1,0:T(4,128)S(1)} %get-tuple-element.18, bf16[128,4,128]{0,2,1:T(8,128)(2,1)S(1)} %bitcast.82, bf16[384,4,128]{0,2,1:T(8,128)(2,1)} %bitcast.77, pred[128,384]{1,0:T(8,128)(4,1)} %fusion.37), kind=kOutput, calls=%fused_computation.45 | convolution fusion | flops 101712768 | bytes 1493120 | tf_op jit(solution)/shard_map/hfs,fhd->shd/dot_general | solution.py:70
  33.3 5.3 %fusion.12 = f32[4,128,384]{2,1,0:T(8,128)} fusion(bf16[128,4,128]{0,2,1:T(8,128)(2,1)S(1)} %bitcast.83, f32[4,128,384]{2,1,0:T(8,128)} %fusion.25, f32[4,128,384]{2,1,0:T(8,128)} %get-tuple-element.19, f32[4,128]{1,0:T(4,128)S(1)} %get-tuple-element.18), kind=kOutput, calls=%fused_computation.22 | convolution fusion | flops 51708800 | bytes 2492416 | tf_op jit(solution)/shard_map/hfs,fhd->shd/dot_general | solution.py:67
  40.9 4.1 %collective-permute-start.2 = (bf16[128,1024]{0,1:T(8,128)(2,1)}, bf16[128,1024]{0,1:T(8,128)(2,1)}, u32[]{:S(2)}, u32[]{:S(2)}) collective-permute-start(bf16[128,1024]{0,1:T(8,128)(2,1)} %get-tuple-element.14), channel_id=1, source_target_pairs={{0,1},{1,2},{2,3},{3,4},{4,5},{5,6},{6,7},{7,8},{8,9},{9,10},{10,1... | collective-permute-start | bytes 786440 | tf_op jit(solution)/shard_map/ppermute | solution.py:21
  45.0 3.9 %collective-permute-start.3 = (bf16[128,1024]{0,1:T(8,128)(2,1)}, bf16[128,1024]{0,1:T(8,128)(2,1)}, u32[]{:S(2)}, u32[]{:S(2)}) collective-permute-start(bf16[128,1024]{0,1:T(8,128)(2,1)} %get-tuple-element.15), channel_id=1, source_target_pairs={{1,0},{2,1},{3,2},{4,3},{5,4},{6,5},{7,6},{8,7},{9,8},{10,9},{11,1... | collective-permute-start | bytes 786440 | tf_op jit(solution)/shard_map/ppermute | solution.py:23
  51.0 4.5 %convolution_convert_fusion.2 = bf16[4,128,128]{2,1,0:T(8,128)(2,1)S(1)} fusion(bf16[384,4,128]{0,2,1:T(8,128)(2,1)} %bitcast.78, f32[4,128,384]{2,1,0:T(8,128)} %fusion.25, f32[4,128,384]{2,1,0:T(8,128)} %get-tuple-element.19, f32[4,128]{1,0:T(4,128)S(1)} %get-tuple-element.18), kind=kOutput, calls=%fused_computation.21 | convolution fusion | flops 51774336 | bytes 2099200 | tf_op jit(solution)/shard_map/hfs,shd->fhd/dot_general | solution.py:64
  55.5 4.1 %collective-permute-done.3 = bf16[128,1024]{0,1:T(8,128)(2,1)} collective-permute-done((bf16[128,1024]{0,1:T(8,128)(2,1)}, bf16[128,1024]{0,1:T(8,128)(2,1)}, u32[]{:S(2)}, u32[]{:S(2)}) %collective-permute-start.3) | collective-permute-done | bytes 262176 | tf_op jit(solution)/shard_map/ppermute | solution.py:23
  61.3 33.3 %all_to_all.19 = bf16[4,128,1280]{1,2,0:T(8,128)(2,1)S(1)} all-to-all(bf16[4,128,1280]{1,2,0:T(8,128)(2,1)S(1)} %bitcast.63), channel_id=1, replica_groups=mesh['calls'=32,'cx'=8,'cy'=4] {'cy'}, dimensions={0} | all-to-all | bytes 2621440 | tf_op jit(solution)/shard_map/all_to_all | solution.py:94
  95.9 2.6 %copy.42 = f32[8,2,16,32,48]{4,3,2,1,0:T(8,128)} copy(f32[8,2,16,32,48]{4,3,1,0,2:T(8,128)S(1)} %convolution_bitcast_fusion) | data formatting | bytes 3145728 | tf_op jit(solution)/shard_map/sfpiza,sfzwjb->pijab/transpose | solution.py:98
  98.5 5.4 %reshape.192 = f32[8,32,1536]{2,1,0:T(8,128)} reshape(f32[8,2,16,32,48]{4,3,2,1,0:T(8,128)} %copy.42) | data formatting | bytes 3145728 | tf_op jit(solution)/shard_map/reshape | solution.py:100
  103.9 43.2 %all_to_all.20 = f32[8,32,1536]{2,1,0:T(8,128)} all-to-all(f32[8,32,1536]{2,1,0:T(8,128)} %reshape.192), channel_id=1, replica_groups=mesh['calls'=32,'cx'=8,'cy'=4] {'cx'}, dimensions={0} | all-to-all | bytes 3145728 | tf_op jit(solution)/shard_map/all_to_all | solution.py:101
  147.2 2.2 %reduce_sum.42 = f32[32,1536]{1,0:T(8,128)} reduce(f32[8,32,1536]{2,1,0:T(8,128)} %all_to_all.20, f32[]{:T(128)} %constant.24.clone.1), dimensions={0}, to_apply=%region_3.4 | reduce | flops 344064 | bytes 1769476 | tf_op jit(solution)/shard_map/reduce_sum | solution.py:101
  149.3 1.7 all_to_all.14
  151.1 23.4 %all-to-all-start.2 = ((f32[32,1,1536]{2,1,0:T(1,128)}), f32[32,1,1536]{2,1,0:T(1,128)}, u32[]{:S(2)}, u32[]{:S(2)}) async-start(f32[32,1,1536]{2,1,0:T(1,128)} %all_to_all.14), calls=%async_computation.2 | async-start | bytes 393216 | tf_op jit(solution)/shard_map/all_to_all | solution.py:102
  174.5 2.5 %fusion.11 = bf16[4,128,128]{2,1,0:T(8,128)(2,1)} fusion(bf16[48,4,8,128]{3,2,1,0:T(8,128)(2,1)} %get-tuple-element.17, f32[128]{0:T(128)S(1)} %copy-done.4, f32[4,128]{1,0:T(4,128)S(1)} %get-tuple-element.18, bf16[128,4,128]{0,2,1:T(8,128)(2,1)} %bitcast.81, bf16[384,4,128]{0,2,1:T(8,128)(2,1)} %bitcast.79, pred[128,384]{1,0:T(8,128)(4,1)} %fusion.37), kind=kOutput, calls=%fused_computation.20 | convolution fusion | flops 101778304 | bytes 1100288 | tf_op jit(solution)/shard_map/hfs,shd->fhd/dot_general | solution.py:55
  178.7 8.4 %all-to-all-done.2 = f32[32,1,1536]{2,1,0:T(1,128)} async-done(((f32[32,1,1536]{2,1,0:T(1,128)}), f32[32,1,1536]{2,1,0:T(1,128)}, u32[]{:S(2)}, u32[]{:S(2)}) %all-to-all-start.2) | async-done | bytes 196640 | tf_op jit(solution)/shard_map/all_to_all | solution.py:102
  188.8 7.0 %collective-permute-start.4 = (f32[32,48]{1,0:T(8,128)}, f32[32,48]{1,0:T(8,128)S(1)}, u32[]{:S(2)}, u32[]{:S(2)}) collective-permute-start(f32[32,48]{1,0:T(8,128)} %reshape.193), channel_id=1, source_target_pairs={{0,0},{1,16},{2,512},{3,528},{4,64},{5,80},{6,576},{7,592},{8,128}... | collective-permute-start | bytes 18440 | tf_op jit(solution)/shard_map/ppermute | solution.py:113
  195.8 1.9 fusion.10
  197.7 7.0 %collective-permute-done.4 = f32[32,48]{1,0:T(8,128)S(1)} collective-permute-done((f32[32,48]{1,0:T(8,128)}, f32[32,48]{1,0:T(8,128)S(1)}, u32[]{:S(2)}, u32[]{:S(2)}) %collective-permute-start.4) | collective-permute-done | bytes 6176 | tf_op jit(solution)/shard_map/ppermute | solution.py:113
  (40 shorter events, 23.0 us)
Async XLA Ops:
  0.6 1.9 copy-start
  4.8 14.6 %collective-permute-start.1 = (bf16[128,1024]{1,0:T(8,128)(2,1)}, bf16[128,1024]{1,0:T(8,128)(2,1)}, u32[]{:S(2)}, u32[]{:S(2)}) collective-permute-start(bf16[128,1024]{1,0:T(8,128)(2,1)} %slice.40), channel_id=1, source_target_pairs={{1,0},{2,1},{3,2},{4,3},{5,4},{6,5},{7,6},{8,7},{9,8},{10,9},{11,1... | collective-permute-start | bytes 786440 | tf_op jit(solution)/shard_map/ppermute | solution.py:23
  10.3 12.9 %collective-permute-start = (bf16[128,1024]{1,0:T(8,128)(2,1)}, bf16[128,1024]{1,0:T(8,128)(2,1)}, u32[]{:S(2)}, u32[]{:S(2)}) collective-permute-start(bf16[128,1024]{1,0:T(8,128)(2,1)} %slice.40), channel_id=1, source_target_pairs={{0,1},{1,2},{2,3},{3,4},{4,5},{5,6},{6,7},{7,8},{8,9},{9,10},{10,1... | collective-permute-start | bytes 786440 | tf_op jit(solution)/shard_map/ppermute | solution.py:21
  26.1 4.7 %copy-start.2 = (bf16[1,128,512]{1,2,0:T(8,128)(2,1)S(1)}, bf16[1,128,512]{1,2,0:T(8,128)(2,1)}, u32[]{:S(2)}) copy-start(bf16[1,128,512]{1,2,0:T(8,128)(2,1)} %copy.47) | copy-start | bytes 393220
  26.1 4.7 %copy-start.3 = (bf16[128,512]{0,1:T(8,128)(2,1)S(1)}, bf16[128,512]{0,1:T(8,128)(2,1)}, u32[]{:S(2)}) copy-start(bf16[128,512]{0,1:T(8,128)(2,1)} %copy.50) | copy-start | bytes 393220
  40.9 14.6 %collective-permute-start.2 = (bf16[128,1024]{0,1:T(8,128)(2,1)}, bf16[128,1024]{0,1:T(8,128)(2,1)}, u32[]{:S(2)}, u32[]{:S(2)}) collective-permute-start(bf16[128,1024]{0,1:T(8,128)(2,1)} %get-tuple-element.14), channel_id=1, source_target_pairs={{0,1},{1,2},{2,3},{3,4},{4,5},{5,6},{6,7},{7,8},{8,9},{9,10},{10,1... | collective-permute-start | bytes 786440 | tf_op jit(solution)/shard_map/ppermute | solution.py:21
  45.0 14.6 %collective-permute-start.3 = (bf16[128,1024]{0,1:T(8,128)(2,1)}, bf16[128,1024]{0,1:T(8,128)(2,1)}, u32[]{:S(2)}, u32[]{:S(2)}) collective-permute-start(bf16[128,1024]{0,1:T(8,128)(2,1)} %get-tuple-element.15), channel_id=1, source_target_pairs={{1,0},{2,1},{3,2},{4,3},{5,4},{6,5},{7,6},{8,7},{9,8},{10,9},{11,1... | collective-permute-start | bytes 786440 | tf_op jit(solution)/shard_map/ppermute | solution.py:23
  55.5 5.5 %copy-start.1 = (bf16[2,128,512]{1,2,0:T(8,128)(2,1)S(1)}, bf16[2,128,512]{1,2,0:T(8,128)(2,1)}, u32[]{:S(2)}) copy-start(bf16[2,128,512]{1,2,0:T(8,128)(2,1)} %copy.39) | copy-start | bytes 786436
  147.2 27.3 %copy-start.4 = (f32[128]{0:T(128)S(1)}, f32[128]{0:T(128)}, u32[]{:S(2)}) copy-start(f32[128]{0:T(128)} %get-tuple-element.12) | copy-start | bytes 1540
  151.1 36.0 %all-to-all-start.2 = ((f32[32,1,1536]{2,1,0:T(1,128)}), f32[32,1,1536]{2,1,0:T(1,128)}, u32[]{:S(2)}, u32[]{:S(2)}) async-start(f32[32,1,1536]{2,1,0:T(1,128)} %all_to_all.14), calls=%async_computation.2 | async-start | bytes 393216 | tf_op jit(solution)/shard_map/all_to_all | solution.py:102
  188.8 15.9 %collective-permute-start.4 = (f32[32,48]{1,0:T(8,128)}, f32[32,48]{1,0:T(8,128)S(1)}, u32[]{:S(2)}, u32[]{:S(2)}) collective-permute-start(f32[32,48]{1,0:T(8,128)} %reshape.193), channel_id=1, source_target_pairs={{0,0},{1,16},{2,512},{3,528},{4,64},{5,80},{6,576},{7,592},{8,128}... | collective-permute-start | bytes 18440 | tf_op jit(solution)/shard_map/ppermute | solution.py:113

commit v7 on v6

--- a/solution.py
+++ b/solution.py
@@ -93,12 +93,13 @@
     sent = jnp.concatenate([row_factor, col_factor], axis=3).reshape(group, frame_count, -1)
     got = lax.all_to_all(sent, "cy", 0, 0, tiled=True)
     pair_rows = tile_rows // (ring * block_rows)
-    row_pieces = got[..., :tile_rows].reshape(group, frame_count, ring, pair_rows, 1, block_rows)
-    col_pieces = got[..., tile_rows:].reshape(group, frame_count, 1, 1, -1, block_cols)
-    parts = jnp.einsum(
-        "sfpiza,sfzwjb->pijab", row_pieces, col_pieces, preferred_element_type=jnp.float32
-    ).reshape(ring, calls, block_rows * block_cols)
+    tile = jnp.einsum(
+        "sfa,sfb->ab", got[..., :tile_rows], got[..., tile_rows:], preferred_element_type=jnp.float32
+    )
+    parts = tile.reshape(ring, pair_rows * block_rows, tile_cols)
     part = jnp.sum(lax.all_to_all(parts, "cx", 0, 0, tiled=True), axis=0)
+    part = part.reshape(pair_rows, block_rows, -1, block_cols).transpose(0, 2, 1, 3)
+    part = part.reshape(calls, block_rows * block_cols)
     summed = jnp.sum(lax.all_to_all(part, "calls", 0, 0, tiled=True), axis=0)
     summed = summed.reshape(block_rows, block_cols)
     col_pieces_per_tile = tile_cols // block_cols

time: 206 us -> 206 us (level)
    reshape x1, local copies, waits for them, and re-layouts: 5.42 us -> 1.98 us  [weight_gradient(): part.reshape(pair_rows, block_rows, -1, block_cols).transpose(0, 2, 1, 3)]
    broadcast_in_dim x1 -> x2, local copies, waits for them, and re-layouts: 0.1 us -> 2.95 us  [weight_gradient(): jnp.broadcast_to(col_factor, (2, group // 2, frame_count, tile_cols))]
    unnamed x12 -> x10, local copies, waits for them, and re-layouts: 4.17 us -> 4.17 us
where the time goes in v7:
time: 206 us; the launch traced here: 205 us
  blocking collectives  76.4 us (37%)
  starting transfers between devices  45.8 us (22%)
  local copies, waits for them, and re-layouts  24.1 us (12%)
  waiting for transfers between devices  23.6 us (11%)
  matrix products  23.5 us (11%)
  other arithmetic  10.5 us (5%)
    all_to_all x1, blocking collectives, weight_gradient(): part = jnp.sum(lax.all_to_all(parts, 'cx', 0, 0, tiled=True), axis=0)  43 us
    all_to_all x1, blocking collectives, weight_gradient(): got = lax.all_to_all(sent, 'cy', 0, 0, tiled=True)  33.3 us
    all_to_all x1, starting transfers between devices, weight_gradient(): summed = jnp.sum(lax.all_to_all(part, 'calls', 0, 0, tiled=True), axis=0)  23.4 us
    ppermute x2, starting transfers between devices, with_halo(): lax.ppermute(head, axis, [((i + 1) % count, i) for i in range(ends)])  9.4 us
    all_to_all x1, waiting for transfers between devices, weight_gradient(): summed = jnp.sum(lax.all_to_all(part, 'calls', 0, 0, tiled=True), axis=0)  8.43 us
    ppermute x1, waiting for transfers between devices, weight_gradient(): return lax.ppermute(summed, ('calls', 'cx', 'cy'), pairs)  7.05 us
    ppermute x1, starting transfers between devices, weight_gradient(): return lax.ppermute(summed, ('calls', 'cx', 'cy'), pairs)  7.01 us
    ppermute x2, starting transfers between devices, with_halo(): lax.ppermute(tail, axis, [(i, (i + 1) % count) for i in range(ends)])  6.03 us
  transfers between devices with their start and end apart: 6, of which 4 were waited for; matrix products, arithmetic and copies ran while one was open for 9% of the time, Pallas kernels for 0%

profile of v7, /device:TPU:5, one launch (start us, length us, event | category | flops | bytes accessed | tf_op | source)
XLA Modules:
  0.0 205.4 jit_solution(5878510813269544835)
XLA Ops:
  0.6 1.9 copy-done
  4.8 5.5 %collective-permute-start.1 = (bf16[128,1024]{1,0:T(8,128)(2,1)}, bf16[128,1024]{1,0:T(8,128)(2,1)}, u32[]{:S(2)}, u32[]{:S(2)}) collective-permute-start(bf16[128,1024]{1,0:T(8,128)(2,1)} %slice.40), channel_id=1, source_target_pairs={{1,0},{2,1},{3,2},{4,3},{5,4},{6,5},{7,6},{8,7},{9,8},{10,9},{11,1... | collective-permute-start | bytes 786440 | tf_op jit(solution)/shard_map/ppermute | solution.py:23
  10.3 1.9 collective-permute-start
  19.4 3.8 %collective-permute-done = bf16[128,1024]{1,0:T(8,128)(2,1)} collective-permute-done((bf16[128,1024]{1,0:T(8,128)(2,1)}, bf16[128,1024]{1,0:T(8,128)(2,1)}, u32[]{:S(2)}, u32[]{:S(2)}) %collective-permute-start) | collective-permute-done | bytes 262176 | tf_op jit(solution)/shard_map/ppermute | solution.py:21
  26.1 2.3 %fusion.25 = f32[4,128,384]{2,1,0:T(8,128)} fusion(bf16[48,4,8,128]{3,2,1,0:T(8,128)(2,1)} %get-tuple-element.20, bf16[128,4,128]{0,2,1:T(8,128)(2,1)} %bitcast.64, pred[128]{0:T(512)(128)(4,1)S(1)} %get-tuple-element.16), kind=kOutput, calls=%fused_computation.34 | convolution fusion | flops 50397184 | bytes 1310848 | tf_op jit(solution)/shard_map/fhd,shd->hfs/dot_general | solution.py:59
  28.5 2.3 %fusion.54 = (f32[4,128]{1,0:T(4,128)S(1)}, f32[4,128,384]{2,1,0:T(8,128)}) fusion(bf16[128,4,128]{0,2,1:T(8,128)(2,1)} %bitcast.72, bf16[384,4,128]{0,2,1:T(8,128)(2,1)} %bitcast.68, pred[128,384]{1,0:T(8,128)(4,1)} %fusion.37), kind=kOutput, calls=%fused_computation.71 | convolution fusion | flops 51118464 | bytes 1361920 | tf_op jit(solution)/shard_map/sub | solution.py:51
  30.8 2.5 %fusion.32 = f32[4,128,384]{2,1,0:T(8,128)} fusion(bf16[128,4,128]{0,2,1:T(8,128)(2,1)S(1)} %bitcast.65, pred[128]{0:T(512)(128)(4,1)S(1)} %get-tuple-element.16, f32[4,128]{1,0:T(4,128)S(1)} %get-tuple-element.21, bf16[128,4,128]{0,2,1:T(8,128)(2,1)S(1)} %bitcast.74, bf16[384,4,128]{0,2,1:T(8,128)(2,1)} %bitcast.69, pred[128,384]{1,0:T(8,128)(4,1)} %fusion.37), kind=kOutput, calls=%fused_computation.44 | convolution fusion | flops 101712768 | bytes 1493120 | tf_op jit(solution)/shard_map/hfs,fhd->shd/dot_general | solution.py:70
  33.3 5.3 %fusion.12 = f32[4,128,384]{2,1,0:T(8,128)} fusion(bf16[128,4,128]{0,2,1:T(8,128)(2,1)S(1)} %bitcast.75, f32[4,128,384]{2,1,0:T(8,128)} %fusion.25, f32[4,128,384]{2,1,0:T(8,128)} %get-tuple-element.22, f32[4,128]{1,0:T(4,128)S(1)} %get-tuple-element.21), kind=kOutput, calls=%fused_computation.21 | convolution fusion | flops 51708800 | bytes 2492416 | tf_op jit(solution)/shard_map/hfs,fhd->shd/dot_general | solution.py:67
  40.9 4.1 %collective-permute-start.2 = (bf16[128,1024]{0,1:T(8,128)(2,1)}, bf16[128,1024]{0,1:T(8,128)(2,1)}, u32[]{:S(2)}, u32[]{:S(2)}) collective-permute-start(bf16[128,1024]{0,1:T(8,128)(2,1)} %get-tuple-element.17), channel_id=1, source_target_pairs={{0,1},{1,2},{2,3},{3,4},{4,5},{5,6},{6,7},{7,8},{8,9},{9,10},{10,1... | collective-permute-start | bytes 786440 | tf_op jit(solution)/shard_map/ppermute | solution.py:21
  45.0 3.9 %collective-permute-start.3 = (bf16[128,1024]{0,1:T(8,128)(2,1)}, bf16[128,1024]{0,1:T(8,128)(2,1)}, u32[]{:S(2)}, u32[]{:S(2)}) collective-permute-start(bf16[128,1024]{0,1:T(8,128)(2,1)} %get-tuple-element.18), channel_id=1, source_target_pairs={{1,0},{2,1},{3,2},{4,3},{5,4},{6,5},{7,6},{8,7},{9,8},{10,9},{11,1... | collective-permute-start | bytes 786440 | tf_op jit(solution)/shard_map/ppermute | solution.py:23
  50.8 4.5 %convolution_convert_fusion.2 = bf16[4,128,128]{2,1,0:T(8,128)(2,1)S(1)} fusion(bf16[384,4,128]{0,2,1:T(8,128)(2,1)} %bitcast.70, f32[4,128,384]{2,1,0:T(8,128)} %fusion.25, f32[4,128,384]{2,1,0:T(8,128)} %get-tuple-element.22, f32[4,128]{1,0:T(4,128)S(1)} %get-tuple-element.21), kind=kOutput, calls=%fused_computation.20 | convolution fusion | flops 51774336 | bytes 2099200 | tf_op jit(solution)/shard_map/hfs,shd->fhd/dot_general | solution.py:64
  55.3 4.3 %collective-permute-done.3 = bf16[128,1024]{0,1:T(8,128)(2,1)} collective-permute-done((bf16[128,1024]{0,1:T(8,128)(2,1)}, bf16[128,1024]{0,1:T(8,128)(2,1)}, u32[]{:S(2)}, u32[]{:S(2)}) %collective-permute-start.3) | collective-permute-done | bytes 262176 | tf_op jit(solution)/shard_map/ppermute | solution.py:23
  61.7 1.9 copy.53
  65.7 33.3 %all_to_all.20 = bf16[4,128,1280]{2,1,0:T(8,128)(2,1)S(1)} all-to-all(bf16[4,128,1280]{2,1,0:T(8,128)(2,1)S(1)} %bitcast.56), channel_id=1, replica_groups=mesh['calls'=32,'cx'=8,'cy'=4] {'cy'}, dimensions={0} | all-to-all | bytes 2621440 | tf_op jit(solution)/shard_map/all_to_all | solution.py:94
  99.7 43.0 %all_to_all.21 = f32[8,64,768]{2,1,0:T(8,128)} all-to-all(f32[8,64,768]{2,1,0:T(8,128)S(1)} %bitcast.55), channel_id=1, replica_groups=mesh['calls'=32,'cx'=8,'cy'=4] {'cx'}, dimensions={0} | all-to-all | bytes 3145728 | tf_op jit(solution)/shard_map/all_to_all | solution.py:100
  142.7 2.2 %reduce_sum.38 = f32[64,768]{1,0:T(8,128)} reduce(f32[8,64,768]{2,1,0:T(8,128)} %all_to_all.21, f32[]{:T(128)} %constant.24.clone.1), dimensions={0}, to_apply=%region_3.4 | reduce | flops 344064 | bytes 1769476 | tf_op jit(solution)/shard_map/reduce_sum | solution.py:100
  144.9 2.0 reshape.184
  146.9 2.0 copy.55
  148.9 2.2 %all_to_all.16 = f32[32,1,1536]{2,1,0:T(1,128)} reshape(f32[2,16,32,48]{3,2,1,0:T(8,128)} %copy.55) | data formatting | bytes 393216 | tf_op jit(solution)/shard_map/all_to_all | solution.py:103
  151.1 23.4 %all-to-all-start.2 = ((f32[32,1,1536]{2,1,0:T(1,128)}), f32[32,1,1536]{2,1,0:T(1,128)}, u32[]{:S(2)}, u32[]{:S(2)}) async-start(f32[32,1,1536]{2,1,0:T(1,128)} %all_to_all.16), calls=%async_computation.2 | async-start | bytes 393216 | tf_op jit(solution)/shard_map/all_to_all | solution.py:103
  174.5 2.5 %fusion.11 = bf16[4,128,128]{2,1,0:T(8,128)(2,1)} fusion(bf16[48,4,8,128]{3,2,1,0:T(8,128)(2,1)} %get-tuple-element.20, f32[128]{0:T(128)S(1)} %copy-done.3, f32[4,128]{1,0:T(4,128)S(1)} %get-tuple-element.21, bf16[128,4,128]{0,2,1:T(8,128)(2,1)} %bitcast.73, bf16[384,4,128]{0,2,1:T(8,128)(2,1)} %bitcast.71, pred[128,384]{1,0:T(8,128)(4,1)} %fusion.37), kind=kOutput, calls=%fused_computation.19 | convolution fusion | flops 101778304 | bytes 1100288 | tf_op jit(solution)/shard_map/hfs,shd->fhd/dot_general | solution.py:55
  178.6 8.4 %all-to-all-done.2 = f32[32,1,1536]{2,1,0:T(1,128)} async-done(((f32[32,1,1536]{2,1,0:T(1,128)}), f32[32,1,1536]{2,1,0:T(1,128)}, u32[]{:S(2)}, u32[]{:S(2)}) %all-to-all-start.2) | async-done | bytes 196640 | tf_op jit(solution)/shard_map/all_to_all | solution.py:103
  188.8 7.0 %collective-permute-start.4 = (f32[32,48]{1,0:T(8,128)}, f32[32,48]{1,0:T(8,128)S(1)}, u32[]{:S(2)}, u32[]{:S(2)}) collective-permute-start(f32[32,48]{1,0:T(8,128)} %reshape.185), channel_id=1, source_target_pairs={{0,0},{1,16},{2,512},{3,528},{4,64},{5,80},{6,576},{7,592},{8,128}... | collective-permute-start | bytes 18440 | tf_op jit(solution)/shard_map/ppermute | solution.py:114
  197.7 7.1 %collective-permute-done.4 = f32[32,48]{1,0:T(8,128)S(1)} collective-permute-done((f32[32,48]{1,0:T(8,128)}, f32[32,48]{1,0:T(8,128)S(1)}, u32[]{:S(2)}, u32[]{:S(2)}) %collective-permute-start.4) | collective-permute-done | bytes 6176 | tf_op jit(solution)/shard_map/ppermute | solution.py:114
  (37 shorter events, 26.5 us)
Async XLA Ops:
  0.6 1.9 copy-start
  4.8 14.6 %collective-permute-start.1 = (bf16[128,1024]{1,0:T(8,128)(2,1)}, bf16[128,1024]{1,0:T(8,128)(2,1)}, u32[]{:S(2)}, u32[]{:S(2)}) collective-permute-start(bf16[128,1024]{1,0:T(8,128)(2,1)} %slice.40), channel_id=1, source_target_pairs={{1,0},{2,1},{3,2},{4,3},{5,4},{6,5},{7,6},{8,7},{9,8},{10,9},{11,1... | collective-permute-start | bytes 786440 | tf_op jit(solution)/shard_map/ppermute | solution.py:23
  10.3 12.9 %collective-permute-start = (bf16[128,1024]{1,0:T(8,128)(2,1)}, bf16[128,1024]{1,0:T(8,128)(2,1)}, u32[]{:S(2)}, u32[]{:S(2)}) collective-permute-start(bf16[128,1024]{1,0:T(8,128)(2,1)} %slice.40), channel_id=1, source_target_pairs={{0,1},{1,2},{2,3},{3,4},{4,5},{5,6},{6,7},{7,8},{8,9},{9,10},{10,1... | collective-permute-start | bytes 786440 | tf_op jit(solution)/shard_map/ppermute | solution.py:21
  26.1 4.7 %copy-start.1 = (bf16[1,128,512]{1,2,0:T(8,128)(2,1)S(1)}, bf16[1,128,512]{1,2,0:T(8,128)(2,1)}, u32[]{:S(2)}) copy-start(bf16[1,128,512]{1,2,0:T(8,128)(2,1)} %copy.60) | copy-start | bytes 393220
  26.1 4.7 %copy-start.2 = (bf16[128,512]{0,1:T(8,128)(2,1)S(1)}, bf16[128,512]{0,1:T(8,128)(2,1)}, u32[]{:S(2)}) copy-start(bf16[128,512]{0,1:T(8,128)(2,1)} %copy.61) | copy-start | bytes 393220
  40.9 14.4 %collective-permute-start.2 = (bf16[128,1024]{0,1:T(8,128)(2,1)}, bf16[128,1024]{0,1:T(8,128)(2,1)}, u32[]{:S(2)}, u32[]{:S(2)}) collective-permute-start(bf16[128,1024]{0,1:T(8,128)(2,1)} %get-tuple-element.17), channel_id=1, source_target_pairs={{0,1},{1,2},{2,3},{3,4},{4,5},{5,6},{6,7},{7,8},{8,9},{9,10},{10,1... | collective-permute-start | bytes 786440 | tf_op jit(solution)/shard_map/ppermute | solution.py:21
  45.0 14.6 %collective-permute-start.3 = (bf16[128,1024]{0,1:T(8,128)(2,1)}, bf16[128,1024]{0,1:T(8,128)(2,1)}, u32[]{:S(2)}, u32[]{:S(2)}) collective-permute-start(bf16[128,1024]{0,1:T(8,128)(2,1)} %get-tuple-element.18), channel_id=1, source_target_pairs={{1,0},{2,1},{3,2},{4,3},{5,4},{6,5},{7,6},{8,7},{9,8},{10,9},{11,1... | collective-permute-start | bytes 786440 | tf_op jit(solution)/shard_map/ppermute | solution.py:23
  144.9 29.6 %copy-start.3 = (f32[128]{0:T(128)S(1)}, f32[128]{0:T(128)}, u32[]{:S(2)}) copy-start(f32[128]{0:T(128)} %get-tuple-element.15) | copy-start | bytes 1540
  151.1 36.0 %all-to-all-start.2 = ((f32[32,1,1536]{2,1,0:T(1,128)}), f32[32,1,1536]{2,1,0:T(1,128)}, u32[]{:S(2)}, u32[]{:S(2)}) async-start(f32[32,1,1536]{2,1,0:T(1,128)} %all_to_all.16), calls=%async_computation.2 | async-start | bytes 393216 | tf_op jit(solution)/shard_map/all_to_all | solution.py:103
  188.8 15.9 %collective-permute-start.4 = (f32[32,48]{1,0:T(8,128)}, f32[32,48]{1,0:T(8,128)S(1)}, u32[]{:S(2)}, u32[]{:S(2)}) collective-permute-start(f32[32,48]{1,0:T(8,128)} %reshape.185), channel_id=1, source_target_pairs={{0,0},{1,16},{2,512},{3,528},{4,64},{5,80},{6,576},{7,592},{8,128}... | collective-permute-start | bytes 18440 | tf_op jit(solution)/shard_map/ppermute | solution.py:114

commit v8 on v7

--- a/solution.py
+++ b/solution.py
@@ -7,6 +7,7 @@
 
 HEADS = 4
 WIN = 128
+CALLS = ("ch", "cz", "cc")
 CTX = ("cx", "cy")
 
 
@@ -78,7 +79,9 @@
 def weight_gradient(frame_rows, grad_all):
     frame_count, model_width = frame_rows.shape
     grad_width = grad_all.shape[1]
-    calls = lax.axis_size("calls")
+    calls = lax.axis_size(CALLS)
+    pair = lax.axis_size("cc")
+    spread = lax.axis_size(CALLS[:2])
     ring = lax.axis_size("cx")
     group = lax.axis_size("cy")
     ctx = ring * group
@@ -92,26 +95,30 @@
     col_factor = jnp.broadcast_to(col_factor, (2, group // 2, frame_count, tile_cols))
     sent = jnp.concatenate([row_factor, col_factor], axis=3).reshape(group, frame_count, -1)
     got = lax.all_to_all(sent, "cy", 0, 0, tiled=True)
-    pair_rows = tile_rows // (ring * block_rows)
     tile = jnp.einsum(
         "sfa,sfb->ab", got[..., :tile_rows], got[..., tile_rows:], preferred_element_type=jnp.float32
     )
-    parts = tile.reshape(ring, pair_rows * block_rows, tile_cols)
+    halves = tile.reshape(pair, tile_rows // pair, tile_cols)
+    core = lax.axis_index("cc")
+    keep = lax.dynamic_index_in_dim(halves, core, 0, keepdims=False)
+    send = lax.dynamic_index_in_dim(halves, pair - 1 - core, 0, keepdims=False)
+    half = keep + lax.ppermute(send, "cc", [(0, 1), (1, 0)])
+    parts = half.reshape(ring, block_rows, tile_cols)
     part = jnp.sum(lax.all_to_all(parts, "cx", 0, 0, tiled=True), axis=0)
-    part = part.reshape(pair_rows, block_rows, -1, block_cols).transpose(0, 2, 1, 3)
-    part = part.reshape(calls, block_rows * block_cols)
-    summed = jnp.sum(lax.all_to_all(part, "calls", 0, 0, tiled=True), axis=0)
+    part = part.reshape(block_rows, spread, block_cols).transpose(1, 0, 2)
+    part = part.reshape(spread, block_rows * block_cols)
+    summed = jnp.sum(lax.all_to_all(part, CALLS[:2], 0, 0, tiled=True), axis=0)
     summed = summed.reshape(block_rows, block_cols)
-    col_pieces_per_tile = tile_cols // block_cols
     pairs = []
-    for piece in range(calls):
-        for x in range(ring):
-            for y in range(group):
-                row_block = (y // (group // 2)) * (tile_rows // block_rows)
-                row_block += x * pair_rows + piece // col_pieces_per_tile
-                col_block = (y % (group // 2)) * col_pieces_per_tile + piece % col_pieces_per_tile
-                pairs.append(((piece * ring + x) * group + y, row_block * ctx + col_block))
-    return lax.ppermute(summed, ("calls", "cx", "cy"), pairs)
+    for far in range(spread):
+        for near in range(pair):
+            for x in range(ring):
+                for y in range(group):
+                    row_block = ((y // (group // 2)) * pair + near) * ring + x
+                    col_block = (y % (group // 2)) * spread + far
+                    source = ((far * pair + near) * ring + x) * group + y
+                    pairs.append((source, row_block * ctx + col_block))
+    return lax.ppermute(summed, CALLS + CTX, pairs)
 
 
 def body(frames_in, w_qkv, out_grad, lengths):
@@ -151,9 +158,11 @@
 
 def solution(mesh):
     calls, ctx = mesh.devices.shape
+    pair = 2
     group = 4
-    fine = Mesh(mesh.devices.reshape(calls, ctx // group, group), ("calls",) + CTX)
-    frames = P("calls", CTX, None)
-    in_specs = (frames, P(), frames, P("calls"))
-    out_specs = (frames, frames, P("calls", CTX))
+    shape = (2, calls // (2 * pair), pair, ctx // group, group)
+    fine = Mesh(mesh.devices.reshape(shape), CALLS + CTX)
+    frames = P(CALLS, CTX, None)
+    in_specs = (frames, P(), frames, P(CALLS))
+    out_specs = (frames, frames, P(CALLS, CTX))
     return jax.shard_map(body, mesh=fine, in_specs=in_specs, out_specs=out_specs, check_vma=False)

time: 206 us -> 201 us (0.976)
  the two profiles are of different devices: /device:TPU:5 before, /device:TPU:6 now
where the time goes in v8:
time: 201 us; the launch traced here: 200 us
  waiting for transfers between devices  63.2 us (31%)
  starting transfers between devices  45.1 us (22%)
  blocking collectives  27.6 us (14%)
  local copies, waits for them, and re-layouts  25.3 us (13%)
  matrix products  24.8 us (12%)
  other arithmetic  12.6 us (6%)
    all_to_all x1, waiting for transfers between devices, weight_gradient(): got = lax.all_to_all(sent, 'cy', 0, 0, tiled=True)  31.8 us
    all_to_all x1, blocking collectives, weight_gradient(): part = jnp.sum(lax.all_to_all(parts, 'cx', 0, 0, tiled=True), axis=0)  27.6 us
    all_to_all x1, starting transfers between devices, weight_gradient(): summed = jnp.sum(lax.all_to_all(part, CALLS[:2], 0, 0, tiled=True), axis=0)  19.7 us
    ppermute x1, waiting for transfers between devices, weight_gradient(): return lax.ppermute(summed, CALLS + CTX, pairs)  12.5 us
    ppermute x2, starting transfers between devices, with_halo(): lax.ppermute(head, axis, [((i + 1) % count, i) for i in range(ends)])  9.97 us
    all_to_all x1, waiting for transfers between devices, weight_gradient(): summed = jnp.sum(lax.all_to_all(part, CALLS[:2], 0, 0, tiled=True), axis=0)  8.32 us
    ppermute x2, starting transfers between devices, with_halo(): lax.ppermute(tail, axis, [(i, (i + 1) % count) for i in range(ends)])  6.3 us
    dot_general x1, matrix products, attend(): jnp.einsum('hfs,fhd->shd', grad_scores, query_heads, preferred_element_ty...  5.35 us
  transfers between devices with their start and end apart: 8, of which 6 were waited for; matrix products, arithmetic and copies ran while one was open for 9% of the time, Pallas kernels for 0%

profile of v8, /device:TPU:6, one launch (start us, length us, event | category | flops | bytes accessed | tf_op | source)
XLA Modules:
  0.0 200.0 jit_solution(10686554635263986738)
XLA Ops:
  0.6 1.9 copy-done
  4.8 5.8 %collective-permute-start.1 = (bf16[128,1024]{1,0:T(8,128)(2,1)}, bf16[128,1024]{1,0:T(8,128)(2,1)}, u32[]{:S(2)}, u32[]{:S(2)}) collective-permute-start(bf16[128,1024]{1,0:T(8,128)(2,1)} %slice.40), channel_id=1, source_target_pairs={{1,0},{2,1},{3,2},{4,3},{5,4},{6,5},{7,6},{8,7},{9,8},{10,9},{11,1... | collective-permute-start | bytes 786440 | tf_op jit(solution)/shard_map/ppermute | solution.py:24
  10.6 1.9 collective-permute-start
  19.7 4.4 %collective-permute-done = bf16[128,1024]{1,0:T(8,128)(2,1)} collective-permute-done((bf16[128,1024]{1,0:T(8,128)(2,1)}, bf16[128,1024]{1,0:T(8,128)(2,1)}, u32[]{:S(2)}, u32[]{:S(2)}) %collective-permute-start) | collective-permute-done | bytes 262176 | tf_op jit(solution)/shard_map/ppermute | solution.py:22
  26.9 2.3 %fusion.25 = f32[4,128,384]{2,1,0:T(8,128)} fusion(bf16[48,4,8,128]{3,2,1,0:T(8,128)(2,1)} %get-tuple-element.20, bf16[128,4,128]{0,2,1:T(8,128)(2,1)} %bitcast.69, pred[128]{0:T(512)(128)(4,1)S(1)} %get-tuple-element.16), kind=kOutput, calls=%fused_computation.36 | convolution fusion | flops 50397184 | bytes 1310848 | tf_op jit(solution)/shard_map/fhd,shd->hfs/dot_general | solution.py:60
  29.3 2.3 %fusion.54 = (f32[4,128]{1,0:T(4,128)S(1)}, f32[4,128,384]{2,1,0:T(8,128)}) fusion(bf16[128,4,128]{0,2,1:T(8,128)(2,1)} %bitcast.77, bf16[384,4,128]{0,2,1:T(8,128)(2,1)} %bitcast.73, pred[128,384]{1,0:T(8,128)(4,1)} %fusion.37), kind=kOutput, calls=%fused_computation.73 | convolution fusion | flops 51118464 | bytes 1361920 | tf_op jit(solution)/shard_map/sub | solution.py:52
  31.6 2.5 %fusion.32 = f32[4,128,384]{2,1,0:T(8,128)} fusion(bf16[128,4,128]{0,2,1:T(8,128)(2,1)S(1)} %bitcast.70, pred[128]{0:T(512)(128)(4,1)S(1)} %get-tuple-element.16, f32[4,128]{1,0:T(4,128)S(1)} %get-tuple-element.21, bf16[128,4,128]{0,2,1:T(8,128)(2,1)S(1)} %bitcast.79, bf16[384,4,128]{0,2,1:T(8,128)(2,1)} %bitcast.74, pred[128,384]{1,0:T(8,128)(4,1)} %fusion.37), kind=kOutput, calls=%fused_computation.46 | convolution fusion | flops 101712768 | bytes 1493120 | tf_op jit(solution)/shard_map/hfs,fhd->shd/dot_general | solution.py:71
  34.1 5.4 %fusion.12 = f32[4,128,384]{2,1,0:T(8,128)} fusion(bf16[128,4,128]{0,2,1:T(8,128)(2,1)S(1)} %bitcast.80, f32[4,128,384]{2,1,0:T(8,128)} %fusion.25, f32[4,128,384]{2,1,0:T(8,128)} %get-tuple-element.22, f32[4,128]{1,0:T(4,128)S(1)} %get-tuple-element.21), kind=kOutput, calls=%fused_computation.21 | convolution fusion | flops 51708800 | bytes 2492416 | tf_op jit(solution)/shard_map/hfs,fhd->shd/dot_general | solution.py:68
  41.7 4.4 %collective-permute-start.2 = (bf16[128,1024]{0,1:T(8,128)(2,1)}, bf16[128,1024]{0,1:T(8,128)(2,1)}, u32[]{:S(2)}, u32[]{:S(2)}) collective-permute-start(bf16[128,1024]{0,1:T(8,128)(2,1)} %get-tuple-element.17), channel_id=1, source_target_pairs={{0,1},{1,2},{2,3},{3,4},{4,5},{5,6},{6,7},{7,8},{8,9},{9,10},{10,1... | collective-permute-start | bytes 786440 | tf_op jit(solution)/shard_map/ppermute | solution.py:22
  46.1 4.2 %collective-permute-start.3 = (bf16[128,1024]{0,1:T(8,128)(2,1)}, bf16[128,1024]{0,1:T(8,128)(2,1)}, u32[]{:S(2)}, u32[]{:S(2)}) collective-permute-start(bf16[128,1024]{0,1:T(8,128)(2,1)} %get-tuple-element.18), channel_id=1, source_target_pairs={{1,0},{2,1},{3,2},{4,3},{5,4},{6,5},{7,6},{8,7},{9,8},{10,9},{11,1... | collective-permute-start | bytes 786440 | tf_op jit(solution)/shard_map/ppermute | solution.py:24
  52.2 4.5 %convolution_convert_fusion.2 = bf16[4,128,128]{2,1,0:T(8,128)(2,1)S(1)} fusion(bf16[384,4,128]{0,2,1:T(8,128)(2,1)} %bitcast.75, f32[4,128,384]{2,1,0:T(8,128)} %fusion.25, f32[4,128,384]{2,1,0:T(8,128)} %get-tuple-element.22, f32[4,128]{1,0:T(4,128)S(1)} %get-tuple-element.21), kind=kOutput, calls=%fused_computation.20 | convolution fusion | flops 51774336 | bytes 2099200 | tf_op jit(solution)/shard_map/hfs,shd->fhd/dot_general | solution.py:65
  56.7 3.6 %collective-permute-done.3 = bf16[128,1024]{0,1:T(8,128)(2,1)} collective-permute-done((bf16[128,1024]{0,1:T(8,128)(2,1)}, bf16[128,1024]{0,1:T(8,128)(2,1)}, u32[]{:S(2)}, u32[]{:S(2)}) %collective-permute-start.3) | collective-permute-done | bytes 262176 | tf_op jit(solution)/shard_map/ppermute | solution.py:24
  62.3 1.9 copy.53
  67.4 4.3 %all-to-all-start = ((bf16[4,128,1280]{2,1,0:T(8,128)(2,1)}), bf16[4,128,1280]{2,1,0:T(8,128)(2,1)}, u32[]{:S(2)}, u32[]{:S(2)}) async-start(bf16[4,128,1280]{2,1,0:T(8,128)(2,1)} %bitcast.60), calls=%async_computation | async-start | bytes 2621440 | tf_op jit(solution)/shard_map/all_to_all | solution.py:97
  71.7 31.8 %all-to-all-done = bf16[4,128,1280]{2,1,0:T(8,128)(2,1)} async-done(((bf16[4,128,1280]{2,1,0:T(8,128)(2,1)}), bf16[4,128,1280]{2,1,0:T(8,128)(2,1)}, u32[]{:S(2)}, u32[]{:S(2)}) %all-to-all-start) | async-done | bytes 1310752 | tf_op jit(solution)/shard_map/all_to_all | solution.py:97
  103.6 1.9 fusion.17
  107.6 1.9 collective-permute-start.4
  109.5 2.6 %collective-permute-done.4 = f32[256,768]{1,0:T(8,128)} collective-permute-done((f32[256,768]{1,0:T(8,128)}, f32[256,768]{1,0:T(8,128)}, u32[]{:S(2)}, u32[]{:S(2)}) %collective-permute-start.4) | collective-permute-done | bytes 786464 | tf_op jit(solution)/shard_map/ppermute | solution.py:105
  113.5 27.6 %all_to_all.20 = f32[8,32,768]{2,1,0:T(8,128)} all-to-all(f32[8,32,768]{2,1,0:T(8,128)S(1)} %bitcast.61), channel_id=1, replica_groups=mesh['ch'=2,'cz'=8,'cc'=2,'cx'=8,'cy'=4] {'cx'}, dimensions={0} | all-to-all | bytes 1572864 | tf_op jit(solution)/shard_map/all_to_all | solution.py:107
  148.2 19.7 %all-to-all-start.2 = ((f32[16,1,1536]{2,1,0:T(1,128)}), f32[16,1,1536]{2,1,0:T(1,128)}, u32[]{:S(2)}, u32[]{:S(2)}) async-start(f32[16,1,1536]{2,1,0:T(1,128)} %all_to_all.16), calls=%async_computation.2 | async-start | bytes 196608 | tf_op jit(solution)/shard_map/all_to_all | solution.py:110
  168.0 2.5 %fusion.11 = bf16[4,128,128]{2,1,0:T(8,128)(2,1)} fusion(bf16[48,4,8,128]{3,2,1,0:T(8,128)(2,1)} %get-tuple-element.20, f32[128]{0:T(128)S(1)} %copy-done.4, f32[4,128]{1,0:T(4,128)S(1)} %get-tuple-element.21, bf16[128,4,128]{0,2,1:T(8,128)(2,1)} %bitcast.78, bf16[384,4,128]{0,2,1:T(8,128)(2,1)} %bitcast.76, pred[128,384]{1,0:T(8,128)(4,1)} %fusion.37), kind=kOutput, calls=%fused_computation.19 | convolution fusion | flops 101778304 | bytes 1100288 | tf_op jit(solution)/shard_map/hfs,shd->fhd/dot_general | solution.py:56
  172.2 8.3 %all-to-all-done.2 = f32[16,1,1536]{2,1,0:T(1,128)} async-done(((f32[16,1,1536]{2,1,0:T(1,128)}), f32[16,1,1536]{2,1,0:T(1,128)}, u32[]{:S(2)}, u32[]{:S(2)}) %all-to-all-start.2) | async-done | bytes 98336 | tf_op jit(solution)/shard_map/all_to_all | solution.py:110
  182.1 2.9 %collective-permute-start.5 = (f32[32,48]{1,0:T(8,128)}, f32[32,48]{1,0:T(8,128)S(1)}, u32[]{:S(2)}, u32[]{:S(2)}) collective-permute-start(f32[32,48]{1,0:T(8,128)} %reshape.189), channel_id=1, source_target_pairs={{0,0},{1,16},{2,512},{3,528},{4,32},{5,48},{6,544},{7,560},{8,64},... | collective-permute-start | bytes 18440 | tf_op jit(solution)/shard_map/ppermute | solution.py:121
  186.9 12.5 %collective-permute-done.5 = f32[32,48]{1,0:T(8,128)S(1)} collective-permute-done((f32[32,48]{1,0:T(8,128)}, f32[32,48]{1,0:T(8,128)S(1)}, u32[]{:S(2)}, u32[]{:S(2)}) %collective-permute-start.5) | collective-permute-done | bytes 6176 | tf_op jit(solution)/shard_map/ppermute | solution.py:121
  (44 shorter events, 37.5 us)
Async XLA Ops:
  0.6 1.9 copy-start
  4.8 14.9 %collective-permute-start.1 = (bf16[128,1024]{1,0:T(8,128)(2,1)}, bf16[128,1024]{1,0:T(8,128)(2,1)}, u32[]{:S(2)}, u32[]{:S(2)}) collective-permute-start(bf16[128,1024]{1,0:T(8,128)(2,1)} %slice.40), channel_id=1, source_target_pairs={{1,0},{2,1},{3,2},{4,3},{5,4},{6,5},{7,6},{8,7},{9,8},{10,9},{11,1... | collective-permute-start | bytes 786440 | tf_op jit(solution)/shard_map/ppermute | solution.py:24
  10.6 13.4 %collective-permute-start = (bf16[128,1024]{1,0:T(8,128)(2,1)}, bf16[128,1024]{1,0:T(8,128)(2,1)}, u32[]{:S(2)}, u32[]{:S(2)}) collective-permute-start(bf16[128,1024]{1,0:T(8,128)(2,1)} %slice.40), channel_id=1, source_target_pairs={{0,1},{1,2},{2,3},{3,4},{4,5},{5,6},{6,7},{7,8},{8,9},{9,10},{10,1... | collective-permute-start | bytes 786440 | tf_op jit(solution)/shard_map/ppermute | solution.py:22
  26.9 4.7 %copy-start.2 = (bf16[1,128,512]{1,2,0:T(8,128)(2,1)S(1)}, bf16[1,128,512]{1,2,0:T(8,128)(2,1)}, u32[]{:S(2)}) copy-start(bf16[1,128,512]{1,2,0:T(8,128)(2,1)} %copy.60) | copy-start | bytes 393220
  26.9 4.7 %copy-start.3 = (bf16[128,512]{0,1:T(8,128)(2,1)S(1)}, bf16[128,512]{0,1:T(8,128)(2,1)}, u32[]{:S(2)}) copy-start(bf16[128,512]{0,1:T(8,128)(2,1)} %copy.61) | copy-start | bytes 393220
  41.7 15.0 %collective-permute-start.2 = (bf16[128,1024]{0,1:T(8,128)(2,1)}, bf16[128,1024]{0,1:T(8,128)(2,1)}, u32[]{:S(2)}, u32[]{:S(2)}) collective-permute-start(bf16[128,1024]{0,1:T(8,128)(2,1)} %get-tuple-element.17), channel_id=1, source_target_pairs={{0,1},{1,2},{2,3},{3,4},{4,5},{5,6},{6,7},{7,8},{8,9},{9,10},{10,1... | collective-permute-start | bytes 786440 | tf_op jit(solution)/shard_map/ppermute | solution.py:22
  46.1 14.2 %collective-permute-start.3 = (bf16[128,1024]{0,1:T(8,128)(2,1)}, bf16[128,1024]{0,1:T(8,128)(2,1)}, u32[]{:S(2)}, u32[]{:S(2)}) collective-permute-start(bf16[128,1024]{0,1:T(8,128)(2,1)} %get-tuple-element.18), channel_id=1, source_target_pairs={{1,0},{2,1},{3,2},{4,3},{5,4},{6,5},{7,6},{8,7},{9,8},{10,9},{11,1... | collective-permute-start | bytes 786440 | tf_op jit(solution)/shard_map/ppermute | solution.py:24
  67.4 36.1 %all-to-all-start = ((bf16[4,128,1280]{2,1,0:T(8,128)(2,1)}), bf16[4,128,1280]{2,1,0:T(8,128)(2,1)}, u32[]{:S(2)}, u32[]{:S(2)}) async-start(bf16[4,128,1280]{2,1,0:T(8,128)(2,1)} %bitcast.60), calls=%async_computation | async-start | bytes 2621440 | tf_op jit(solution)/shard_map/all_to_all | solution.py:97
  105.5 1.2 copy-start.1
  107.6 4.5 %collective-permute-start.4 = (f32[256,768]{1,0:T(8,128)}, f32[256,768]{1,0:T(8,128)}, u32[]{:S(2)}, u32[]{:S(2)}) collective-permute-start(f32[256,768]{1,0:T(8,128)} %dynamic-slice_bitcast_fusion), channel_id=1, source_target_pairs={{0,32},{32,0},{1,33},{33,1},{2,34},{34,2},{3,35},{35,3},{4,36},{36... | collective-permute-start | bytes 2359304 | tf_op jit(solution)/shard_map/ppermute | solution.py:105
  113.5 54.5 %copy-start.4 = (f32[128]{0:T(128)S(1)}, f32[128]{0:T(128)}, u32[]{:S(2)}) copy-start(f32[128]{0:T(128)} %get-tuple-element.15) | copy-start | bytes 1540
  148.2 32.3 %all-to-all-start.2 = ((f32[16,1,1536]{2,1,0:T(1,128)}), f32[16,1,1536]{2,1,0:T(1,128)}, u32[]{:S(2)}, u32[]{:S(2)}) async-start(f32[16,1,1536]{2,1,0:T(1,128)} %all_to_all.16), calls=%async_computation.2 | async-start | bytes 196608 | tf_op jit(solution)/shard_map/all_to_all | solution.py:110
  182.1 17.2 %collective-permute-start.5 = (f32[32,48]{1,0:T(8,128)}, f32[32,48]{1,0:T(8,128)S(1)}, u32[]{:S(2)}, u32[]{:S(2)}) collective-permute-start(f32[32,48]{1,0:T(8,128)} %reshape.189), channel_id=1, source_target_pairs={{0,0},{1,16},{2,512},{3,528},{4,32},{5,48},{6,544},{7,560},{8,64},... | collective-permute-start | bytes 18440 | tf_op jit(solution)/shard_map/ppermute | solution.py:121

commit v9 on v8

--- a/solution.py
+++ b/solution.py
@@ -87,38 +87,23 @@
     ctx = ring * group
     block_rows = model_width // calls
     block_cols = grad_width // ctx
-    tile_rows = model_width // 2
-    tile_cols = grad_width // (group // 2)
-    row_factor = frame_rows.reshape(frame_count, 2, 1, tile_rows).transpose(1, 2, 0, 3)
-    col_factor = grad_all.reshape(frame_count, 1, group // 2, tile_cols).transpose(1, 2, 0, 3)
-    row_factor = jnp.broadcast_to(row_factor, (2, group // 2, frame_count, tile_rows))
-    col_factor = jnp.broadcast_to(col_factor, (2, group // 2, frame_count, tile_cols))
-    sent = jnp.concatenate([row_factor, col_factor], axis=3).reshape(group, frame_count, -1)
+    col_factor = grad_all.reshape(frame_count, ring, group, block_cols).transpose(2, 0, 1, 3)
+    col_factor = col_factor.reshape(group, frame_count, ring * block_cols)
+    row_factor = jnp.broadcast_to(frame_rows[None], (group, frame_count, model_width))
+    sent = jnp.concatenate([row_factor, col_factor], axis=2)
     got = lax.all_to_all(sent, "cy", 0, 0, tiled=True)
+    row_pieces = got[..., :model_width].reshape(group, frame_count, spread, pair, block_rows)
+    col_pieces = got[..., model_width:].reshape(group, frame_count, ring, block_cols)
     tile = jnp.einsum(
-        "sfa,sfb->ab", got[..., :tile_rows], got[..., tile_rows:], preferred_element_type=jnp.float32
-    )
-    halves = tile.reshape(pair, tile_rows // pair, tile_cols)
+        "sfnha,sfxb->hxnab", row_pieces, col_pieces, preferred_element_type=jnp.float32
+    ).reshape(pair, ring, spread, block_rows * block_cols)
     core = lax.axis_index("cc")
-    keep = lax.dynamic_index_in_dim(halves, core, 0, keepdims=False)
-    send = lax.dynamic_index_in_dim(halves, pair - 1 - core, 0, keepdims=False)
+    keep = lax.dynamic_index_in_dim(tile, core, 0, keepdims=False)
+    send = lax.dynamic_index_in_dim(tile, pair - 1 - core, 0, keepdims=False)
     half = keep + lax.ppermute(send, "cc", [(0, 1), (1, 0)])
-    parts = half.reshape(ring, block_rows, tile_cols)
-    part = jnp.sum(lax.all_to_all(parts, "cx", 0, 0, tiled=True), axis=0)
-    part = part.reshape(block_rows, spread, block_cols).transpose(1, 0, 2)
-    part = part.reshape(spread, block_rows * block_cols)
+    part = jnp.sum(lax.all_to_all(half, "cx", 0, 0, tiled=True), axis=0)
     summed = jnp.sum(lax.all_to_all(part, CALLS[:2], 0, 0, tiled=True), axis=0)
-    summed = summed.reshape(block_rows, block_cols)
-    pairs = []
-    for far in range(spread):
-        for near in range(pair):
-            for x in range(ring):
-                for y in range(group):
-                    row_block = ((y // (group // 2)) * pair + near) * ring + x
-                    col_block = (y % (group // 2)) * spread + far
-                    source = ((far * pair + near) * ring + x) * group + y
-                    pairs.append((source, row_block * ctx + col_block))
-    return lax.ppermute(summed, CALLS + CTX, pairs)
+    return summed.reshape(block_rows, block_cols)
 
 
 def body(frames_in, w_qkv, out_grad, lengths):

time: 201 us -> 190 us (0.945)
  the two profiles are of different devices: /device:TPU:6 before, /device:TPU:1 now
where the time goes in v9:
time: 190 us; the launch traced here: 189 us
  waiting for transfers between devices  66 us (35%)
  starting transfers between devices  57.6 us (30%)
  local copies, waits for them, and re-layouts  26.1 us (14%)
  matrix products  26.1 us (14%)
  other arithmetic  11.5 us (6%)
    all_to_all x1, waiting for transfers between devices, weight_gradient(): got = lax.all_to_all(sent, 'cy', 0, 0, tiled=True)  33.8 us
    all_to_all x1, starting transfers between devices, weight_gradient(): summed = jnp.sum(lax.all_to_all(part, CALLS[:2], 0, 0, tiled=True), axis=0)  20.2 us
    all_to_all x1, waiting for transfers between devices, weight_gradient(): part = jnp.sum(lax.all_to_all(half, 'cx', 0, 0, tiled=True), axis=0)  19.5 us
    all_to_all x1, starting transfers between devices, weight_gradient(): got = lax.all_to_all(sent, 'cy', 0, 0, tiled=True)  12.8 us
    ppermute x2, starting transfers between devices, with_halo(): lax.ppermute(tail, axis, [(i, (i + 1) % count) for i in range(ends)])  10.6 us
    all_to_all x1, waiting for transfers between devices, weight_gradient(): summed = jnp.sum(lax.all_to_all(part, CALLS[:2], 0, 0, tiled=True), axis=0)  9.5 us
    all_to_all x1, starting transfers between devices, weight_gradient(): part = jnp.sum(lax.all_to_all(half, 'cx', 0, 0, tiled=True), axis=0)  7.97 us
    reshape x1, local copies, waits for them, and re-layouts, weight_gradient(): tile = jnp.einsum('sfnha,sfxb->hxnab', row_pieces, col_pieces, preferred_...  6.09 us
  transfers between devices with their start and end apart: 8, of which 5 were waited for; matrix products, arithmetic and copies ran while one was open for 9% of the time, Pallas kernels for 0%

profile of v9, /device:TPU:1, one launch (start us, length us, event | category | flops | bytes accessed | tf_op | source)
XLA Modules:
  0.0 188.9 jit_solution(3856201314865099324)
XLA Ops:
  0.6 1.9 copy-done
  6.1 5.5 %collective-permute-start = (bf16[128,1024]{1,0:T(8,128)(2,1)}, bf16[128,1024]{1,0:T(8,128)(2,1)}, u32[]{:S(2)}, u32[]{:S(2)}) collective-permute-start(bf16[128,1024]{1,0:T(8,128)(2,1)} %slice.40), channel_id=1, source_target_pairs={{0,1},{1,2},{2,3},{3,4},{4,5},{5,6},{6,7},{7,8},{8,9},{9,10},{10,1... | collective-permute-start | bytes 786440 | tf_op jit(solution)/shard_map/ppermute | solution.py:22
  15.7 1.7 copy.57
  23.0 2.4 %fusion.54 = (f32[4,128]{1,0:T(4,128)S(1)}, f32[4,128,384]{2,1,0:T(8,128)}) fusion(bf16[128,4,128]{0,2,1:T(8,128)(2,1)} %bitcast.83, bf16[384,4,128]{0,2,1:T(8,128)(2,1)} %bitcast.78, pred[128,384]{1,0:T(8,128)(4,1)} %fusion.36), kind=kOutput, calls=%fused_computation.76 | convolution fusion | flops 51118464 | bytes 1361920 | tf_op jit(solution)/shard_map/sub | solution.py:52
  25.4 2.1 %fusion.24 = f32[4,128,384]{2,1,0:T(8,128)} fusion(bf16[48,4,8,128]{3,2,1,0:T(8,128)(2,1)S(1)} %copy-done.1, bf16[128,4,128]{0,2,1:T(8,128)(2,1)} %bitcast.74, pred[128]{0:T(512)(128)(4,1)S(1)} %get-tuple-element.16), kind=kOutput, calls=%fused_computation.36 | convolution fusion | flops 50397184 | bytes 1310848 | tf_op jit(solution)/shard_map/fhd,shd->hfs/dot_general | solution.py:60
  27.6 2.7 %fusion.31 = f32[4,128,384]{2,1,0:T(8,128)} fusion(bf16[128,4,128]{0,2,1:T(8,128)(2,1)} %bitcast.75, pred[128]{0:T(512)(128)(4,1)S(1)} %get-tuple-element.16, f32[4,128]{1,0:T(4,128)S(1)} %get-tuple-element.23, bf16[128,4,128]{0,2,1:T(8,128)(2,1)} %bitcast.84, bf16[384,4,128]{0,2,1:T(8,128)(2,1)} %bitcast.79, pred[128,384]{1,0:T(8,128)(4,1)} %fusion.36), kind=kOutput, calls=%fused_computation.46 | convolution fusion | flops 101712768 | bytes 1493120 | tf_op jit(solution)/shard_map/hfs,fhd->shd/dot_general | solution.py:71
  30.2 5.3 %fusion.14 = f32[4,128,384]{2,1,0:T(8,128)} fusion(bf16[128,4,128]{0,2,1:T(8,128)(2,1)S(1)} %bitcast.86, f32[4,128,384]{2,1,0:T(8,128)} %fusion.24, f32[4,128,384]{2,1,0:T(8,128)} %get-tuple-element.24, f32[4,128]{1,0:T(4,128)S(1)} %get-tuple-element.23), kind=kOutput, calls=%fused_computation.24 | convolution fusion | flops 51708800 | bytes 2492416 | tf_op jit(solution)/shard_map/hfs,fhd->shd/dot_general | solution.py:68
  39.2 5.2 %collective-permute-start.2 = (bf16[128,1024]{0,1:T(8,128)(2,1)}, bf16[128,1024]{0,1:T(8,128)(2,1)}, u32[]{:S(2)}, u32[]{:S(2)}) collective-permute-start(bf16[128,1024]{0,1:T(8,128)(2,1)} %get-tuple-element.19), channel_id=1, source_target_pairs={{0,1},{1,2},{2,3},{3,4},{4,5},{5,6},{6,7},{7,8},{8,9},{9,10},{10,1... | collective-permute-start | bytes 786440 | tf_op jit(solution)/shard_map/ppermute | solution.py:22
  45.2 4.5 %convolution_convert_fusion.2 = bf16[4,128,128]{2,1,0:T(8,128)(2,1)S(1)} fusion(bf16[384,4,128]{0,2,1:T(8,128)(2,1)} %bitcast.80, f32[4,128,384]{2,1,0:T(8,128)} %fusion.24, f32[4,128,384]{2,1,0:T(8,128)} %get-tuple-element.24, f32[4,128]{1,0:T(4,128)S(1)} %get-tuple-element.23), kind=kOutput, calls=%fused_computation.21 | convolution fusion | flops 51774336 | bytes 2099200 | tf_op jit(solution)/shard_map/hfs,shd->fhd/dot_general | solution.py:65
  52.5 12.8 %all-to-all-start = ((bf16[4,128,1408]{1,2,0:T(8,128)(2,1)}), bf16[4,128,1408]{1,2,0:T(8,128)(2,1)}, u32[]{:S(2)}, u32[]{:S(2)}) async-start(bf16[4,128,1408]{1,2,0:T(8,128)(2,1)} %pad_maximum_fusion.1), calls=%async_computation | async-start | bytes 2883584 | tf_op jit(solution)/shard_map/all_to_all | solution.py:94
  65.3 33.8 %all-to-all-done = bf16[4,128,1408]{1,2,0:T(8,128)(2,1)} async-done(((bf16[4,128,1408]{1,2,0:T(8,128)(2,1)}), bf16[4,128,1408]{1,2,0:T(8,128)(2,1)}, u32[]{:S(2)}, u32[]{:S(2)}) %all-to-all-start) | async-done | bytes 1441824 | tf_op jit(solution)/shard_map/all_to_all | solution.py:94
  101.4 3.2 %convolution_bitcast_fusion = f32[2,8,16,32,48]{4,3,0,2,1:T(8,128)} fusion(bf16[4,128,16,2,32]{1,4,3,2,0:T(8,128)(2,1)S(1)} %bitcast.71, bf16[4,128,8,48,1,1]{1,3,2,0,5,4:T(8,128)(2,1)S(1)} %bitcast.82), kind=kOutput, calls=%fused_computation.3 | convolution fusion | flops 402653184 | bytes 3014656 | tf_op jit(solution)/shard_map/sfnha,sfxb->hxnab/dot_general | solution.py:97
  104.6 6.1 %reshape.186 = f32[2,8,16,1536]{3,0,2,1:T(2,128)} reshape(f32[2,8,16,32,48]{4,3,0,2,1:T(8,128)} %convolution_bitcast_fusion) | data formatting | bytes 3145728 | tf_op jit(solution)/shard_map/reshape | solution.py:99
  110.7 3.5 %constant_dynamic-slice_fusion.1 = (f32[1,8,16,1536]{3,0,2,1:T(1,128)S(1)}, f32[1,8,16,1536]{3,0,2,1:T(1,128)S(1)}) fusion(f32[2,8,16,1536]{3,0,2,1:T(2,128)} %reshape.186, s32[]{:T(128)S(6)} %select_n.18, s32[]{:T(128)S(6)} %select_n.19), kind=kLoop, calls=%fused_computation.60 | loop fusion | bytes 3145736 | tf_op jit(solution)/shard_map/jit(dynamic_index_in_dim)/dynamic_slice | solution.py:101
  114.3 3.4 %collective-permute-start.4 = (f32[8,16,1536]{2,1,0:T(8,128)S(1)}, f32[8,16,1536]{2,1,0:T(8,128)S(1)}, u32[]{:S(2)}, u32[]{:S(2)}) collective-permute-start(f32[8,16,1536]{2,1,0:T(8,128)S(1)} %bitcast.73), channel_id=1, source_target_pairs={{0,32},{32,0},{1,33},{33,1},{2,34},{34,2},{3,35},{35,3},{4,36},{36... | collective-permute-start | bytes 2359304 | tf_op jit(solution)/shard_map/ppermute | solution.py:103
  117.7 1.9 %collective-permute-done.4 = f32[8,16,1536]{2,1,0:T(8,128)S(1)} collective-permute-done((f32[8,16,1536]{2,1,0:T(8,128)S(1)}, f32[8,16,1536]{2,1,0:T(8,128)S(1)}, u32[]{:S(2)}, u32[]{:S(2)}) %collective-permute-start.4) | collective-permute-done | bytes 786464 | tf_op jit(solution)/shard_map/ppermute | solution.py:103
  120.6 8.0 %all-to-all-start.1 = ((f32[8,16,1536]{2,1,0:T(8,128)}), f32[8,16,1536]{2,1,0:T(8,128)}, u32[]{:S(2)}, u32[]{:S(2)}) async-start(f32[8,16,1536]{2,1,0:T(8,128)} %bitcast_add_fusion), calls=%async_computation.1 | async-start | bytes 1572864 | tf_op jit(solution)/shard_map/all_to_all | solution.py:104
  128.5 2.5 %fusion.11 = bf16[4,128,128]{2,1,0:T(8,128)(2,1)} fusion(bf16[48,4,8,128]{3,2,1,0:T(8,128)(2,1)} %get-tuple-element.22, f32[128]{0:T(128)S(1)} %copy-done.5, f32[4,128]{1,0:T(4,128)S(1)} %get-tuple-element.23, bf16[128,4,128]{0,2,1:T(8,128)(2,1)} %bitcast.85, bf16[384,4,128]{0,2,1:T(8,128)(2,1)} %bitcast.81, pred[128,384]{1,0:T(8,128)(4,1)} %fusion.36), kind=kOutput, calls=%fused_computation.20 | convolution fusion | flops 101778304 | bytes 1100288 | tf_op jit(solution)/shard_map/hfs,shd->fhd/dot_general | solution.py:56
  131.1 1.7 copy.53
  132.7 19.5 %all-to-all-done.1 = f32[8,16,1536]{2,1,0:T(8,128)} async-done(((f32[8,16,1536]{2,1,0:T(8,128)}), f32[8,16,1536]{2,1,0:T(8,128)}, u32[]{:S(2)}, u32[]{:S(2)}) %all-to-all-start.1) | async-done | bytes 786464 | tf_op jit(solution)/shard_map/all_to_all | solution.py:104
  152.2 1.8 reduce_sum.38
  155.6 20.2 %all-to-all-start.2 = ((f32[16,1,1536]{2,1,0:T(1,128)}), f32[16,1,1536]{2,1,0:T(1,128)}, u32[]{:S(2)}, u32[]{:S(2)}) async-start(f32[16,1,1536]{2,1,0:T(1,128)} %all_to_all.14), calls=%async_computation.2 | async-start | bytes 196608 | tf_op jit(solution)/shard_map/all_to_all | solution.py:105
  175.9 1.9 fusion.10
  177.7 9.5 %all-to-all-done.2 = f32[16,1,1536]{2,1,0:T(1,128)} async-done(((f32[16,1,1536]{2,1,0:T(1,128)}), f32[16,1,1536]{2,1,0:T(1,128)}, u32[]{:S(2)}, u32[]{:S(2)}) %all-to-all-start.2) | async-done | bytes 98336 | tf_op jit(solution)/shard_map/all_to_all | solution.py:105
  (44 shorter events, 26.5 us)
Async XLA Ops:
  0.6 1.9 %copy-start = (bf16[1024,1536]{1,0:T(8,128)(2,1)S(1)}, bf16[1024,1536]{1,0:T(8,128)(2,1)}, u32[]{:S(2)}) copy-start(bf16[1024,1536]{1,0:T(8,128)(2,1)} %param.5) | copy-start | bytes 9437188
  4.8 14.0 %collective-permute-start.1 = (bf16[128,1024]{1,0:T(8,128)(2,1)}, bf16[128,1024]{1,0:T(8,128)(2,1)}, u32[]{:S(2)}, u32[]{:S(2)}) collective-permute-start(bf16[128,1024]{1,0:T(8,128)(2,1)} %slice.40), channel_id=1, source_target_pairs={{1,0},{2,1},{3,2},{4,3},{5,4},{6,5},{7,6},{8,7},{9,8},{10,9},{11,1... | collective-permute-start | bytes 786440 | tf_op jit(solution)/shard_map/ppermute | solution.py:24
  6.1 14.1 %collective-permute-start = (bf16[128,1024]{1,0:T(8,128)(2,1)}, bf16[128,1024]{1,0:T(8,128)(2,1)}, u32[]{:S(2)}, u32[]{:S(2)}) collective-permute-start(bf16[128,1024]{1,0:T(8,128)(2,1)} %slice.40), channel_id=1, source_target_pairs={{0,1},{1,2},{2,3},{3,4},{4,5},{5,6},{6,7},{7,8},{8,9},{9,10},{10,1... | collective-permute-start | bytes 786440 | tf_op jit(solution)/shard_map/ppermute | solution.py:22
  23.0 2.4 %copy-start.1 = (bf16[48,4,8,128]{3,2,1,0:T(8,128)(2,1)S(1)}, bf16[48,4,8,128]{3,2,1,0:T(8,128)(2,1)}, u32[]{:S(2)}) copy-start(bf16[48,4,8,128]{3,2,1,0:T(8,128)(2,1)} %get-tuple-element.22) | copy-start | bytes 1179652
  27.6 2.7 %copy-start.4 = (bf16[128,512]{0,1:T(8,128)(2,1)S(1)}, bf16[128,512]{0,1:T(8,128)(2,1)}, u32[]{:S(2)}) copy-start(bf16[128,512]{0,1:T(8,128)(2,1)} %copy.62) | copy-start | bytes 393220
  35.5 8.8 %copy-start.3 = (bf16[1,128,1024]{2,1,0:T(8,128)(2,1)S(1)}, bf16[1,128,1024]{2,1,0:T(8,128)(2,1)}, u32[]{:S(2)}) copy-start(bf16[1,128,1024]{2,1,0:T(8,128)(2,1)} %param.4) | copy-start | bytes 786436
  37.9 11.8 %collective-permute-start.3 = (bf16[128,1024]{0,1:T(8,128)(2,1)}, bf16[128,1024]{0,1:T(8,128)(2,1)}, u32[]{:S(2)}, u32[]{:S(2)}) collective-permute-start(bf16[128,1024]{0,1:T(8,128)(2,1)} %get-tuple-element.20), channel_id=1, source_target_pairs={{1,0},{2,1},{3,2},{4,3},{5,4},{6,5},{7,6},{8,7},{9,8},{10,9},{11,1... | collective-permute-start | bytes 786440 | tf_op jit(solution)/shard_map/ppermute | solution.py:24
  39.2 10.6 %collective-permute-start.2 = (bf16[128,1024]{0,1:T(8,128)(2,1)}, bf16[128,1024]{0,1:T(8,128)(2,1)}, u32[]{:S(2)}, u32[]{:S(2)}) collective-permute-start(bf16[128,1024]{0,1:T(8,128)(2,1)} %get-tuple-element.19), channel_id=1, source_target_pairs={{0,1},{1,2},{2,3},{3,4},{4,5},{5,6},{6,7},{7,8},{8,9},{9,10},{10,1... | collective-permute-start | bytes 786440 | tf_op jit(solution)/shard_map/ppermute | solution.py:22
  49.7 1.4 copy-start.2
  52.5 46.6 %all-to-all-start = ((bf16[4,128,1408]{1,2,0:T(8,128)(2,1)}), bf16[4,128,1408]{1,2,0:T(8,128)(2,1)}, u32[]{:S(2)}, u32[]{:S(2)}) async-start(bf16[4,128,1408]{1,2,0:T(8,128)(2,1)} %pad_maximum_fusion.1), calls=%async_computation | async-start | bytes 2883584 | tf_op jit(solution)/shard_map/all_to_all | solution.py:94
  114.3 5.3 %collective-permute-start.4 = (f32[8,16,1536]{2,1,0:T(8,128)S(1)}, f32[8,16,1536]{2,1,0:T(8,128)S(1)}, u32[]{:S(2)}, u32[]{:S(2)}) collective-permute-start(f32[8,16,1536]{2,1,0:T(8,128)S(1)} %bitcast.73), channel_id=1, source_target_pairs={{0,32},{32,0},{1,33},{33,1},{2,34},{34,2},{3,35},{35,3},{4,36},{36... | collective-permute-start | bytes 2359304 | tf_op jit(solution)/shard_map/ppermute | solution.py:103
  119.6 9.0 %copy-start.5 = (f32[128]{0:T(128)S(1)}, f32[128]{0:T(128)}, u32[]{:S(2)}) copy-start(f32[128]{0:T(128)} %get-tuple-element.15) | copy-start | bytes 1540
  120.6 31.7 %all-to-all-start.1 = ((f32[8,16,1536]{2,1,0:T(8,128)}), f32[8,16,1536]{2,1,0:T(8,128)}, u32[]{:S(2)}, u32[]{:S(2)}) async-start(f32[8,16,1536]{2,1,0:T(8,128)} %bitcast_add_fusion), calls=%async_computation.1 | async-start | bytes 1572864 | tf_op jit(solution)/shard_map/all_to_all | solution.py:104
  155.6 31.6 %all-to-all-start.2 = ((f32[16,1,1536]{2,1,0:T(1,128)}), f32[16,1,1536]{2,1,0:T(1,128)}, u32[]{:S(2)}, u32[]{:S(2)}) async-start(f32[16,1,1536]{2,1,0:T(1,128)} %all_to_all.14), calls=%async_computation.2 | async-start | bytes 196608 | tf_op jit(solution)/shard_map/all_to_all | solution.py:105

commit v10 on v9

--- a/solution.py
+++ b/solution.py
@@ -92,16 +92,17 @@
     row_factor = jnp.broadcast_to(frame_rows[None], (group, frame_count, model_width))
     sent = jnp.concatenate([row_factor, col_factor], axis=2)
     got = lax.all_to_all(sent, "cy", 0, 0, tiled=True)
-    row_pieces = got[..., :model_width].reshape(group, frame_count, spread, pair, block_rows)
-    col_pieces = got[..., model_width:].reshape(group, frame_count, ring, block_cols)
     tile = jnp.einsum(
-        "sfnha,sfxb->hxnab", row_pieces, col_pieces, preferred_element_type=jnp.float32
-    ).reshape(pair, ring, spread, block_rows * block_cols)
+        "sfr,sfc->rc", got[..., :model_width], got[..., model_width:],
+        preferred_element_type=jnp.float32,
+    ).reshape(spread, pair, block_rows, ring * block_cols)
     core = lax.axis_index("cc")
-    keep = lax.dynamic_index_in_dim(tile, core, 0, keepdims=False)
-    send = lax.dynamic_index_in_dim(tile, pair - 1 - core, 0, keepdims=False)
+    keep = lax.dynamic_index_in_dim(tile, core, 1, keepdims=False)
+    send = lax.dynamic_index_in_dim(tile, pair - 1 - core, 1, keepdims=False)
     half = keep + lax.ppermute(send, "cc", [(0, 1), (1, 0)])
-    part = jnp.sum(lax.all_to_all(half, "cx", 0, 0, tiled=True), axis=0)
+    half = half.reshape(spread, block_rows, ring, block_cols)
+    part = jnp.sum(lax.all_to_all(half, "cx", 2, 2, tiled=True), axis=2)
+    part = part.reshape(spread, block_rows * block_cols)
     summed = jnp.sum(lax.all_to_all(part, CALLS[:2], 0, 0, tiled=True), axis=0)
     return summed.reshape(block_rows, block_cols)
 

time: 190 us -> 205 us (1.079)
  local copies, waits for them, and re-layouts: 26.1 us -> 34.2 us
  other arithmetic: 11.5 us -> 18.1 us
  waiting for transfers between devices: 66 us -> 68.6 us
    unnamed x14 -> x17, local copies, waits for them, and re-layouts: 3.64 us -> 12.8 us
    all_to_all x0 -> x1, other arithmetic: none -> 4.56 us  [weight_gradient(): part = jnp.sum(lax.all_to_all(half, 'cx', 2, 2, tiled=True), axis=2)]
    all_to_all x1, starting transfers between devices: 7.97 us -> 11.7 us  [weight_gradient(): part = jnp.sum(lax.all_to_all(half, 'cx', 2, 2, tiled=True), axis=2)]
    dynamic_slice x1 -> x0, local copies, waits for them, and re-layouts: 3.54 us -> none  [weight_gradient(): keep = lax.dynamic_index_in_dim(tile, core, 0, keepdims=False)]
    all_to_all x1, starting transfers between devices: 12.8 us -> 10.5 us  [weight_gradient(): got = lax.all_to_all(sent, 'cy', 0, 0, tiled=True)]
    slice x2 -> x0, local copies, waits for them, and re-layouts: 2.32 us -> none  [the longest x1 1.29 us: weight_gradient(): got[..., :model_width].reshape(group, frame_count, spread, pair, block_rows)]
    ppermute x2, waiting for transfers between devices: 0.01 us -> 2.23 us  [with_halo(): lax.ppermute(head, axis, [((i + 1) % count, i) for i in range(ends)])]
    reshape x1 -> x3, local copies, waits for them, and re-layouts: 6.09 us -> 8.21 us  [the longest x2 6.29 us: weight_gradient(): half = half.reshape(spread, block_rows, ring, block_cols)]
  transfers between devices with their start and end apart: 8 -> 8, of which waited for: 5 -> 6; matrix products, arithmetic and copies ran while one was open for 9% -> 8% of each run, Pallas kernels for 0% -> 0%
where the time goes in v10:
time: 205 us; the launch traced here: 204 us
  waiting for transfers between devices  68.6 us (33%)
  starting transfers between devices  56.9 us (28%)
  local copies, waits for them, and re-layouts  34.2 us (17%)
  matrix products  25 us (12%)
  other arithmetic  18.1 us (9%)
    all_to_all x1, waiting for transfers between devices, weight_gradient(): got = lax.all_to_all(sent, 'cy', 0, 0, tiled=True)  33.7 us
    all_to_all x1, waiting for transfers between devices, weight_gradient(): part = jnp.sum(lax.all_to_all(half, 'cx', 2, 2, tiled=True), axis=2)  19.5 us
    all_to_all x1, starting transfers between devices, weight_gradient(): summed = jnp.sum(lax.all_to_all(part, CALLS[:2], 0, 0, tiled=True), axis=0)  19.5 us
    unnamed x17, local copies, waits for them, and re-layouts  12.8 us
    all_to_all x1, starting transfers between devices, weight_gradient(): part = jnp.sum(lax.all_to_all(half, 'cx', 2, 2, tiled=True), axis=2)  11.7 us
    all_to_all x1, starting transfers between devices, weight_gradient(): got = lax.all_to_all(sent, 'cy', 0, 0, tiled=True)  10.5 us
    all_to_all x1, waiting for transfers between devices, weight_gradient(): summed = jnp.sum(lax.all_to_all(part, CALLS[:2], 0, 0, tiled=True), axis=0)  9.49 us
    ppermute x2, starting transfers between devices, with_halo(): lax.ppermute(tail, axis, [(i, (i + 1) % count) for i in range(ends)])  9.3 us
  transfers between devices with their start and end apart: 8, of which 6 were waited for; matrix products, arithmetic and copies ran while one was open for 8% of the time, Pallas kernels for 0%

profile of v10, /device:TPU:1, one launch (start us, length us, event | category | flops | bytes accessed | tf_op | source)
XLA Modules:
  0.0 204.3 jit_solution(10205678585338440973)
XLA Ops:
  6.1 5.5 %collective-permute-start = (bf16[128,1024]{1,0:T(8,128)(2,1)}, bf16[128,1024]{1,0:T(8,128)(2,1)}, u32[]{:S(2)}, u32[]{:S(2)}) collective-permute-start(bf16[128,1024]{1,0:T(8,128)(2,1)} %slice.40), channel_id=1, source_target_pairs={{0,1},{1,2},{2,3},{3,4},{4,5},{5,6},{6,7},{7,8},{8,9},{9,10},{10,1... | collective-permute-start | bytes 786440 | tf_op jit(solution)/shard_map/ppermute | solution.py:22
  23.1 2.3 %fusion.24 = f32[4,128,384]{2,1,0:T(8,128)} fusion(bf16[48,4,8,128]{3,2,1,0:T(8,128)(2,1)} %get-tuple-element.23, bf16[128,4,128]{0,2,1:T(8,128)(2,1)} %bitcast.66, pred[128]{0:T(512)(128)(4,1)S(1)} %get-tuple-element.19), kind=kOutput, calls=%fused_computation.35 | convolution fusion | flops 50397184 | bytes 1310848 | tf_op jit(solution)/shard_map/fhd,shd->hfs/dot_general | solution.py:60
  25.4 2.3 %fusion.54 = (f32[4,128]{1,0:T(4,128)S(1)}, f32[4,128,384]{2,1,0:T(8,128)}) fusion(bf16[128,4,128]{0,2,1:T(8,128)(2,1)} %bitcast.74, bf16[384,4,128]{0,2,1:T(8,128)(2,1)} %bitcast.70, pred[128,384]{1,0:T(8,128)(4,1)} %fusion.36), kind=kOutput, calls=%fused_computation.73 | convolution fusion | flops 51118464 | bytes 1361920 | tf_op jit(solution)/shard_map/sub | solution.py:52
  27.7 2.5 %fusion.31 = f32[4,128,384]{2,1,0:T(8,128)} fusion(bf16[128,4,128]{0,2,1:T(8,128)(2,1)S(1)} %bitcast.67, pred[128]{0:T(512)(128)(4,1)S(1)} %get-tuple-element.19, f32[4,128]{1,0:T(4,128)S(1)} %get-tuple-element.24, bf16[128,4,128]{0,2,1:T(8,128)(2,1)S(1)} %bitcast.76, bf16[384,4,128]{0,2,1:T(8,128)(2,1)} %bitcast.71, pred[128,384]{1,0:T(8,128)(4,1)} %fusion.36), kind=kOutput, calls=%fused_computation.45 | convolution fusion | flops 101712768 | bytes 1493120 | tf_op jit(solution)/shard_map/hfs,fhd->shd/dot_general | solution.py:71
  30.2 5.4 %fusion.14 = f32[4,128,384]{2,1,0:T(8,128)} fusion(bf16[128,4,128]{0,2,1:T(8,128)(2,1)S(1)} %bitcast.77, f32[4,128,384]{2,1,0:T(8,128)} %fusion.24, f32[4,128,384]{2,1,0:T(8,128)} %get-tuple-element.25, f32[4,128]{1,0:T(4,128)S(1)} %get-tuple-element.24), kind=kOutput, calls=%fused_computation.23 | convolution fusion | flops 51708800 | bytes 2492416 | tf_op jit(solution)/shard_map/hfs,fhd->shd/dot_general | solution.py:68
  37.9 3.8 %collective-permute-start.2 = (bf16[128,1024]{0,1:T(8,128)(2,1)}, bf16[128,1024]{0,1:T(8,128)(2,1)S(1)}, u32[]{:S(2)}, u32[]{:S(2)}) collective-permute-start(bf16[128,1024]{0,1:T(8,128)(2,1)} %get-tuple-element.20), channel_id=1, source_target_pairs={{0,1},{1,2},{2,3},{3,4},{4,5},{5,6},{6,7},{7,8},{8,9},{9,10},{10,1... | collective-permute-start | bytes 786440 | tf_op jit(solution)/shard_map/ppermute | solution.py:22
  43.0 4.5 %convolution_convert_fusion.2 = bf16[4,128,128]{2,1,0:T(8,128)(2,1)S(1)} fusion(bf16[384,4,128]{0,2,1:T(8,128)(2,1)} %bitcast.72, f32[4,128,384]{2,1,0:T(8,128)} %fusion.24, f32[4,128,384]{2,1,0:T(8,128)} %get-tuple-element.25, f32[4,128]{1,0:T(4,128)S(1)} %get-tuple-element.24), kind=kOutput, calls=%fused_computation.20 | convolution fusion | flops 51774336 | bytes 2099200 | tf_op jit(solution)/shard_map/hfs,shd->fhd/dot_general | solution.py:65
  48.2 2.2 %collective-permute-done.3 = bf16[128,1024]{0,1:T(8,128)(2,1)} collective-permute-done((bf16[128,1024]{0,1:T(8,128)(2,1)}, bf16[128,1024]{0,1:T(8,128)(2,1)}, u32[]{:S(2)}, u32[]{:S(2)}) %collective-permute-start.3) | collective-permute-done | bytes 262176 | tf_op jit(solution)/shard_map/ppermute | solution.py:24
  56.8 10.5 %all-to-all-start = ((bf16[4,128,1408]{2,1,0:T(8,128)(2,1)}), bf16[4,128,1408]{2,1,0:T(8,128)(2,1)}, u32[]{:S(2)}, u32[]{:S(2)}) async-start(bf16[4,128,1408]{2,1,0:T(8,128)(2,1)} %pad_maximum_fusion.1), calls=%async_computation | async-start | bytes 2883584 | tf_op jit(solution)/shard_map/all_to_all | solution.py:94
  67.3 33.7 %all-to-all-done = bf16[4,128,1408]{2,1,0:T(8,128)(2,1)} async-done(((bf16[4,128,1408]{2,1,0:T(8,128)(2,1)}), bf16[4,128,1408]{2,1,0:T(8,128)(2,1)}, u32[]{:S(2)}, u32[]{:S(2)}) %all-to-all-start) | async-done | bytes 1441824 | tf_op jit(solution)/shard_map/all_to_all | solution.py:94
  105.2 3.4 %collective-permute-start.4 = (f32[16,32,384]{2,1,0:T(8,128)}, f32[16,32,384]{2,1,0:T(8,128)}, u32[]{:S(2)}, u32[]{:S(2)}) collective-permute-start(f32[16,32,384]{2,1,0:T(8,128)} %dynamic-slice_bitcast_fusion), channel_id=1, source_target_pairs={{0,32},{32,0},{1,33},{33,1},{2,34},{34,2},{3,35},{35,3},{4,36},{36... | collective-permute-start | bytes 2359304 | tf_op jit(solution)/shard_map/ppermute | solution.py:102
  108.6 2.2 %collective-permute-done.4 = f32[16,32,384]{2,1,0:T(8,128)} collective-permute-done((f32[16,32,384]{2,1,0:T(8,128)}, f32[16,32,384]{2,1,0:T(8,128)}, u32[]{:S(2)}, u32[]{:S(2)}) %collective-permute-start.4) | collective-permute-done | bytes 786464 | tf_op jit(solution)/shard_map/ppermute | solution.py:102
  110.8 2.4 %bitcast_add_fusion = f32[16,32,384]{2,1,0:T(8,128)} fusion(f32[16,32,384]{2,1,0:T(8,128)} %collective-permute-done.4, f32[16,2,32,384]{3,2,1,0:T(8,128)} %bitcast.62, s32[]{:T(128)S(6)} %select_n.18), kind=kLoop, calls=%fused_computation.28 | loop fusion | flops 196608 | bytes 2359300 | tf_op jit(solution)/shard_map/add | solution.py:102
  113.2 3.0 %reshape.184 = f32[16,32,8,48]{3,2,1,0:T(8,128)} reshape(f32[16,32,384]{2,1,0:T(8,128)} %bitcast_add_fusion) | data formatting | bytes 1572864 | tf_op jit(solution)/shard_map/reshape | solution.py:103
  116.2 3.3 %copy.81 = f32[16,32,8,48]{3,1,0,2:T(8,128)} copy(f32[16,32,8,48]{3,2,1,0:T(8,128)} %reshape.184) | data formatting | bytes 1572864 | tf_op jit(solution)/shard_map/reshape | solution.py:103
  119.5 4.1 %reshape.187 = f32[8,1,24576]{2,1,0:T(1,128)} reshape(f32[8,16,32,48]{3,2,1,0:T(8,128)} %bitcast.56) | data formatting | bytes 1572864
  123.5 11.7 %all-to-all-start.1 = ((f32[8,1,24576]{2,1,0:T(1,128)}), f32[8,1,24576]{2,1,0:T(1,128)}, u32[]{:S(2)}, u32[]{:S(2)}) async-start(f32[8,1,24576]{2,1,0:T(1,128)} %reshape.187), calls=%async_computation.1 | async-start | bytes 1572864 | tf_op jit(solution)/shard_map/all_to_all | solution.py:104
  135.3 2.5 %fusion.11 = bf16[4,128,128]{2,1,0:T(8,128)(2,1)} fusion(bf16[48,4,8,128]{3,2,1,0:T(8,128)(2,1)} %get-tuple-element.23, f32[128]{0:T(128)S(1)} %copy-done.6, f32[4,128]{1,0:T(4,128)S(1)} %get-tuple-element.24, bf16[128,4,128]{0,2,1:T(8,128)(2,1)} %bitcast.75, bf16[384,4,128]{0,2,1:T(8,128)(2,1)} %bitcast.73, pred[128,384]{1,0:T(8,128)(4,1)} %fusion.36), kind=kOutput, calls=%fused_computation.19 | convolution fusion | flops 101778304 | bytes 1100288 | tf_op jit(solution)/shard_map/hfs,shd->fhd/dot_general | solution.py:56
  139.4 19.5 %all-to-all-done.1 = f32[8,1,24576]{2,1,0:T(1,128)} async-done(((f32[8,1,24576]{2,1,0:T(1,128)}), f32[8,1,24576]{2,1,0:T(1,128)}, u32[]{:S(2)}, u32[]{:S(2)}) %all-to-all-start.1) | async-done | bytes 786464 | tf_op jit(solution)/shard_map/all_to_all | solution.py:104
  159.4 4.6 %reduce.1 = f32[8,24576]{1,0:T(8,128)} reduce(f32[8,1,24576]{2,1,0:T(1,128)} %all-to-all-done.1, f32[]{:T(128)} %broadcast.137), dimensions={1}, to_apply=%all_to_all.13.reduce_sub_computation | reduce | bytes 1572868 | tf_op jit(solution)/shard_map/all_to_all | solution.py:104
  164.0 3.4 %reshape.188 = f32[8,16,32,48]{3,2,1,0:T(8,128)} reshape(f32[8,24576]{1,0:T(8,128)} %reduce.1) | data formatting | bytes 1572864
  167.4 2.6 %bitcast_reduce_fusion = f32[16,32,48]{2,1,0:T(8,128)} fusion(f32[8,16,32,48]{3,2,1,0:T(8,128)} %reshape.188), kind=kLoop, calls=%fused_computation.74 | loop fusion | flops 172032 | bytes 884736 | tf_op jit(solution)/shard_map/reduce_sum | solution.py:104
  171.8 19.5 %all-to-all-start.2 = ((f32[16,1,1536]{2,1,0:T(1,128)}), f32[16,1,1536]{2,1,0:T(1,128)}, u32[]{:S(2)}, u32[]{:S(2)}) async-start(f32[16,1,1536]{2,1,0:T(1,128)} %all_to_all.14), calls=%async_computation.2 | async-start | bytes 196608 | tf_op jit(solution)/shard_map/all_to_all | solution.py:106
  193.1 9.5 %all-to-all-done.2 = f32[16,1,1536]{2,1,0:T(1,128)} async-done(((f32[16,1,1536]{2,1,0:T(1,128)}), f32[16,1,1536]{2,1,0:T(1,128)}, u32[]{:S(2)}, u32[]{:S(2)}) %all-to-all-start.2) | async-done | bytes 98336 | tf_op jit(solution)/shard_map/all_to_all | solution.py:106
  (48 shorter events, 38.6 us)
Async XLA Ops:
  0.6 1.9 copy-start
  4.8 13.9 %collective-permute-start.1 = (bf16[128,1024]{1,0:T(8,128)(2,1)}, bf16[128,1024]{1,0:T(8,128)(2,1)}, u32[]{:S(2)}, u32[]{:S(2)}) collective-permute-start(bf16[128,1024]{1,0:T(8,128)(2,1)} %slice.40), channel_id=1, source_target_pairs={{1,0},{2,1},{3,2},{4,3},{5,4},{6,5},{7,6},{8,7},{9,8},{10,9},{11,1... | collective-permute-start | bytes 786440 | tf_op jit(solution)/shard_map/ppermute | solution.py:24
  6.1 14.1 %collective-permute-start = (bf16[128,1024]{1,0:T(8,128)(2,1)}, bf16[128,1024]{1,0:T(8,128)(2,1)}, u32[]{:S(2)}, u32[]{:S(2)}) collective-permute-start(bf16[128,1024]{1,0:T(8,128)(2,1)} %slice.40), channel_id=1, source_target_pairs={{0,1},{1,2},{2,3},{3,4},{4,5},{5,6},{6,7},{7,8},{8,9},{9,10},{10,1... | collective-permute-start | bytes 786440 | tf_op jit(solution)/shard_map/ppermute | solution.py:22
  23.1 4.7 %copy-start.3 = (bf16[1,128,512]{1,2,0:T(8,128)(2,1)S(1)}, bf16[1,128,512]{1,2,0:T(8,128)(2,1)}, u32[]{:S(2)}) copy-start(bf16[1,128,512]{1,2,0:T(8,128)(2,1)} %copy.68) | copy-start | bytes 393220
  23.1 4.7 %copy-start.5 = (bf16[128,512]{0,1:T(8,128)(2,1)S(1)}, bf16[128,512]{0,1:T(8,128)(2,1)}, u32[]{:S(2)}) copy-start(bf16[128,512]{0,1:T(8,128)(2,1)} %copy.69) | copy-start | bytes 393220
  37.9 9.7 %collective-permute-start.2 = (bf16[128,1024]{0,1:T(8,128)(2,1)}, bf16[128,1024]{0,1:T(8,128)(2,1)S(1)}, u32[]{:S(2)}, u32[]{:S(2)}) collective-permute-start(bf16[128,1024]{0,1:T(8,128)(2,1)} %get-tuple-element.20), channel_id=1, source_target_pairs={{0,1},{1,2},{2,3},{3,4},{4,5},{5,6},{6,7},{7,8},{8,9},{9,10},{10,1... | collective-permute-start | bytes 786440 | tf_op jit(solution)/shard_map/ppermute | solution.py:22
  41.7 8.8 %collective-permute-start.3 = (bf16[128,1024]{0,1:T(8,128)(2,1)}, bf16[128,1024]{0,1:T(8,128)(2,1)}, u32[]{:S(2)}, u32[]{:S(2)}) collective-permute-start(bf16[128,1024]{0,1:T(8,128)(2,1)} %get-tuple-element.21), channel_id=1, source_target_pairs={{1,0},{2,1},{3,2},{4,3},{5,4},{6,5},{7,6},{8,7},{9,8},{10,9},{11,1... | collective-permute-start | bytes 786440 | tf_op jit(solution)/shard_map/ppermute | solution.py:24
  47.5 0.7 copy-start.4
  54.5 1.1 copy-start.2
  56.8 44.2 %all-to-all-start = ((bf16[4,128,1408]{2,1,0:T(8,128)(2,1)}), bf16[4,128,1408]{2,1,0:T(8,128)(2,1)}, u32[]{:S(2)}, u32[]{:S(2)}) async-start(bf16[4,128,1408]{2,1,0:T(8,128)(2,1)} %pad_maximum_fusion.1), calls=%async_computation | async-start | bytes 2883584 | tf_op jit(solution)/shard_map/all_to_all | solution.py:94
  103.1 1.2 copy-start.1
  105.2 5.6 %collective-permute-start.4 = (f32[16,32,384]{2,1,0:T(8,128)}, f32[16,32,384]{2,1,0:T(8,128)}, u32[]{:S(2)}, u32[]{:S(2)}) collective-permute-start(f32[16,32,384]{2,1,0:T(8,128)} %dynamic-slice_bitcast_fusion), channel_id=1, source_target_pairs={{0,32},{32,0},{1,33},{33,1},{2,34},{34,2},{3,35},{35,3},{4,36},{36... | collective-permute-start | bytes 2359304 | tf_op jit(solution)/shard_map/ppermute | solution.py:102
  119.5 15.8 %copy-start.6 = (f32[128]{0:T(128)S(1)}, f32[128]{0:T(128)}, u32[]{:S(2)}) copy-start(f32[128]{0:T(128)} %get-tuple-element.18) | copy-start | bytes 1540
  123.5 35.4 %all-to-all-start.1 = ((f32[8,1,24576]{2,1,0:T(1,128)}), f32[8,1,24576]{2,1,0:T(1,128)}, u32[]{:S(2)}, u32[]{:S(2)}) async-start(f32[8,1,24576]{2,1,0:T(1,128)} %reshape.187), calls=%async_computation.1 | async-start | bytes 1572864 | tf_op jit(solution)/shard_map/all_to_all | solution.py:104
  171.8 30.8 %all-to-all-start.2 = ((f32[16,1,1536]{2,1,0:T(1,128)}), f32[16,1,1536]{2,1,0:T(1,128)}, u32[]{:S(2)}, u32[]{:S(2)}) async-start(f32[16,1,1536]{2,1,0:T(1,128)} %all_to_all.14), calls=%async_computation.2 | async-start | bytes 196608 | tf_op jit(solution)/shard_map/all_to_all | solution.py:106

commit v11 on v9

--- a/solution.py
+++ b/solution.py
@@ -94,12 +94,15 @@
     got = lax.all_to_all(sent, "cy", 0, 0, tiled=True)
     row_pieces = got[..., :model_width].reshape(group, frame_count, spread, pair, block_rows)
     col_pieces = got[..., model_width:].reshape(group, frame_count, ring, block_cols)
-    tile = jnp.einsum(
-        "sfnha,sfxb->hxnab", row_pieces, col_pieces, preferred_element_type=jnp.float32
-    ).reshape(pair, ring, spread, block_rows * block_cols)
+    halves = [
+        jnp.einsum(
+            "sfna,sfxb->xnab", row_pieces[:, :, :, h], col_pieces, preferred_element_type=jnp.float32
+        ).reshape(ring, spread, block_rows * block_cols)
+        for h in range(pair)
+    ]
     core = lax.axis_index("cc")
-    keep = lax.dynamic_index_in_dim(tile, core, 0, keepdims=False)
-    send = lax.dynamic_index_in_dim(tile, pair - 1 - core, 0, keepdims=False)
+    keep = jnp.where(core == 0, halves[0], halves[1])
+    send = jnp.where(core == 0, halves[1], halves[0])
     half = keep + lax.ppermute(send, "cc", [(0, 1), (1, 0)])
     part = jnp.sum(lax.all_to_all(half, "cx", 0, 0, tiled=True), axis=0)
     summed = jnp.sum(lax.all_to_all(part, CALLS[:2], 0, 0, tiled=True), axis=0)

time: 190 us -> 188 us (0.989)
  local copies, waits for them, and re-layouts: 26.1 us -> 23.5 us
    select_n x0 -> x2, local copies, waits for them, and re-layouts: none -> 7.01 us  [the longest x1 3.51 us: weight_gradient(): keep = jnp.where(core == 0, halves[0], halves[1])]
    reshape x1 -> x0, local copies, waits for them, and re-layouts: 6.09 us -> none  [weight_gradient(): tile = jnp.einsum('sfnha,sfxb->hxnab', row_pieces, col_pieces, preferred_...]
    all_to_all x1, starting transfers between devices: 7.97 us -> 11.7 us  [weight_gradient(): part = jnp.sum(lax.all_to_all(half, 'cx', 0, 0, tiled=True), axis=0)]
    dynamic_slice x1 -> x0, local copies, waits for them, and re-layouts: 3.54 us -> none  [weight_gradient(): keep = lax.dynamic_index_in_dim(tile, core, 0, keepdims=False)]
    all_to_all x1, starting transfers between devices: 12.8 us -> 10.4 us  [weight_gradient(): got = lax.all_to_all(sent, 'cy', 0, 0, tiled=True)]
  transfers between devices with their start and end apart: 8 -> 8, of which waited for: 5 -> 5; matrix products, arithmetic and copies ran while one was open for 9% -> 11% of each run, Pallas kernels for 0% -> 0%
where the time goes in v11:
time: 188 us; the launch traced here: 187 us
  waiting for transfers between devices  65.7 us (35%)
  starting transfers between devices  57.5 us (31%)
  matrix products  26.4 us (14%)
  local copies, waits for them, and re-layouts  23.5 us (12%)
  other arithmetic  12.8 us (7%)
    all_to_all x1, waiting for transfers between devices, weight_gradient(): got = lax.all_to_all(sent, 'cy', 0, 0, tiled=True)  33.8 us
    all_to_all x1, waiting for transfers between devices, weight_gradient(): part = jnp.sum(lax.all_to_all(half, 'cx', 0, 0, tiled=True), axis=0)  19.6 us
    all_to_all x1, starting transfers between devices, weight_gradient(): summed = jnp.sum(lax.all_to_all(part, CALLS[:2], 0, 0, tiled=True), axis=0)  19.5 us
    all_to_all x1, starting transfers between devices, weight_gradient(): part = jnp.sum(lax.all_to_all(half, 'cx', 0, 0, tiled=True), axis=0)  11.7 us
    all_to_all x1, starting transfers between devices, weight_gradient(): got = lax.all_to_all(sent, 'cy', 0, 0, tiled=True)  10.4 us
    ppermute x2, starting transfers between devices, with_halo(): lax.ppermute(tail, axis, [(i, (i + 1) % count) for i in range(ends)])  10 us
    all_to_all x1, waiting for transfers between devices, weight_gradient(): summed = jnp.sum(lax.all_to_all(part, CALLS[:2], 0, 0, tiled=True), axis=0)  9.5 us
    dot_general x1, matrix products, attend(): jnp.einsum('hfs,fhd->shd', grad_scores, query_heads, preferred_element_ty...  5.36 us
  transfers between devices with their start and end apart: 8, of which 5 were waited for; matrix products, arithmetic and copies ran while one was open for 11% of the time, Pallas kernels for 0%

profile of v11, /device:TPU:1, one launch (start us, length us, event | category | flops | bytes accessed | tf_op | source)
XLA Modules:
  0.0 187.4 jit_solution(17163360968631185269)
XLA Ops:
  0.6 1.9 %copy-done = bf16[1024,1536]{1,0:T(8,128)(2,1)S(1)} copy-done((bf16[1024,1536]{1,0:T(8,128)(2,1)S(1)}, bf16[1024,1536]{1,0:T(8,128)(2,1)}, u32[]{:S(2)}) %copy-start) | copy-done | bytes 3145752
  6.1 5.5 %collective-permute-start = (bf16[128,1024]{1,0:T(8,128)(2,1)}, bf16[128,1024]{1,0:T(8,128)(2,1)}, u32[]{:S(2)}, u32[]{:S(2)}) collective-permute-start(bf16[128,1024]{1,0:T(8,128)(2,1)} %slice.48), channel_id=1, source_target_pairs={{0,1},{1,2},{2,3},{3,4},{4,5},{5,6},{6,7},{7,8},{8,9},{9,10},{10,1... | collective-permute-start | bytes 786440 | tf_op jit(solution)/shard_map/ppermute | solution.py:22
  15.6 1.7 copy.72
  23.1 2.3 %fusion.26 = f32[4,128,384]{2,1,0:T(8,128)} fusion(bf16[48,4,8,128]{3,2,1,0:T(8,128)(2,1)} %get-tuple-element.24, bf16[128,4,128]{0,2,1:T(8,128)(2,1)} %bitcast.89, pred[128]{0:T(512)(128)(4,1)S(1)} %get-tuple-element.16), kind=kOutput, calls=%fused_computation.39 | convolution fusion | flops 50397184 | bytes 1310848 | tf_op jit(solution)/shard_map/fhd,shd->hfs/dot_general | solution.py:60
  25.4 2.3 %fusion.58 = (f32[4,128]{1,0:T(4,128)S(1)}, f32[4,128,384]{2,1,0:T(8,128)}) fusion(bf16[128,4,128]{0,2,1:T(8,128)(2,1)} %bitcast.97, bf16[384,4,128]{0,2,1:T(8,128)(2,1)} %bitcast.93, pred[128,384]{1,0:T(8,128)(4,1)} %fusion.39), kind=kOutput, calls=%fused_computation.79 | convolution fusion | flops 51118464 | bytes 1361920 | tf_op jit(solution)/shard_map/sub | solution.py:52
  27.7 2.5 %fusion.34 = f32[4,128,384]{2,1,0:T(8,128)} fusion(bf16[128,4,128]{0,2,1:T(8,128)(2,1)S(1)} %bitcast.90, pred[128]{0:T(512)(128)(4,1)S(1)} %get-tuple-element.16, f32[4,128]{1,0:T(4,128)S(1)} %get-tuple-element.25, bf16[128,4,128]{0,2,1:T(8,128)(2,1)S(1)} %bitcast.99, bf16[384,4,128]{0,2,1:T(8,128)(2,1)} %bitcast.94, pred[128,384]{1,0:T(8,128)(4,1)} %fusion.39), kind=kOutput, calls=%fused_computation.50 | convolution fusion | flops 101712768 | bytes 1493120 | tf_op jit(solution)/shard_map/hfs,fhd->shd/dot_general | solution.py:71
  30.2 5.4 %fusion.14 = f32[4,128,384]{2,1,0:T(8,128)} fusion(bf16[128,4,128]{0,2,1:T(8,128)(2,1)S(1)} %bitcast.100, f32[4,128,384]{2,1,0:T(8,128)} %fusion.26, f32[4,128,384]{2,1,0:T(8,128)} %get-tuple-element.26, f32[4,128]{1,0:T(4,128)S(1)} %get-tuple-element.25), kind=kOutput, calls=%fused_computation.25 | convolution fusion | flops 51708800 | bytes 2492416 | tf_op jit(solution)/shard_map/hfs,fhd->shd/dot_general | solution.py:68
  37.9 4.5 %collective-permute-start.2 = (bf16[128,1024]{0,1:T(8,128)(2,1)}, bf16[128,1024]{0,1:T(8,128)(2,1)}, u32[]{:S(2)}, u32[]{:S(2)}) collective-permute-start(bf16[128,1024]{0,1:T(8,128)(2,1)} %get-tuple-element.21), channel_id=1, source_target_pairs={{0,1},{1,2},{2,3},{3,4},{4,5},{5,6},{6,7},{7,8},{8,9},{9,10},{10,1... | collective-permute-start | bytes 786440 | tf_op jit(solution)/shard_map/ppermute | solution.py:22
  44.6 4.5 %convolution_convert_fusion.2 = bf16[4,128,128]{2,1,0:T(8,128)(2,1)S(1)} fusion(bf16[384,4,128]{0,2,1:T(8,128)(2,1)} %bitcast.95, f32[4,128,384]{2,1,0:T(8,128)} %fusion.26, f32[4,128,384]{2,1,0:T(8,128)} %get-tuple-element.26, f32[4,128]{1,0:T(4,128)S(1)} %get-tuple-element.25), kind=kOutput, calls=%fused_computation.24 | convolution fusion | flops 51774336 | bytes 2099200 | tf_op jit(solution)/shard_map/hfs,shd->fhd/dot_general | solution.py:65
  53.3 10.4 %all-to-all-start = ((bf16[4,128,1408]{1,2,0:T(8,128)(2,1)}), bf16[4,128,1408]{1,2,0:T(8,128)(2,1)}, u32[]{:S(2)}, u32[]{:S(2)}) async-start(bf16[4,128,1408]{1,2,0:T(8,128)(2,1)} %pad_maximum_fusion.1), calls=%async_computation | async-start | bytes 2883584 | tf_op jit(solution)/shard_map/all_to_all | solution.py:94
  63.7 33.8 %all-to-all-done = bf16[4,128,1408]{1,2,0:T(8,128)(2,1)} async-done(((bf16[4,128,1408]{1,2,0:T(8,128)(2,1)}), bf16[4,128,1408]{1,2,0:T(8,128)(2,1)}, u32[]{:S(2)}, u32[]{:S(2)}) %all-to-all-start) | async-done | bytes 1441824 | tf_op jit(solution)/shard_map/all_to_all | solution.py:94
  100.6 2.7 %fusion.3 = (f32[8,16,32,48]{3,2,1,0:T(8,128)}, f32[8,16,32,48]{3,2,1,0:T(8,128)}) fusion(f32[8,48,16,32,1]{1,3,4,2,0:T(8,128)S(1)} %fusion.23, pred[]{:T(512)S(6)} %eq.18, bf16[4,128,16,1,32]{1,4,3,2,0:T(8,128)(2,1)S(1)} %get-tuple-element.19, bf16[4,128,8,48,1]{1,3,2,0,4:T(8,128)(2,1)S(1)} %bitcast.81), kind=kOutput, calls=%fused_computation.6 | convolution fusion | flops 201719808 | bytes 3276801 | tf_op jit(solution)/shard_map/sfna,sfxb->xnab/dot_general | solution.py:98
  103.3 3.5 %select_n.41 = f32[8,16,1536]{2,1,0:T(8,128)} reshape(f32[8,16,32,48]{3,2,1,0:T(8,128)} %get-tuple-element.17) | data formatting | bytes 1572864 | tf_op jit(solution)/shard_map/jit(_where)/select_n | solution.py:105
  106.8 3.4 %collective-permute-start.4 = (f32[8,16,1536]{2,1,0:T(8,128)}, f32[8,16,1536]{2,1,0:T(8,128)}, u32[]{:S(2)}, u32[]{:S(2)}) collective-permute-start(f32[8,16,1536]{2,1,0:T(8,128)} %select_n.41), channel_id=1, source_target_pairs={{0,32},{32,0},{1,33},{33,1},{2,34},{34,2},{3,35},{35,3},{4,36},{36... | collective-permute-start | bytes 2359304 | tf_op jit(solution)/shard_map/ppermute | solution.py:106
  110.2 3.5 %select_n.38 = f32[8,16,1536]{2,1,0:T(8,128)} reshape(f32[8,16,32,48]{3,2,1,0:T(8,128)} %get-tuple-element.18) | data formatting | bytes 1572864 | tf_op jit(solution)/shard_map/jit(_where)/select_n | solution.py:104
  113.7 2.3 %add.53 = f32[8,16,1536]{2,1,0:T(8,128)} add(f32[8,16,1536]{2,1,0:T(8,128)} %select_n.38, f32[8,16,1536]{2,1,0:T(8,128)} %collective-permute-done.4) | non-fusion elementwise | flops 196608 | bytes 2359296 | tf_op jit(solution)/shard_map/add | solution.py:106
  116.0 11.7 %all-to-all-start.1 = ((f32[8,16,1536]{2,1,0:T(8,128)}), f32[8,16,1536]{2,1,0:T(8,128)}, u32[]{:S(2)}, u32[]{:S(2)}) async-start(f32[8,16,1536]{2,1,0:T(8,128)} %add.53), calls=%async_computation.1 | async-start | bytes 1572864 | tf_op jit(solution)/shard_map/all_to_all | solution.py:107
  127.8 2.5 %fusion.13 = bf16[4,128,128]{2,1,0:T(8,128)(2,1)} fusion(bf16[48,4,8,128]{3,2,1,0:T(8,128)(2,1)} %get-tuple-element.24, f32[128]{0:T(128)S(1)} %copy-done.5, f32[4,128]{1,0:T(4,128)S(1)} %get-tuple-element.25, bf16[128,4,128]{0,2,1:T(8,128)(2,1)} %bitcast.98, bf16[384,4,128]{0,2,1:T(8,128)(2,1)} %bitcast.96, pred[128,384]{1,0:T(8,128)(4,1)} %fusion.39), kind=kOutput, calls=%fused_computation.23 | convolution fusion | flops 101778304 | bytes 1100288 | tf_op jit(solution)/shard_map/hfs,shd->fhd/dot_general | solution.py:56
  130.3 1.7 copy.59
  131.9 19.6 %all-to-all-done.1 = f32[8,16,1536]{2,1,0:T(8,128)} async-done(((f32[8,16,1536]{2,1,0:T(8,128)}), f32[8,16,1536]{2,1,0:T(8,128)}, u32[]{:S(2)}, u32[]{:S(2)}) %all-to-all-start.1) | async-done | bytes 786464 | tf_op jit(solution)/shard_map/all_to_all | solution.py:107
  151.5 1.8 reduce_sum.38
  154.9 19.5 %all-to-all-start.2 = ((f32[16,1,1536]{2,1,0:T(1,128)}), f32[16,1,1536]{2,1,0:T(1,128)}, u32[]{:S(2)}, u32[]{:S(2)}) async-start(f32[16,1,1536]{2,1,0:T(1,128)} %all_to_all.14), calls=%async_computation.2 | async-start | bytes 196608 | tf_op jit(solution)/shard_map/all_to_all | solution.py:108
  174.4 1.9 fusion.12
  176.3 9.5 %all-to-all-done.2 = f32[16,1,1536]{2,1,0:T(1,128)} async-done(((f32[16,1,1536]{2,1,0:T(1,128)}), f32[16,1,1536]{2,1,0:T(1,128)}, u32[]{:S(2)}, u32[]{:S(2)}) %all-to-all-start.2) | async-done | bytes 98336 | tf_op jit(solution)/shard_map/all_to_all | solution.py:108
  (45 shorter events, 27.6 us)
Async XLA Ops:
  0.6 1.9 %copy-start = (bf16[1024,1536]{1,0:T(8,128)(2,1)S(1)}, bf16[1024,1536]{1,0:T(8,128)(2,1)}, u32[]{:S(2)}) copy-start(bf16[1024,1536]{1,0:T(8,128)(2,1)} %param.5) | copy-start | bytes 9437188
  4.8 13.9 %collective-permute-start.1 = (bf16[128,1024]{1,0:T(8,128)(2,1)}, bf16[128,1024]{1,0:T(8,128)(2,1)}, u32[]{:S(2)}, u32[]{:S(2)}) collective-permute-start(bf16[128,1024]{1,0:T(8,128)(2,1)} %slice.48), channel_id=1, source_target_pairs={{1,0},{2,1},{3,2},{4,3},{5,4},{6,5},{7,6},{8,7},{9,8},{10,9},{11,1... | collective-permute-start | bytes 786440 | tf_op jit(solution)/shard_map/ppermute | solution.py:24
  6.1 14.1 %collective-permute-start = (bf16[128,1024]{1,0:T(8,128)(2,1)}, bf16[128,1024]{1,0:T(8,128)(2,1)}, u32[]{:S(2)}, u32[]{:S(2)}) collective-permute-start(bf16[128,1024]{1,0:T(8,128)(2,1)} %slice.48), channel_id=1, source_target_pairs={{0,1},{1,2},{2,3},{3,4},{4,5},{5,6},{6,7},{7,8},{8,9},{9,10},{10,1... | collective-permute-start | bytes 786440 | tf_op jit(solution)/shard_map/ppermute | solution.py:22
  23.0 4.7 %copy-start.3 = (bf16[1,128,512]{1,2,0:T(8,128)(2,1)S(1)}, bf16[1,128,512]{1,2,0:T(8,128)(2,1)}, u32[]{:S(2)}) copy-start(bf16[1,128,512]{1,2,0:T(8,128)(2,1)} %copy.65) | copy-start | bytes 393220
  23.1 4.7 %copy-start.4 = (bf16[128,512]{0,1:T(8,128)(2,1)S(1)}, bf16[128,512]{0,1:T(8,128)(2,1)}, u32[]{:S(2)}) copy-start(bf16[128,512]{0,1:T(8,128)(2,1)} %copy.72) | copy-start | bytes 393220
  35.6 8.1 %copy-start.2 = (bf16[1,128,1024]{2,1,0:T(8,128)(2,1)S(1)}, bf16[1,128,1024]{2,1,0:T(8,128)(2,1)}, u32[]{:S(2)}) copy-start(bf16[1,128,1024]{2,1,0:T(8,128)(2,1)} %param.4) | copy-start | bytes 786436
  37.9 11.2 %collective-permute-start.2 = (bf16[128,1024]{0,1:T(8,128)(2,1)}, bf16[128,1024]{0,1:T(8,128)(2,1)}, u32[]{:S(2)}, u32[]{:S(2)}) collective-permute-start(bf16[128,1024]{0,1:T(8,128)(2,1)} %get-tuple-element.21), channel_id=1, source_target_pairs={{0,1},{1,2},{2,3},{3,4},{4,5},{5,6},{6,7},{7,8},{8,9},{9,10},{10,1... | collective-permute-start | bytes 786440 | tf_op jit(solution)/shard_map/ppermute | solution.py:22
  42.4 8.1 %collective-permute-start.3 = (bf16[128,1024]{0,1:T(8,128)(2,1)}, bf16[128,1024]{0,1:T(8,128)(2,1)}, u32[]{:S(2)}, u32[]{:S(2)}) collective-permute-start(bf16[128,1024]{0,1:T(8,128)(2,1)} %get-tuple-element.22), channel_id=1, source_target_pairs={{1,0},{2,1},{3,2},{4,3},{5,4},{6,5},{7,6},{8,7},{9,8},{10,9},{11,1... | collective-permute-start | bytes 786440 | tf_op jit(solution)/shard_map/ppermute | solution.py:24
  49.1 2.8 %copy-start.1 = (bf16[128,1024]{0,1:T(8,128)(2,1)S(1)}, bf16[128,1024]{0,1:T(8,128)(2,1)}, u32[]{:S(2)}) copy-start(bf16[128,1024]{0,1:T(8,128)(2,1)} %copy.53) | copy-start | bytes 786436
  53.3 44.2 %all-to-all-start = ((bf16[4,128,1408]{1,2,0:T(8,128)(2,1)}), bf16[4,128,1408]{1,2,0:T(8,128)(2,1)}, u32[]{:S(2)}, u32[]{:S(2)}) async-start(bf16[4,128,1408]{1,2,0:T(8,128)(2,1)} %pad_maximum_fusion.1), calls=%async_computation | async-start | bytes 2883584 | tf_op jit(solution)/shard_map/all_to_all | solution.py:94
  106.8 6.9 %collective-permute-start.4 = (f32[8,16,1536]{2,1,0:T(8,128)}, f32[8,16,1536]{2,1,0:T(8,128)}, u32[]{:S(2)}, u32[]{:S(2)}) collective-permute-start(f32[8,16,1536]{2,1,0:T(8,128)} %select_n.41), channel_id=1, source_target_pairs={{0,32},{32,0},{1,33},{33,1},{2,34},{34,2},{3,35},{35,3},{4,36},{36... | collective-permute-start | bytes 2359304 | tf_op jit(solution)/shard_map/ppermute | solution.py:106
  113.7 14.1 %copy-start.5 = (f32[128]{0:T(128)S(1)}, f32[128]{0:T(128)}, u32[]{:S(2)}) copy-start(f32[128]{0:T(128)} %get-tuple-element.15) | copy-start | bytes 1540
  116.0 35.5 %all-to-all-start.1 = ((f32[8,16,1536]{2,1,0:T(8,128)}), f32[8,16,1536]{2,1,0:T(8,128)}, u32[]{:S(2)}, u32[]{:S(2)}) async-start(f32[8,16,1536]{2,1,0:T(8,128)} %add.53), calls=%async_computation.1 | async-start | bytes 1572864 | tf_op jit(solution)/shard_map/all_to_all | solution.py:107
  154.9 30.8 %all-to-all-start.2 = ((f32[16,1,1536]{2,1,0:T(1,128)}), f32[16,1,1536]{2,1,0:T(1,128)}, u32[]{:S(2)}, u32[]{:S(2)}) async-start(f32[16,1,1536]{2,1,0:T(1,128)} %all_to_all.14), calls=%async_computation.2 | async-start | bytes 196608 | tf_op jit(solution)/shard_map/all_to_all | solution.py:108

commit v12 on v11

--- a/solution.py
+++ b/solution.py
@@ -94,15 +94,16 @@
     got = lax.all_to_all(sent, "cy", 0, 0, tiled=True)
     row_pieces = got[..., :model_width].reshape(group, frame_count, spread, pair, block_rows)
     col_pieces = got[..., model_width:].reshape(group, frame_count, ring, block_cols)
-    halves = [
+    core = lax.axis_index("cc")
+    keep, send = [
         jnp.einsum(
-            "sfna,sfxb->xnab", row_pieces[:, :, :, h], col_pieces, preferred_element_type=jnp.float32
+            "sfna,sfxb->xnab",
+            lax.dynamic_index_in_dim(row_pieces, h, 3, keepdims=False),
+            col_pieces,
+            preferred_element_type=jnp.float32,
         ).reshape(ring, spread, block_rows * block_cols)
-        for h in range(pair)
+        for h in (core, pair - 1 - core)
     ]
-    core = lax.axis_index("cc")
-    keep = jnp.where(core == 0, halves[0], halves[1])
-    send = jnp.where(core == 0, halves[1], halves[0])
     half = keep + lax.ppermute(send, "cc", [(0, 1), (1, 0)])
     part = jnp.sum(lax.all_to_all(half, "cx", 0, 0, tiled=True), axis=0)
     summed = jnp.sum(lax.all_to_all(part, CALLS[:2], 0, 0, tiled=True), axis=0)

time: 188 us -> 192 us (1.021)
    select_n x2 -> x0, local copies, waits for them, and re-layouts: 7.01 us -> none  [the longest x1 3.51 us: weight_gradient(): keep = jnp.where(core == 0, halves[0], halves[1])]
    reshape x0 -> x2, local copies, waits for them, and re-layouts: none -> 7 us  [weight_gradient(): keep, send = [jnp.einsum('sfna,sfxb->xnab', lax.dynamic_index_in_dim(row_...]
    unnamed x13 -> x19, local copies, waits for them, and re-layouts: 3.57 us -> 4.28 us
  transfers between devices with their start and end apart: 8 -> 8, of which waited for: 5 -> 5; matrix products, arithmetic and copies ran while one was open for 11% -> 13% of each run, Pallas kernels for 0% -> 0%
where the time goes in v12:
time: 192 us; the launch traced here: 191 us
  waiting for transfers between devices  65.4 us (34%)
  starting transfers between devices  57.6 us (30%)
  matrix products  28 us (15%)
  local copies, waits for them, and re-layouts  25.4 us (13%)
  other arithmetic  12.8 us (7%)
    all_to_all x1, waiting for transfers between devices, weight_gradient(): got = lax.all_to_all(sent, 'cy', 0, 0, tiled=True)  33.8 us
    all_to_all x1, waiting for transfers between devices, weight_gradient(): part = jnp.sum(lax.all_to_all(half, 'cx', 0, 0, tiled=True), axis=0)  19.7 us
    all_to_all x1, starting transfers between devices, weight_gradient(): summed = jnp.sum(lax.all_to_all(part, CALLS[:2], 0, 0, tiled=True), axis=0)  19.5 us
    all_to_all x1, starting transfers between devices, weight_gradient(): part = jnp.sum(lax.all_to_all(half, 'cx', 0, 0, tiled=True), axis=0)  11.7 us
    all_to_all x1, starting transfers between devices, weight_gradient(): got = lax.all_to_all(sent, 'cy', 0, 0, tiled=True)  10.4 us
    ppermute x2, starting transfers between devices, with_halo(): lax.ppermute(tail, axis, [(i, (i + 1) % count) for i in range(ends)])  10 us
    all_to_all x1, waiting for transfers between devices, weight_gradient(): summed = jnp.sum(lax.all_to_all(part, CALLS[:2], 0, 0, tiled=True), axis=0)  9.47 us
    reshape x2, local copies, waits for them, and re-layouts, weight_gradient(): keep, send = [jnp.einsum('sfna,sfxb->xnab', lax.dynamic_index_in_dim(row_...  7 us
  transfers between devices with their start and end apart: 8, of which 5 were waited for; matrix products, arithmetic and copies ran while one was open for 13% of the time, Pallas kernels for 0%

profile of v12, /device:TPU:1, one launch (start us, length us, event | category | flops | bytes accessed | tf_op | source)
XLA Modules:
  0.0 190.6 jit_solution(13709833687161908025)
XLA Ops:
  0.6 1.9 copy-done
  6.1 5.5 %collective-permute-start = (bf16[128,1024]{1,0:T(8,128)(2,1)}, bf16[128,1024]{1,0:T(8,128)(2,1)}, u32[]{:S(2)}, u32[]{:S(2)}) collective-permute-start(bf16[128,1024]{1,0:T(8,128)(2,1)} %slice.40), channel_id=1, source_target_pairs={{0,1},{1,2},{2,3},{3,4},{4,5},{5,6},{6,7},{7,8},{8,9},{9,10},{10,1... | collective-permute-start | bytes 786440 | tf_op jit(solution)/shard_map/ppermute | solution.py:22
  23.1 2.3 %fusion.26 = f32[4,128,384]{2,1,0:T(8,128)} fusion(bf16[48,4,8,128]{3,2,1,0:T(8,128)(2,1)} %get-tuple-element.22, bf16[128,4,128]{0,2,1:T(8,128)(2,1)} %bitcast.81, pred[128]{0:T(512)(128)(4,1)S(1)} %get-tuple-element.16), kind=kOutput, calls=%fused_computation.37 | convolution fusion | flops 50397184 | bytes 1310848 | tf_op jit(solution)/shard_map/fhd,shd->hfs/dot_general | solution.py:60
  25.4 2.3 %fusion.57 = (f32[4,128]{1,0:T(4,128)S(1)}, f32[4,128,384]{2,1,0:T(8,128)}) fusion(bf16[128,4,128]{0,2,1:T(8,128)(2,1)} %bitcast.89, bf16[384,4,128]{0,2,1:T(8,128)(2,1)} %bitcast.85, pred[128,384]{1,0:T(8,128)(4,1)} %fusion.39), kind=kOutput, calls=%fused_computation.78 | convolution fusion | flops 51118464 | bytes 1361920 | tf_op jit(solution)/shard_map/sub | solution.py:52
  27.8 2.5 %fusion.34 = f32[4,128,384]{2,1,0:T(8,128)} fusion(bf16[128,4,128]{0,2,1:T(8,128)(2,1)S(1)} %bitcast.82, pred[128]{0:T(512)(128)(4,1)S(1)} %get-tuple-element.16, f32[4,128]{1,0:T(4,128)S(1)} %get-tuple-element.23, bf16[128,4,128]{0,2,1:T(8,128)(2,1)S(1)} %bitcast.91, bf16[384,4,128]{0,2,1:T(8,128)(2,1)} %bitcast.86, pred[128,384]{1,0:T(8,128)(4,1)} %fusion.39), kind=kOutput, calls=%fused_computation.48 | convolution fusion | flops 101712768 | bytes 1493120 | tf_op jit(solution)/shard_map/hfs,fhd->shd/dot_general | solution.py:71
  30.3 5.3 %fusion.12 = f32[4,128,384]{2,1,0:T(8,128)} fusion(bf16[128,4,128]{0,2,1:T(8,128)(2,1)S(1)} %bitcast.92, f32[4,128,384]{2,1,0:T(8,128)} %fusion.26, f32[4,128,384]{2,1,0:T(8,128)} %get-tuple-element.24, f32[4,128]{1,0:T(4,128)S(1)} %get-tuple-element.23), kind=kOutput, calls=%fused_computation.23 | convolution fusion | flops 51708800 | bytes 2492416 | tf_op jit(solution)/shard_map/hfs,fhd->shd/dot_general | solution.py:68
  37.9 4.5 %collective-permute-start.2 = (bf16[128,1024]{0,1:T(8,128)(2,1)}, bf16[128,1024]{0,1:T(8,128)(2,1)}, u32[]{:S(2)}, u32[]{:S(2)}) collective-permute-start(bf16[128,1024]{0,1:T(8,128)(2,1)} %get-tuple-element.19), channel_id=1, source_target_pairs={{0,1},{1,2},{2,3},{3,4},{4,5},{5,6},{6,7},{7,8},{8,9},{9,10},{10,1... | collective-permute-start | bytes 786440 | tf_op jit(solution)/shard_map/ppermute | solution.py:22
  44.8 4.5 %convolution_convert_fusion.2 = bf16[4,128,128]{2,1,0:T(8,128)(2,1)S(1)} fusion(bf16[384,4,128]{0,2,1:T(8,128)(2,1)} %bitcast.87, f32[4,128,384]{2,1,0:T(8,128)} %fusion.26, f32[4,128,384]{2,1,0:T(8,128)} %get-tuple-element.24, f32[4,128]{1,0:T(4,128)S(1)} %get-tuple-element.23), kind=kOutput, calls=%fused_computation.22 | convolution fusion | flops 51774336 | bytes 2099200 | tf_op jit(solution)/shard_map/hfs,shd->fhd/dot_general | solution.py:65
  53.9 10.4 %all-to-all-start = ((bf16[4,128,1408]{1,2,0:T(8,128)(2,1)}), bf16[4,128,1408]{1,2,0:T(8,128)(2,1)}, u32[]{:S(2)}, u32[]{:S(2)}) async-start(bf16[4,128,1408]{1,2,0:T(8,128)(2,1)} %pad_maximum_fusion.1), calls=%async_computation | async-start | bytes 2883584 | tf_op jit(solution)/shard_map/all_to_all | solution.py:94
  64.3 33.8 %all-to-all-done = bf16[4,128,1408]{1,2,0:T(8,128)(2,1)} async-done(((bf16[4,128,1408]{1,2,0:T(8,128)(2,1)}), bf16[4,128,1408]{1,2,0:T(8,128)(2,1)}, u32[]{:S(2)}, u32[]{:S(2)}) %all-to-all-start) | async-done | bytes 1441824 | tf_op jit(solution)/shard_map/all_to_all | solution.py:94
  101.3 2.1 %convolution_bitcast_fusion = f32[8,16,32,48]{3,2,1,0:T(8,128)} fusion(bf16[4,128,16,1,32]{1,4,3,2,0:T(8,128)(2,1)S(1)} %get-tuple-element.17, bf16[4,128,8,48,1]{1,3,2,0,4:T(8,128)(2,1)S(1)} %bitcast.72), kind=kOutput, calls=%fused_computation.6 | convolution fusion | flops 201326592 | bytes 1703936 | tf_op jit(solution)/shard_map/sfna,sfxb->xnab/dot_general | solution.py:99
  103.4 3.5 %reshape.190 = f32[8,16,1536]{2,1,0:T(8,128)} reshape(f32[8,16,32,48]{3,2,1,0:T(8,128)} %convolution_bitcast_fusion) | data formatting | bytes 1572864 | tf_op jit(solution)/shard_map/reshape | solution.py:104
  106.9 3.4 %collective-permute-start.4 = (f32[8,16,1536]{2,1,0:T(8,128)}, f32[8,16,1536]{2,1,0:T(8,128)}, u32[]{:S(2)}, u32[]{:S(2)}) collective-permute-start(f32[8,16,1536]{2,1,0:T(8,128)} %reshape.190), channel_id=1, source_target_pairs={{0,32},{32,0},{1,33},{33,1},{2,34},{34,2},{3,35},{35,3},{4,36},{36... | collective-permute-start | bytes 2359304 | tf_op jit(solution)/shard_map/ppermute | solution.py:107
  110.2 3.1 %convolution_bitcast_fusion.1 = f32[8,16,32,48]{3,2,1,0:T(8,128)} fusion(bf16[4,128,16,1,32]{1,4,3,2,0:T(8,128)(2,1)} %get-tuple-element.18, bf16[4,128,8,48,1]{1,3,2,0,4:T(8,128)(2,1)S(1)} %bitcast.73), kind=kOutput, calls=%fused_computation.7 | convolution fusion | flops 201326592 | bytes 1703936 | tf_op jit(solution)/shard_map/sfna,sfxb->xnab/dot_general | solution.py:99
  113.3 3.5 %reshape.189 = f32[8,16,1536]{2,1,0:T(8,128)} reshape(f32[8,16,32,48]{3,2,1,0:T(8,128)} %convolution_bitcast_fusion.1) | data formatting | bytes 1572864 | tf_op jit(solution)/shard_map/reshape | solution.py:104
  116.8 2.4 %add.63 = f32[8,16,1536]{2,1,0:T(8,128)} add(f32[8,16,1536]{2,1,0:T(8,128)} %reshape.189, f32[8,16,1536]{2,1,0:T(8,128)} %collective-permute-done.4) | non-fusion elementwise | flops 196608 | bytes 2359296 | tf_op jit(solution)/shard_map/add | solution.py:107
  119.2 11.7 %all-to-all-start.1 = ((f32[8,16,1536]{2,1,0:T(8,128)}), f32[8,16,1536]{2,1,0:T(8,128)}, u32[]{:S(2)}, u32[]{:S(2)}) async-start(f32[8,16,1536]{2,1,0:T(8,128)} %add.63), calls=%async_computation.1 | async-start | bytes 1572864 | tf_op jit(solution)/shard_map/all_to_all | solution.py:108
  131.0 2.4 %fusion.11 = bf16[4,128,128]{2,1,0:T(8,128)(2,1)} fusion(bf16[48,4,8,128]{3,2,1,0:T(8,128)(2,1)S(1)} %copy-done.3, f32[128]{0:T(128)S(1)} %copy-done.8, f32[4,128]{1,0:T(4,128)S(1)} %get-tuple-element.23, bf16[128,4,128]{0,2,1:T(8,128)(2,1)} %bitcast.90, bf16[384,4,128]{0,2,1:T(8,128)(2,1)} %bitcast.88, pred[128,384]{1,0:T(8,128)(4,1)} %fusion.39), kind=kOutput, calls=%fused_computation.21 | convolution fusion | flops 101778304 | bytes 1100288 | tf_op jit(solution)/shard_map/hfs,shd->fhd/dot_general | solution.py:56
  133.3 1.7 copy.59
  135.1 19.7 %all-to-all-done.1 = f32[8,16,1536]{2,1,0:T(8,128)} async-done(((f32[8,16,1536]{2,1,0:T(8,128)}), f32[8,16,1536]{2,1,0:T(8,128)}, u32[]{:S(2)}, u32[]{:S(2)}) %all-to-all-start.1) | async-done | bytes 786464 | tf_op jit(solution)/shard_map/all_to_all | solution.py:108
  154.7 1.8 reduce_sum.38
  158.1 19.5 %all-to-all-start.2 = ((f32[16,1,1536]{2,1,0:T(1,128)}), f32[16,1,1536]{2,1,0:T(1,128)}, u32[]{:S(2)}, u32[]{:S(2)}) async-start(f32[16,1,1536]{2,1,0:T(1,128)} %all_to_all.14), calls=%async_computation.2 | async-start | bytes 196608 | tf_op jit(solution)/shard_map/all_to_all | solution.py:109
  177.6 1.9 fusion.10
  179.5 9.5 %all-to-all-done.2 = f32[16,1,1536]{2,1,0:T(1,128)} async-done(((f32[16,1,1536]{2,1,0:T(1,128)}), f32[16,1,1536]{2,1,0:T(1,128)}, u32[]{:S(2)}, u32[]{:S(2)}) %all-to-all-start.2) | async-done | bytes 98336 | tf_op jit(solution)/shard_map/all_to_all | solution.py:109
  (51 shorter events, 30.0 us)
Async XLA Ops:
  0.6 1.9 copy-start
  4.8 13.9 %collective-permute-start.1 = (bf16[128,1024]{1,0:T(8,128)(2,1)}, bf16[128,1024]{1,0:T(8,128)(2,1)}, u32[]{:S(2)}, u32[]{:S(2)}) collective-permute-start(bf16[128,1024]{1,0:T(8,128)(2,1)} %slice.40), channel_id=1, source_target_pairs={{1,0},{2,1},{3,2},{4,3},{5,4},{6,5},{7,6},{8,7},{9,8},{10,9},{11,1... | collective-permute-start | bytes 786440 | tf_op jit(solution)/shard_map/ppermute | solution.py:24
  6.1 14.1 %collective-permute-start = (bf16[128,1024]{1,0:T(8,128)(2,1)}, bf16[128,1024]{1,0:T(8,128)(2,1)}, u32[]{:S(2)}, u32[]{:S(2)}) collective-permute-start(bf16[128,1024]{1,0:T(8,128)(2,1)} %slice.40), channel_id=1, source_target_pairs={{0,1},{1,2},{2,3},{3,4},{4,5},{5,6},{6,7},{7,8},{8,9},{9,10},{10,1... | collective-permute-start | bytes 786440 | tf_op jit(solution)/shard_map/ppermute | solution.py:22
  23.1 4.7 %copy-start.4 = (bf16[1,128,512]{1,2,0:T(8,128)(2,1)S(1)}, bf16[1,128,512]{1,2,0:T(8,128)(2,1)}, u32[]{:S(2)}) copy-start(bf16[1,128,512]{1,2,0:T(8,128)(2,1)} %copy.65) | copy-start | bytes 393220
  23.1 4.7 %copy-start.7 = (bf16[128,512]{0,1:T(8,128)(2,1)S(1)}, bf16[128,512]{0,1:T(8,128)(2,1)}, u32[]{:S(2)}) copy-start(bf16[128,512]{0,1:T(8,128)(2,1)} %copy.70) | copy-start | bytes 393220
  37.9 11.5 %collective-permute-start.2 = (bf16[128,1024]{0,1:T(8,128)(2,1)}, bf16[128,1024]{0,1:T(8,128)(2,1)}, u32[]{:S(2)}, u32[]{:S(2)}) collective-permute-start(bf16[128,1024]{0,1:T(8,128)(2,1)} %get-tuple-element.19), channel_id=1, source_target_pairs={{0,1},{1,2},{2,3},{3,4},{4,5},{5,6},{6,7},{7,8},{8,9},{9,10},{10,1... | collective-permute-start | bytes 786440 | tf_op jit(solution)/shard_map/ppermute | solution.py:22
  42.4 8.1 %collective-permute-start.3 = (bf16[128,1024]{0,1:T(8,128)(2,1)}, bf16[128,1024]{0,1:T(8,128)(2,1)}, u32[]{:S(2)}, u32[]{:S(2)}) collective-permute-start(bf16[128,1024]{0,1:T(8,128)(2,1)} %get-tuple-element.20), channel_id=1, source_target_pairs={{1,0},{2,1},{3,2},{4,3},{5,4},{6,5},{7,6},{8,7},{9,8},{10,9},{11,1... | collective-permute-start | bytes 786440 | tf_op jit(solution)/shard_map/ppermute | solution.py:24
  49.4 2.5 %copy-start.5 = (bf16[4,128,128]{2,1,0:T(8,128)(2,1)}, bf16[4,128,128]{2,1,0:T(8,128)(2,1)S(1)}, u32[]{:S(2)}) copy-start(bf16[4,128,128]{2,1,0:T(8,128)(2,1)S(1)} %convolution_convert_fusion.2) | copy-start | bytes 393220
  51.8 0.7 copy-start.1
  53.9 44.2 %all-to-all-start = ((bf16[4,128,1408]{1,2,0:T(8,128)(2,1)}), bf16[4,128,1408]{1,2,0:T(8,128)(2,1)}, u32[]{:S(2)}, u32[]{:S(2)}) async-start(bf16[4,128,1408]{1,2,0:T(8,128)(2,1)} %pad_maximum_fusion.1), calls=%async_computation | async-start | bytes 2883584 | tf_op jit(solution)/shard_map/all_to_all | solution.py:94
  106.9 10.0 %collective-permute-start.4 = (f32[8,16,1536]{2,1,0:T(8,128)}, f32[8,16,1536]{2,1,0:T(8,128)}, u32[]{:S(2)}, u32[]{:S(2)}) collective-permute-start(f32[8,16,1536]{2,1,0:T(8,128)} %reshape.190), channel_id=1, source_target_pairs={{0,32},{32,0},{1,33},{33,1},{2,34},{34,2},{3,35},{35,3},{4,36},{36... | collective-permute-start | bytes 2359304 | tf_op jit(solution)/shard_map/ppermute | solution.py:107
  116.8 14.2 %copy-start.3 = (bf16[48,4,8,128]{3,2,1,0:T(8,128)(2,1)S(1)}, bf16[48,4,8,128]{3,2,1,0:T(8,128)(2,1)}, u32[]{:S(2)}) copy-start(bf16[48,4,8,128]{3,2,1,0:T(8,128)(2,1)} %get-tuple-element.22) | copy-start | bytes 1179652
  116.8 14.2 %copy-start.8 = (f32[128]{0:T(128)S(1)}, f32[128]{0:T(128)}, u32[]{:S(2)}) copy-start(f32[128]{0:T(128)} %get-tuple-element.15) | copy-start | bytes 1540
  119.2 35.5 %all-to-all-start.1 = ((f32[8,16,1536]{2,1,0:T(8,128)}), f32[8,16,1536]{2,1,0:T(8,128)}, u32[]{:S(2)}, u32[]{:S(2)}) async-start(f32[8,16,1536]{2,1,0:T(8,128)} %add.63), calls=%async_computation.1 | async-start | bytes 1572864 | tf_op jit(solution)/shard_map/all_to_all | solution.py:108
  133.3 44.3 %copy-start.2 = (bf16[128,1024]{0,1:T(8,128)(2,1)S(1)}, bf16[128,1024]{0,1:T(8,128)(2,1)}, u32[]{:S(2)}) copy-start(bf16[128,1024]{0,1:T(8,128)(2,1)} %copy-done.1) | copy-start | bytes 786436
  133.3 44.3 %copy-start.6 = (bf16[4,128,128]{2,1,0:T(8,128)(2,1)S(1)}, bf16[4,128,128]{2,1,0:T(8,128)(2,1)}, u32[]{:S(2)}) copy-start(bf16[4,128,128]{2,1,0:T(8,128)(2,1)} %copy-done.5) | copy-start | bytes 393220
  158.1 30.8 %all-to-all-start.2 = ((f32[16,1,1536]{2,1,0:T(1,128)}), f32[16,1,1536]{2,1,0:T(1,128)}, u32[]{:S(2)}, u32[]{:S(2)}) async-start(f32[16,1,1536]{2,1,0:T(1,128)} %all_to_all.14), calls=%async_computation.2 | async-start | bytes 196608 | tf_op jit(solution)/shard_map/all_to_all | solution.py:109

commit v13 on v11

--- a/solution.py
+++ b/solution.py
@@ -90,10 +90,10 @@
     col_factor = grad_all.reshape(frame_count, ring, group, block_cols).transpose(2, 0, 1, 3)
     col_factor = col_factor.reshape(group, frame_count, ring * block_cols)
     row_factor = jnp.broadcast_to(frame_rows[None], (group, frame_count, model_width))
-    sent = jnp.concatenate([row_factor, col_factor], axis=2)
-    got = lax.all_to_all(sent, "cy", 0, 0, tiled=True)
-    row_pieces = got[..., :model_width].reshape(group, frame_count, spread, pair, block_rows)
-    col_pieces = got[..., model_width:].reshape(group, frame_count, ring, block_cols)
+    got_rows = lax.all_to_all(row_factor, "cy", 0, 0, tiled=True)
+    got_cols = lax.all_to_all(col_factor, "cy", 0, 0, tiled=True)
+    row_pieces = got_rows.reshape(group, frame_count, spread, pair, block_rows)
+    col_pieces = got_cols.reshape(group, frame_count, ring, block_cols)
     halves = [
         jnp.einsum(
             "sfna,sfxb->xnab", row_pieces[:, :, :, h], col_pieces, preferred_element_type=jnp.float32

time: 188 us -> 168 us (0.89)
  waiting for transfers between devices: 65.7 us -> 35.9 us
  starting transfers between devices: 57.5 us -> 62.7 us
  local copies, waits for them, and re-layouts: 23.5 us -> 27.8 us
    all_to_all x1 -> x2, waiting for transfers between devices: 33.8 us -> 5.47 us  [the longest x1 5.47 us: weight_gradient(): got_cols = lax.all_to_all(col_factor, 'cy', 0, 0, tiled=True)]
    ppermute x1, starting transfers between devices: 3.36 us -> 15.2 us  [weight_gradient(): half = keep + lax.ppermute(send, 'cc', [(0, 1), (1, 0)])]
    all_to_all x1, starting transfers between devices: 11.7 us -> 4.21 us  [weight_gradient(): part = jnp.sum(lax.all_to_all(half, 'cx', 0, 0, tiled=True), axis=0)]
    all_to_all x1 -> x2, starting transfers between devices: 10.4 us -> 13.7 us  [the longest x1 6.98 us: weight_gradient(): got_rows = lax.all_to_all(row_factor, 'cy', 0, 0, tiled=True)]
    slice x2 -> x0, local copies, waits for them, and re-layouts: 2.33 us -> none  [the longest x1 1.3 us: weight_gradient(): got[..., :model_width].reshape(group, frame_count, spread, pair, block_rows)]
    slice x1, local copies, waits for them, and re-layouts: 0.07 us -> 2.31 us  [weight_gradient(): row_pieces[:, :, :, h]]
    broadcast_in_dim x1, local copies, waits for them, and re-layouts: 0.14 us -> 2.11 us  [weight_gradient(): jnp.broadcast_to(frame_rows[None], (group, frame_count, model_width))]
    unnamed x13 -> x19, local copies, waits for them, and re-layouts: 3.57 us -> 4.28 us
  transfers between devices with their start and end apart: 8 -> 9, of which waited for: 5 -> 4; matrix products, arithmetic and copies ran while one was open for 11% -> 28% of each run, Pallas kernels for 0% -> 0%
where the time goes in v13:
time: 168 us; the launch traced here: 167 us
  starting transfers between devices  62.7 us (37%)
  waiting for transfers between devices  35.9 us (21%)
  local copies, waits for them, and re-layouts  27.8 us (17%)
  matrix products  27.5 us (16%)
  other arithmetic  11.5 us (7%)
    all_to_all x1, waiting for transfers between devices, weight_gradient(): part = jnp.sum(lax.all_to_all(half, 'cx', 0, 0, tiled=True), axis=0)  19.4 us
    all_to_all x1, starting transfers between devices, weight_gradient(): summed = jnp.sum(lax.all_to_all(part, CALLS[:2], 0, 0, tiled=True), axis=0)  18.2 us
    ppermute x1, starting transfers between devices, weight_gradient(): half = keep + lax.ppermute(send, 'cc', [(0, 1), (1, 0)])  15.2 us
    all_to_all x1, waiting for transfers between devices, weight_gradient(): summed = jnp.sum(lax.all_to_all(part, CALLS[:2], 0, 0, tiled=True), axis=0)  9.48 us
    ppermute x2, starting transfers between devices, with_halo(): lax.ppermute(tail, axis, [(i, (i + 1) % count) for i in range(ends)])  8.85 us
    all_to_all x1, starting transfers between devices, weight_gradient(): got_rows = lax.all_to_all(row_factor, 'cy', 0, 0, tiled=True)  6.98 us
    all_to_all x1, starting transfers between devices, weight_gradient(): got_cols = lax.all_to_all(col_factor, 'cy', 0, 0, tiled=True)  6.69 us
    all_to_all x1, waiting for transfers between devices, weight_gradient(): got_cols = lax.all_to_all(col_factor, 'cy', 0, 0, tiled=True)  5.47 us
  transfers between devices with their start and end apart: 9, of which 4 were waited for; matrix products, arithmetic and copies ran while one was open for 28% of the time, Pallas kernels for 0%

profile of v13, /device:TPU:1, one launch (start us, length us, event | category | flops | bytes accessed | tf_op | source)
XLA Modules:
  0.0 166.8 jit_solution(18154929095364796870)
XLA Ops:
  0.6 1.9 %copy-done = bf16[1024,1536]{1,0:T(8,128)(2,1)S(1)} copy-done((bf16[1024,1536]{1,0:T(8,128)(2,1)S(1)}, bf16[1024,1536]{1,0:T(8,128)(2,1)}, u32[]{:S(2)}) %copy-start) | copy-done | bytes 3145752
  6.1 5.5 %collective-permute-start = (bf16[128,1024]{1,0:T(8,128)(2,1)}, bf16[128,1024]{1,0:T(8,128)(2,1)}, u32[]{:S(2)}, u32[]{:S(2)}) collective-permute-start(bf16[128,1024]{1,0:T(8,128)(2,1)} %slice.40), channel_id=1, source_target_pairs={{0,1},{1,2},{2,3},{3,4},{4,5},{5,6},{6,7},{7,8},{8,9},{9,10},{10,1... | collective-permute-start | bytes 786440 | tf_op jit(solution)/shard_map/ppermute | solution.py:22
  13.4 2.1 %broadcast_in_dim.31 = bf16[4,128,1024]{1,2,0:T(8,128)(2,1)} broadcast(bf16[128,1024]{0,1:T(8,128)(2,1)} %copy.54), dimensions={1,2} | broadcast | bytes 1310720 | tf_op jit(solution)/shard_map/broadcast_in_dim | solution.py:92
  15.5 7.0 %all-to-all-start.1 = ((bf16[4,128,1024]{1,2,0:T(8,128)(2,1)}), bf16[4,128,1024]{1,2,0:T(8,128)(2,1)}, u32[]{:S(2)}, u32[]{:S(2)}) async-start(bf16[4,128,1024]{1,2,0:T(8,128)(2,1)} %broadcast_in_dim.31), calls=%async_computation.1 | async-start | bytes 2097152 | tf_op jit(solution)/shard_map/all_to_all | solution.py:93
  32.5 2.3 %fusion.26 = f32[4,128,384]{2,1,0:T(8,128)} fusion(bf16[48,4,8,128]{3,2,1,0:T(8,128)(2,1)} %get-tuple-element.24, bf16[128,4,128]{0,2,1:T(8,128)(2,1)} %bitcast.88, pred[128]{0:T(512)(128)(4,1)S(1)} %get-tuple-element.16), kind=kOutput, calls=%fused_computation.38 | convolution fusion | flops 50397184 | bytes 1310848 | tf_op jit(solution)/shard_map/fhd,shd->hfs/dot_general | solution.py:60
  34.8 2.3 %fusion.58 = (f32[4,128]{1,0:T(4,128)S(1)}, f32[4,128,384]{2,1,0:T(8,128)}) fusion(bf16[128,4,128]{0,2,1:T(8,128)(2,1)} %bitcast.96, bf16[384,4,128]{0,2,1:T(8,128)(2,1)} %bitcast.92, pred[128,384]{1,0:T(8,128)(4,1)} %fusion.39), kind=kOutput, calls=%fused_computation.78 | convolution fusion | flops 51118464 | bytes 1361920 | tf_op jit(solution)/shard_map/sub | solution.py:52
  37.1 5.4 %fusion.14 = f32[4,128,384]{2,1,0:T(8,128)} fusion(bf16[128,4,128]{0,2,1:T(8,128)(2,1)S(1)} %bitcast.98, f32[4,128,384]{2,1,0:T(8,128)} %fusion.26, f32[4,128,384]{2,1,0:T(8,128)} %get-tuple-element.26, f32[4,128]{1,0:T(4,128)S(1)} %get-tuple-element.25), kind=kOutput, calls=%fused_computation.24 | convolution fusion | flops 51708800 | bytes 2492416 | tf_op jit(solution)/shard_map/hfs,fhd->shd/dot_general | solution.py:68
  42.5 2.5 %fusion.34 = f32[4,128,384]{2,1,0:T(8,128)} fusion(bf16[128,4,128]{0,2,1:T(8,128)(2,1)S(1)} %bitcast.89, pred[128]{0:T(512)(128)(4,1)S(1)} %get-tuple-element.16, f32[4,128]{1,0:T(4,128)S(1)} %get-tuple-element.25, bf16[128,4,128]{0,2,1:T(8,128)(2,1)S(1)} %bitcast.99, bf16[384,4,128]{0,2,1:T(8,128)(2,1)} %bitcast.93, pred[128,384]{1,0:T(8,128)(4,1)} %fusion.39), kind=kOutput, calls=%fused_computation.49 | convolution fusion | flops 101712768 | bytes 1493120 | tf_op jit(solution)/shard_map/hfs,fhd->shd/dot_general | solution.py:71
  47.3 3.4 %collective-permute-start.2 = (bf16[128,1024]{0,1:T(8,128)(2,1)}, bf16[128,1024]{0,1:T(8,128)(2,1)S(1)}, u32[]{:S(2)}, u32[]{:S(2)}) collective-permute-start(bf16[128,1024]{0,1:T(8,128)(2,1)} %get-tuple-element.21), channel_id=1, source_target_pairs={{0,1},{1,2},{2,3},{3,4},{4,5},{5,6},{6,7},{7,8},{8,9},{9,10},{10,1... | collective-permute-start | bytes 786440 | tf_op jit(solution)/shard_map/ppermute | solution.py:22
  51.9 4.5 %convolution_convert_fusion.2 = bf16[4,128,128]{2,1,0:T(8,128)(2,1)S(1)} fusion(bf16[384,4,128]{0,2,1:T(8,128)(2,1)} %bitcast.94, f32[4,128,384]{2,1,0:T(8,128)} %fusion.26, f32[4,128,384]{2,1,0:T(8,128)} %get-tuple-element.26, f32[4,128]{1,0:T(4,128)S(1)} %get-tuple-element.25), kind=kOutput, calls=%fused_computation.23 | convolution fusion | flops 51774336 | bytes 2099200 | tf_op jit(solution)/shard_map/hfs,shd->fhd/dot_general | solution.py:65
  60.8 6.7 %all-to-all-start = ((bf16[4,128,384]{1,2,0:T(8,128)(2,1)}), bf16[4,128,384]{1,2,0:T(8,128)(2,1)S(1)}, u32[]{:S(2)}, u32[]{:S(2)}) async-start(bf16[4,128,384]{1,2,0:T(8,128)(2,1)} %bitcast.85), calls=%async_computation | async-start | bytes 786432 | tf_op jit(solution)/shard_map/all_to_all | solution.py:94
  67.5 2.3 %fusion.55 = (bf16[4,128,16,1,32]{1,4,3,2,0:T(8,128)(2,1)}, bf16[4,128,16,1,32]{1,4,3,2,0:T(8,128)(2,1)}) fusion(bf16[4,128,16,2,32]{1,4,3,2,0:T(8,128)(2,1)} %bitcast.17), kind=kLoop, calls=%fused_computation.75 | loop fusion | bytes 2097152 | tf_op jit(solution)/shard_map/slice | solution.py:99
  69.8 5.5 %all-to-all-done = bf16[4,128,384]{1,2,0:T(8,128)(2,1)S(1)} async-done(((bf16[4,128,384]{1,2,0:T(8,128)(2,1)}), bf16[4,128,384]{1,2,0:T(8,128)(2,1)S(1)}, u32[]{:S(2)}, u32[]{:S(2)}) %all-to-all-start) | async-done | bytes 393248 | tf_op jit(solution)/shard_map/all_to_all | solution.py:94
  77.1 2.7 %fusion.3 = (f32[8,16,32,48]{3,2,1,0:T(8,128)}, f32[8,16,32,48]{3,2,1,0:T(8,128)}) fusion(f32[8,48,16,32,1]{1,3,4,2,0:T(8,128)S(1)} %fusion.23, pred[]{:T(512)S(6)} %eq.18, bf16[4,128,16,1,32]{1,4,3,2,0:T(8,128)(2,1)S(1)} %copy-done.3, bf16[4,128,8,48,1]{1,3,2,0,4:T(8,128)(2,1)S(1)} %bitcast.80), kind=kOutput, calls=%fused_computation.6 | convolution fusion | flops 201719808 | bytes 3276801 | tf_op jit(solution)/shard_map/sfna,sfxb->xnab/dot_general | solution.py:98
  79.8 3.5 %select_n.41 = f32[8,16,1536]{2,1,0:T(8,128)} reshape(f32[8,16,32,48]{3,2,1,0:T(8,128)} %get-tuple-element.17) | data formatting | bytes 1572864 | tf_op jit(solution)/shard_map/jit(_where)/select_n | solution.py:105
  83.3 15.2 %collective-permute-start.4 = (f32[8,16,1536]{2,1,0:T(8,128)}, f32[8,16,1536]{2,1,0:T(8,128)}, u32[]{:S(2)}, u32[]{:S(2)}) collective-permute-start(f32[8,16,1536]{2,1,0:T(8,128)} %select_n.41), channel_id=1, source_target_pairs={{0,32},{32,0},{1,33},{33,1},{2,34},{34,2},{3,35},{35,3},{4,36},{36... | collective-permute-start | bytes 2359304 | tf_op jit(solution)/shard_map/ppermute | solution.py:106
  98.4 3.5 %select_n.38 = f32[8,16,1536]{2,1,0:T(8,128)} reshape(f32[8,16,32,48]{3,2,1,0:T(8,128)} %get-tuple-element.18) | data formatting | bytes 1572864 | tf_op jit(solution)/shard_map/jit(_where)/select_n | solution.py:104
  102.0 2.3 %add.53 = f32[8,16,1536]{2,1,0:T(8,128)} add(f32[8,16,1536]{2,1,0:T(8,128)} %select_n.38, f32[8,16,1536]{2,1,0:T(8,128)} %collective-permute-done.4) | non-fusion elementwise | flops 196608 | bytes 2359296 | tf_op jit(solution)/shard_map/add | solution.py:106
  104.3 4.2 %all-to-all-start.2 = ((f32[8,16,1536]{2,1,0:T(8,128)}), f32[8,16,1536]{2,1,0:T(8,128)}, u32[]{:S(2)}, u32[]{:S(2)}) async-start(f32[8,16,1536]{2,1,0:T(8,128)} %add.53), calls=%async_computation.2 | async-start | bytes 1572864 | tf_op jit(solution)/shard_map/all_to_all | solution.py:107
  108.5 2.6 %fusion.13 = bf16[4,128,128]{2,1,0:T(8,128)(2,1)} fusion(bf16[48,4,8,128]{3,2,1,0:T(8,128)(2,1)} %get-tuple-element.24, f32[128]{0:T(128)S(1)} %copy-done.8, f32[4,128]{1,0:T(4,128)S(1)} %get-tuple-element.25, bf16[128,4,128]{0,2,1:T(8,128)(2,1)} %bitcast.97, bf16[384,4,128]{0,2,1:T(8,128)(2,1)} %bitcast.95, pred[128,384]{1,0:T(8,128)(4,1)} %fusion.39), kind=kOutput, calls=%fused_computation.22 | convolution fusion | flops 101778304 | bytes 1100288 | tf_op jit(solution)/shard_map/hfs,shd->fhd/dot_general | solution.py:56
  112.8 19.4 %all-to-all-done.2 = f32[8,16,1536]{2,1,0:T(8,128)} async-done(((f32[8,16,1536]{2,1,0:T(8,128)}), f32[8,16,1536]{2,1,0:T(8,128)}, u32[]{:S(2)}, u32[]{:S(2)}) %all-to-all-start.2) | async-done | bytes 786464 | tf_op jit(solution)/shard_map/all_to_all | solution.py:107
  135.6 18.2 %all-to-all-start.3 = ((f32[16,1,1536]{2,1,0:T(1,128)}), f32[16,1,1536]{2,1,0:T(1,128)}, u32[]{:S(2)}, u32[]{:S(2)}) async-start(f32[16,1,1536]{2,1,0:T(1,128)} %all_to_all.18), calls=%async_computation.3 | async-start | bytes 196608 | tf_op jit(solution)/shard_map/all_to_all | solution.py:108
  153.8 1.9 %fusion.12 = bf16[1,128,1024]{2,1,0:T(8,128)(2,1)} fusion(bf16[1024,1536]{1,0:T(8,128)(2,1)S(1)} %copy-done, bf16[128,1024]{0,1:T(8,128)(2,1)S(1)} %copy-done.2, bf16[128,512]{0,1:T(8,128)(2,1)S(1)} %bitcast.91), kind=kOutput, calls=%fused_computation.21 | convolution fusion | flops 403570688 | bytes 3801088 | tf_op jit(solution)/shard_map/dot_general | solution.py:140
  155.7 9.5 %all-to-all-done.3 = f32[16,1,1536]{2,1,0:T(1,128)} async-done(((f32[16,1,1536]{2,1,0:T(1,128)}), f32[16,1,1536]{2,1,0:T(1,128)}, u32[]{:S(2)}, u32[]{:S(2)}) %all-to-all-start.3) | async-done | bytes 98336 | tf_op jit(solution)/shard_map/all_to_all | solution.py:108
  (50 shorter events, 31.1 us)
Async XLA Ops:
  0.6 1.9 %copy-start = (bf16[1024,1536]{1,0:T(8,128)(2,1)S(1)}, bf16[1024,1536]{1,0:T(8,128)(2,1)}, u32[]{:S(2)}) copy-start(bf16[1024,1536]{1,0:T(8,128)(2,1)} %param.5) | copy-start | bytes 9437188
  4.8 24.8 %collective-permute-start.1 = (bf16[128,1024]{1,0:T(8,128)(2,1)}, bf16[128,1024]{1,0:T(8,128)(2,1)}, u32[]{:S(2)}, u32[]{:S(2)}) collective-permute-start(bf16[128,1024]{1,0:T(8,128)(2,1)} %slice.40), channel_id=1, source_target_pairs={{1,0},{2,1},{3,2},{4,3},{5,4},{6,5},{7,6},{8,7},{9,8},{10,9},{11,1... | collective-permute-start | bytes 786440 | tf_op jit(solution)/shard_map/ppermute | solution.py:24
  6.1 23.5 %collective-permute-start = (bf16[128,1024]{1,0:T(8,128)(2,1)}, bf16[128,1024]{1,0:T(8,128)(2,1)}, u32[]{:S(2)}, u32[]{:S(2)}) collective-permute-start(bf16[128,1024]{1,0:T(8,128)(2,1)} %slice.40), channel_id=1, source_target_pairs={{0,1},{1,2},{2,3},{3,4},{4,5},{5,6},{6,7},{7,8},{8,9},{9,10},{10,1... | collective-permute-start | bytes 786440 | tf_op jit(solution)/shard_map/ppermute | solution.py:22
  15.5 45.3 %all-to-all-start.1 = ((bf16[4,128,1024]{1,2,0:T(8,128)(2,1)}), bf16[4,128,1024]{1,2,0:T(8,128)(2,1)}, u32[]{:S(2)}, u32[]{:S(2)}) async-start(bf16[4,128,1024]{1,2,0:T(8,128)(2,1)} %broadcast_in_dim.31), calls=%async_computation.1 | async-start | bytes 2097152 | tf_op jit(solution)/shard_map/all_to_all | solution.py:93
  32.5 4.6 %copy-start.7 = (bf16[128,512]{0,1:T(8,128)(2,1)S(1)}, bf16[128,512]{0,1:T(8,128)(2,1)}, u32[]{:S(2)}) copy-start(bf16[128,512]{0,1:T(8,128)(2,1)} %copy.72) | copy-start | bytes 393220
  37.1 5.4 %copy-start.4 = (bf16[1,128,512]{1,2,0:T(8,128)(2,1)S(1)}, bf16[1,128,512]{1,2,0:T(8,128)(2,1)}, u32[]{:S(2)}) copy-start(bf16[1,128,512]{1,2,0:T(8,128)(2,1)} %copy.65) | copy-start | bytes 393220
  47.3 9.2 %collective-permute-start.2 = (bf16[128,1024]{0,1:T(8,128)(2,1)}, bf16[128,1024]{0,1:T(8,128)(2,1)S(1)}, u32[]{:S(2)}, u32[]{:S(2)}) collective-permute-start(bf16[128,1024]{0,1:T(8,128)(2,1)} %get-tuple-element.21), channel_id=1, source_target_pairs={{0,1},{1,2},{2,3},{3,4},{4,5},{5,6},{6,7},{7,8},{8,9},{9,10},{10,1... | collective-permute-start | bytes 786440 | tf_op jit(solution)/shard_map/ppermute | solution.py:22
  50.6 7.4 %collective-permute-start.3 = (bf16[128,1024]{0,1:T(8,128)(2,1)}, bf16[128,1024]{0,1:T(8,128)(2,1)}, u32[]{:S(2)}, u32[]{:S(2)}) collective-permute-start(bf16[128,1024]{0,1:T(8,128)(2,1)} %get-tuple-element.22), channel_id=1, source_target_pairs={{1,0},{2,1},{3,2},{4,3},{5,4},{6,5},{7,6},{8,7},{9,8},{10,9},{11,1... | collective-permute-start | bytes 786440 | tf_op jit(solution)/shard_map/ppermute | solution.py:24
  56.5 4.3 %copy-start.5 = (bf16[4,128,128]{2,1,0:T(8,128)(2,1)}, bf16[4,128,128]{2,1,0:T(8,128)(2,1)S(1)}, u32[]{:S(2)}) copy-start(bf16[4,128,128]{2,1,0:T(8,128)(2,1)S(1)} %convolution_convert_fusion.2) | copy-start | bytes 393220
  59.3 0.7 copy-start.1
  60.8 14.5 %all-to-all-start = ((bf16[4,128,384]{1,2,0:T(8,128)(2,1)}), bf16[4,128,384]{1,2,0:T(8,128)(2,1)S(1)}, u32[]{:S(2)}, u32[]{:S(2)}) async-start(bf16[4,128,384]{1,2,0:T(8,128)(2,1)} %bitcast.85), calls=%async_computation | async-start | bytes 786432 | tf_op jit(solution)/shard_map/all_to_all | solution.py:94
  75.2 1.8 %copy-start.3 = (bf16[4,128,16,1,32]{1,4,3,2,0:T(8,128)(2,1)S(1)}, bf16[4,128,16,1,32]{1,4,3,2,0:T(8,128)(2,1)}, u32[]{:S(2)}) copy-start(bf16[4,128,16,1,32]{1,4,3,2,0:T(8,128)(2,1)} %get-tuple-element.19) | copy-start | bytes 1572868
  83.3 18.7 %collective-permute-start.4 = (f32[8,16,1536]{2,1,0:T(8,128)}, f32[8,16,1536]{2,1,0:T(8,128)}, u32[]{:S(2)}, u32[]{:S(2)}) collective-permute-start(f32[8,16,1536]{2,1,0:T(8,128)} %select_n.41), channel_id=1, source_target_pairs={{0,32},{32,0},{1,33},{33,1},{2,34},{34,2},{3,35},{35,3},{4,36},{36... | collective-permute-start | bytes 2359304 | tf_op jit(solution)/shard_map/ppermute | solution.py:106
  102.0 6.6 %copy-start.8 = (f32[128]{0:T(128)S(1)}, f32[128]{0:T(128)}, u32[]{:S(2)}) copy-start(f32[128]{0:T(128)} %get-tuple-element.15) | copy-start | bytes 1540
  104.3 27.9 %all-to-all-start.2 = ((f32[8,16,1536]{2,1,0:T(8,128)}), f32[8,16,1536]{2,1,0:T(8,128)}, u32[]{:S(2)}, u32[]{:S(2)}) async-start(f32[8,16,1536]{2,1,0:T(8,128)} %add.53), calls=%async_computation.2 | async-start | bytes 1572864 | tf_op jit(solution)/shard_map/all_to_all | solution.py:107
  108.5 45.3 %copy-start.2 = (bf16[128,1024]{0,1:T(8,128)(2,1)S(1)}, bf16[128,1024]{0,1:T(8,128)(2,1)}, u32[]{:S(2)}) copy-start(bf16[128,1024]{0,1:T(8,128)(2,1)} %copy-done.1) | copy-start | bytes 786436
  108.5 45.3 %copy-start.6 = (bf16[4,128,128]{2,1,0:T(8,128)(2,1)S(1)}, bf16[4,128,128]{2,1,0:T(8,128)(2,1)}, u32[]{:S(2)}) copy-start(bf16[4,128,128]{2,1,0:T(8,128)(2,1)} %copy-done.5) | copy-start | bytes 393220
  135.6 29.6 %all-to-all-start.3 = ((f32[16,1,1536]{2,1,0:T(1,128)}), f32[16,1,1536]{2,1,0:T(1,128)}, u32[]{:S(2)}, u32[]{:S(2)}) async-start(f32[16,1,1536]{2,1,0:T(1,128)} %all_to_all.18), calls=%async_computation.3 | async-start | bytes 196608 | tf_op jit(solution)/shard_map/all_to_all | solution.py:108

commit v14 on v13

--- a/solution.py
+++ b/solution.py
@@ -89,20 +89,20 @@
     block_cols = grad_width // ctx
     col_factor = grad_all.reshape(frame_count, ring, group, block_cols).transpose(2, 0, 1, 3)
     col_factor = col_factor.reshape(group, frame_count, ring * block_cols)
-    row_factor = jnp.broadcast_to(frame_rows[None], (group, frame_count, model_width))
+    core = lax.axis_index("cc")
+    own_rows = frame_rows.reshape(frame_count, spread, pair, block_rows)
+    own_rows = jnp.where(core == 0, own_rows, own_rows[:, :, ::-1])
+    row_factor = jnp.broadcast_to(own_rows.reshape(1, frame_count, -1), (group, frame_count, model_width))
     got_rows = lax.all_to_all(row_factor, "cy", 0, 0, tiled=True)
     got_cols = lax.all_to_all(col_factor, "cy", 0, 0, tiled=True)
     row_pieces = got_rows.reshape(group, frame_count, spread, pair, block_rows)
     col_pieces = got_cols.reshape(group, frame_count, ring, block_cols)
-    halves = [
+    keep, send = [
         jnp.einsum(
             "sfna,sfxb->xnab", row_pieces[:, :, :, h], col_pieces, preferred_element_type=jnp.float32
         ).reshape(ring, spread, block_rows * block_cols)
         for h in range(pair)
     ]
-    core = lax.axis_index("cc")
-    keep = jnp.where(core == 0, halves[0], halves[1])
-    send = jnp.where(core == 0, halves[1], halves[0])
     half = keep + lax.ppermute(send, "cc", [(0, 1), (1, 0)])
     part = jnp.sum(lax.all_to_all(half, "cx", 0, 0, tiled=True), axis=0)
     summed = jnp.sum(lax.all_to_all(part, CALLS[:2], 0, 0, tiled=True), axis=0)

time: 168 us -> 170 us (1.012)
    select_n x2 -> x0, local copies, waits for them, and re-layouts: 7.01 us -> none  [the longest x1 3.51 us: weight_gradient(): send = jnp.where(core == 0, halves[1], halves[0])]
    reshape x0 -> x2, local copies, waits for them, and re-layouts: none -> 6.98 us  [weight_gradient(): keep, send = [jnp.einsum('sfna,sfxb->xnab', row_pieces[:, :, :, h], col_p...]
    squeeze x1 -> x0, local copies, waits for them, and re-layouts: 1.79 us -> none  [body(): frame_rows = frames_in[0]]
    unnamed x19 -> x18, local copies, waits for them, and re-layouts: 4.28 us -> 6.05 us
  transfers between devices with their start and end apart: 9 -> 9, of which waited for: 4 -> 4; matrix products, arithmetic and copies ran while one was open for 28% -> 29% of each run, Pallas kernels for 0% -> 0%
where the time goes in v14:
time: 170 us; the launch traced here: 169 us
  starting transfers between devices  62.7 us (37%)
  waiting for transfers between devices  35.9 us (21%)
  matrix products  29.2 us (17%)
  local copies, waits for them, and re-layouts  26.8 us (16%)
  other arithmetic  12.5 us (7%)
    all_to_all x1, waiting for transfers between devices, weight_gradient(): part = jnp.sum(lax.all_to_all(half, 'cx', 0, 0, tiled=True), axis=0)  19.4 us
    all_to_all x1, starting transfers between devices, weight_gradient(): summed = jnp.sum(lax.all_to_all(part, CALLS[:2], 0, 0, tiled=True), axis=0)  18.3 us
    ppermute x1, starting transfers between devices, weight_gradient(): half = keep + lax.ppermute(send, 'cc', [(0, 1), (1, 0)])  15.2 us
    all_to_all x1, waiting for transfers between devices, weight_gradient(): summed = jnp.sum(lax.all_to_all(part, CALLS[:2], 0, 0, tiled=True), axis=0)  9.48 us
    ppermute x2, starting transfers between devices, with_halo(): lax.ppermute(tail, axis, [(i, (i + 1) % count) for i in range(ends)])  8.85 us
    all_to_all x1, starting transfers between devices, weight_gradient(): got_rows = lax.all_to_all(row_factor, 'cy', 0, 0, tiled=True)  6.98 us
    reshape x2, local copies, waits for them, and re-layouts, weight_gradient(): keep, send = [jnp.einsum('sfna,sfxb->xnab', row_pieces[:, :, :, h], col_p...  6.98 us
    all_to_all x1, starting transfers between devices, weight_gradient(): got_cols = lax.all_to_all(col_factor, 'cy', 0, 0, tiled=True)  6.69 us
  transfers between devices with their start and end apart: 9, of which 4 were waited for; matrix products, arithmetic and copies ran while one was open for 29% of the time, Pallas kernels for 0%

profile of v14, /device:TPU:1, one launch (start us, length us, event | category | flops | bytes accessed | tf_op | source)
XLA Modules:
  0.0 168.6 jit_solution(14695750723151251484)
XLA Ops:
  0.6 1.9 %copy-done = bf16[1024,1536]{1,0:T(8,128)(2,1)S(1)} copy-done((bf16[1024,1536]{1,0:T(8,128)(2,1)S(1)}, bf16[1024,1536]{1,0:T(8,128)(2,1)}, u32[]{:S(2)}) %copy-start) | copy-done | bytes 3145752
  6.1 5.5 %collective-permute-start = (bf16[128,1024]{1,0:T(8,128)(2,1)}, bf16[128,1024]{1,0:T(8,128)(2,1)}, u32[]{:S(2)}, u32[]{:S(2)}) collective-permute-start(bf16[128,1024]{1,0:T(8,128)(2,1)} %slice.40), channel_id=1, source_target_pairs={{0,1},{1,2},{2,3},{3,4},{4,5},{5,6},{6,7},{7,8},{8,9},{9,10},{10,1... | collective-permute-start | bytes 786440 | tf_op jit(solution)/shard_map/ppermute | solution.py:22
  15.6 7.0 %all-to-all-start.1 = ((bf16[4,128,1024]{1,2,0:T(8,128)(2,1)}), bf16[4,128,1024]{1,2,0:T(8,128)(2,1)}, u32[]{:S(2)}, u32[]{:S(2)}) async-start(bf16[4,128,1024]{1,2,0:T(8,128)(2,1)} %broadcast_in_dim.52), calls=%async_computation.1 | async-start | bytes 2097152 | tf_op jit(solution)/shard_map/all_to_all | solution.py:96
  32.6 2.3 %fusion.22 = f32[4,128,384]{2,1,0:T(8,128)} fusion(bf16[48,4,8,128]{3,2,1,0:T(8,128)(2,1)} %get-tuple-element.22, bf16[128,4,128]{0,2,1:T(8,128)(2,1)} %bitcast.83, pred[128]{0:T(512)(128)(4,1)S(1)} %get-tuple-element.16), kind=kOutput, calls=%fused_computation.34 | convolution fusion | flops 50397184 | bytes 1310848 | tf_op jit(solution)/shard_map/fhd,shd->hfs/dot_general | solution.py:60
  34.9 2.3 %fusion.54 = (f32[4,128]{1,0:T(4,128)S(1)}, f32[4,128,384]{2,1,0:T(8,128)}) fusion(bf16[128,4,128]{0,2,1:T(8,128)(2,1)} %bitcast.91, bf16[384,4,128]{0,2,1:T(8,128)(2,1)} %bitcast.87, pred[128,384]{1,0:T(8,128)(4,1)} %fusion.36), kind=kOutput, calls=%fused_computation.75 | convolution fusion | flops 51118464 | bytes 1361920 | tf_op jit(solution)/shard_map/sub | solution.py:52
  37.3 5.4 %fusion.12 = f32[4,128,384]{2,1,0:T(8,128)} fusion(bf16[128,4,128]{0,2,1:T(8,128)(2,1)S(1)} %bitcast.93, f32[4,128,384]{2,1,0:T(8,128)} %fusion.22, f32[4,128,384]{2,1,0:T(8,128)} %get-tuple-element.24, f32[4,128]{1,0:T(4,128)S(1)} %get-tuple-element.23), kind=kOutput, calls=%fused_computation.22 | convolution fusion | flops 51708800 | bytes 2492416 | tf_op jit(solution)/shard_map/hfs,fhd->shd/dot_general | solution.py:68
  42.7 2.5 %fusion.31 = f32[4,128,384]{2,1,0:T(8,128)} fusion(bf16[128,4,128]{0,2,1:T(8,128)(2,1)S(1)} %bitcast.84, pred[128]{0:T(512)(128)(4,1)S(1)} %get-tuple-element.16, f32[4,128]{1,0:T(4,128)S(1)} %get-tuple-element.23, bf16[128,4,128]{0,2,1:T(8,128)(2,1)S(1)} %bitcast.94, bf16[384,4,128]{0,2,1:T(8,128)(2,1)} %bitcast.88, pred[128,384]{1,0:T(8,128)(4,1)} %fusion.36), kind=kOutput, calls=%fused_computation.47 | convolution fusion | flops 101712768 | bytes 1493120 | tf_op jit(solution)/shard_map/hfs,fhd->shd/dot_general | solution.py:71
  47.4 3.4 %collective-permute-start.2 = (bf16[128,1024]{0,1:T(8,128)(2,1)}, bf16[128,1024]{0,1:T(8,128)(2,1)S(1)}, u32[]{:S(2)}, u32[]{:S(2)}) collective-permute-start(bf16[128,1024]{0,1:T(8,128)(2,1)} %get-tuple-element.19), channel_id=1, source_target_pairs={{0,1},{1,2},{2,3},{3,4},{4,5},{5,6},{6,7},{7,8},{8,9},{9,10},{10,1... | collective-permute-start | bytes 786440 | tf_op jit(solution)/shard_map/ppermute | solution.py:22
  52.1 4.5 %convolution_convert_fusion.2 = bf16[4,128,128]{2,1,0:T(8,128)(2,1)S(1)} fusion(bf16[384,4,128]{0,2,1:T(8,128)(2,1)} %bitcast.89, f32[4,128,384]{2,1,0:T(8,128)} %fusion.22, f32[4,128,384]{2,1,0:T(8,128)} %get-tuple-element.24, f32[4,128]{1,0:T(4,128)S(1)} %get-tuple-element.23), kind=kOutput, calls=%fused_computation.21 | convolution fusion | flops 51774336 | bytes 2099200 | tf_op jit(solution)/shard_map/hfs,shd->fhd/dot_general | solution.py:65
  61.0 6.7 %all-to-all-start = ((bf16[4,128,384]{1,2,0:T(8,128)(2,1)}), bf16[4,128,384]{1,2,0:T(8,128)(2,1)S(1)}, u32[]{:S(2)}, u32[]{:S(2)}) async-start(bf16[4,128,384]{1,2,0:T(8,128)(2,1)} %bitcast.79), calls=%async_computation | async-start | bytes 786432 | tf_op jit(solution)/shard_map/all_to_all | solution.py:97
  67.7 2.3 %fusion.51 = (bf16[4,128,16,1,32]{1,4,3,2,0:T(8,128)(2,1)}, bf16[4,128,16,1,32]{1,4,3,2,0:T(8,128)(2,1)}) fusion(bf16[4,128,16,2,32]{1,4,3,2,0:T(8,128)(2,1)} %bitcast.19), kind=kLoop, calls=%fused_computation.72 | loop fusion | bytes 2097152 | tf_op jit(solution)/shard_map/slice | solution.py:102
  69.9 5.5 %all-to-all-done = bf16[4,128,384]{1,2,0:T(8,128)(2,1)S(1)} async-done(((bf16[4,128,384]{1,2,0:T(8,128)(2,1)}), bf16[4,128,384]{1,2,0:T(8,128)(2,1)S(1)}, u32[]{:S(2)}, u32[]{:S(2)}) %all-to-all-start) | async-done | bytes 393248 | tf_op jit(solution)/shard_map/all_to_all | solution.py:97
  75.4 3.1 %convolution_bitcast_fusion = f32[8,16,32,48]{3,2,1,0:T(8,128)} fusion(bf16[4,128,16,1,32]{1,4,3,2,0:T(8,128)(2,1)} %get-tuple-element.17, bf16[4,128,8,48,1]{1,3,2,0,4:T(8,128)(2,1)S(1)} %bitcast.73), kind=kOutput, calls=%fused_computation.6 | convolution fusion | flops 201326592 | bytes 1703936 | tf_op jit(solution)/shard_map/sfna,sfxb->xnab/dot_general | solution.py:101
  78.5 3.5 %reshape.192 = f32[8,16,1536]{2,1,0:T(8,128)} reshape(f32[8,16,32,48]{3,2,1,0:T(8,128)} %convolution_bitcast_fusion) | data formatting | bytes 1572864 | tf_op jit(solution)/shard_map/reshape | solution.py:103
  82.0 15.2 %collective-permute-start.4 = (f32[8,16,1536]{2,1,0:T(8,128)}, f32[8,16,1536]{2,1,0:T(8,128)}, u32[]{:S(2)}, u32[]{:S(2)}) collective-permute-start(f32[8,16,1536]{2,1,0:T(8,128)} %reshape.192), channel_id=1, source_target_pairs={{0,32},{32,0},{1,33},{33,1},{2,34},{34,2},{3,35},{35,3},{4,36},{36... | collective-permute-start | bytes 2359304 | tf_op jit(solution)/shard_map/ppermute | solution.py:106
  97.2 3.1 %convolution_bitcast_fusion.1 = f32[8,16,32,48]{3,2,1,0:T(8,128)} fusion(bf16[4,128,16,1,32]{1,4,3,2,0:T(8,128)(2,1)} %get-tuple-element.18, bf16[4,128,8,48,1]{1,3,2,0,4:T(8,128)(2,1)S(1)} %bitcast.74), kind=kOutput, calls=%fused_computation.7 | convolution fusion | flops 201326592 | bytes 1703936 | tf_op jit(solution)/shard_map/sfna,sfxb->xnab/dot_general | solution.py:101
  100.3 3.5 %reshape.191 = f32[8,16,1536]{2,1,0:T(8,128)} reshape(f32[8,16,32,48]{3,2,1,0:T(8,128)} %convolution_bitcast_fusion.1) | data formatting | bytes 1572864 | tf_op jit(solution)/shard_map/reshape | solution.py:103
  103.8 2.3 %add.53 = f32[8,16,1536]{2,1,0:T(8,128)} add(f32[8,16,1536]{2,1,0:T(8,128)} %reshape.191, f32[8,16,1536]{2,1,0:T(8,128)} %collective-permute-done.4) | non-fusion elementwise | flops 196608 | bytes 2359296 | tf_op jit(solution)/shard_map/add | solution.py:106
  106.1 4.2 %all-to-all-start.2 = ((f32[8,16,1536]{2,1,0:T(8,128)}), f32[8,16,1536]{2,1,0:T(8,128)}, u32[]{:S(2)}, u32[]{:S(2)}) async-start(f32[8,16,1536]{2,1,0:T(8,128)} %add.53), calls=%async_computation.2 | async-start | bytes 1572864 | tf_op jit(solution)/shard_map/all_to_all | solution.py:107
  110.3 2.6 %fusion.11 = bf16[4,128,128]{2,1,0:T(8,128)(2,1)} fusion(bf16[48,4,8,128]{3,2,1,0:T(8,128)(2,1)} %get-tuple-element.22, f32[128]{0:T(128)S(1)} %copy-done.7, f32[4,128]{1,0:T(4,128)S(1)} %get-tuple-element.23, bf16[128,4,128]{0,2,1:T(8,128)(2,1)} %bitcast.92, bf16[384,4,128]{0,2,1:T(8,128)(2,1)} %bitcast.90, pred[128,384]{1,0:T(8,128)(4,1)} %fusion.36), kind=kOutput, calls=%fused_computation.20 | convolution fusion | flops 101778304 | bytes 1100288 | tf_op jit(solution)/shard_map/hfs,shd->fhd/dot_general | solution.py:56
  114.6 19.4 %all-to-all-done.2 = f32[8,16,1536]{2,1,0:T(8,128)} async-done(((f32[8,16,1536]{2,1,0:T(8,128)}), f32[8,16,1536]{2,1,0:T(8,128)}, u32[]{:S(2)}, u32[]{:S(2)}) %all-to-all-start.2) | async-done | bytes 786464 | tf_op jit(solution)/shard_map/all_to_all | solution.py:107
  137.4 18.3 %all-to-all-start.3 = ((f32[16,1,1536]{2,1,0:T(1,128)}), f32[16,1,1536]{2,1,0:T(1,128)}, u32[]{:S(2)}, u32[]{:S(2)}) async-start(f32[16,1,1536]{2,1,0:T(1,128)} %all_to_all.18), calls=%async_computation.3 | async-start | bytes 196608 | tf_op jit(solution)/shard_map/all_to_all | solution.py:108
  155.7 1.9 %fusion.10 = bf16[1,128,1024]{2,1,0:T(8,128)(2,1)} fusion(bf16[1024,1536]{1,0:T(8,128)(2,1)S(1)} %copy-done, bf16[128,1024]{0,1:T(8,128)(2,1)S(1)} %copy-done.2, bf16[128,512]{0,1:T(8,128)(2,1)S(1)} %bitcast.86), kind=kOutput, calls=%fused_computation.19 | convolution fusion | flops 403570688 | bytes 3801088 | tf_op jit(solution)/shard_map/dot_general | solution.py:140
  157.5 9.5 %all-to-all-done.3 = f32[16,1,1536]{2,1,0:T(1,128)} async-done(((f32[16,1,1536]{2,1,0:T(1,128)}), f32[16,1,1536]{2,1,0:T(1,128)}, u32[]{:S(2)}, u32[]{:S(2)}) %all-to-all-start.3) | async-done | bytes 98336 | tf_op jit(solution)/shard_map/all_to_all | solution.py:108
  (49 shorter events, 31.5 us)
Async XLA Ops:
  0.6 1.9 %copy-start = (bf16[1024,1536]{1,0:T(8,128)(2,1)S(1)}, bf16[1024,1536]{1,0:T(8,128)(2,1)}, u32[]{:S(2)}) copy-start(bf16[1024,1536]{1,0:T(8,128)(2,1)} %param.5) | copy-start | bytes 9437188
  4.8 24.9 %collective-permute-start.1 = (bf16[128,1024]{1,0:T(8,128)(2,1)}, bf16[128,1024]{1,0:T(8,128)(2,1)}, u32[]{:S(2)}, u32[]{:S(2)}) collective-permute-start(bf16[128,1024]{1,0:T(8,128)(2,1)} %slice.40), channel_id=1, source_target_pairs={{1,0},{2,1},{3,2},{4,3},{5,4},{6,5},{7,6},{8,7},{9,8},{10,9},{11,1... | collective-permute-start | bytes 786440 | tf_op jit(solution)/shard_map/ppermute | solution.py:24
  6.1 23.6 %collective-permute-start = (bf16[128,1024]{1,0:T(8,128)(2,1)}, bf16[128,1024]{1,0:T(8,128)(2,1)}, u32[]{:S(2)}, u32[]{:S(2)}) collective-permute-start(bf16[128,1024]{1,0:T(8,128)(2,1)} %slice.40), channel_id=1, source_target_pairs={{0,1},{1,2},{2,3},{3,4},{4,5},{5,6},{6,7},{7,8},{8,9},{9,10},{10,1... | collective-permute-start | bytes 786440 | tf_op jit(solution)/shard_map/ppermute | solution.py:22
  15.6 45.4 %all-to-all-start.1 = ((bf16[4,128,1024]{1,2,0:T(8,128)(2,1)}), bf16[4,128,1024]{1,2,0:T(8,128)(2,1)}, u32[]{:S(2)}, u32[]{:S(2)}) async-start(bf16[4,128,1024]{1,2,0:T(8,128)(2,1)} %broadcast_in_dim.52), calls=%async_computation.1 | async-start | bytes 2097152 | tf_op jit(solution)/shard_map/all_to_all | solution.py:96
  32.6 4.6 %copy-start.6 = (bf16[128,512]{0,1:T(8,128)(2,1)S(1)}, bf16[128,512]{0,1:T(8,128)(2,1)}, u32[]{:S(2)}) copy-start(bf16[128,512]{0,1:T(8,128)(2,1)} %copy.72) | copy-start | bytes 393220
  37.3 5.4 %copy-start.3 = (bf16[1,128,512]{1,2,0:T(8,128)(2,1)S(1)}, bf16[1,128,512]{1,2,0:T(8,128)(2,1)}, u32[]{:S(2)}) copy-start(bf16[1,128,512]{1,2,0:T(8,128)(2,1)} %copy.65) | copy-start | bytes 393220
  47.4 9.2 %collective-permute-start.2 = (bf16[128,1024]{0,1:T(8,128)(2,1)}, bf16[128,1024]{0,1:T(8,128)(2,1)S(1)}, u32[]{:S(2)}, u32[]{:S(2)}) collective-permute-start(bf16[128,1024]{0,1:T(8,128)(2,1)} %get-tuple-element.19), channel_id=1, source_target_pairs={{0,1},{1,2},{2,3},{3,4},{4,5},{5,6},{6,7},{7,8},{8,9},{9,10},{10,1... | collective-permute-start | bytes 786440 | tf_op jit(solution)/shard_map/ppermute | solution.py:22
  50.8 7.4 %collective-permute-start.3 = (bf16[128,1024]{0,1:T(8,128)(2,1)}, bf16[128,1024]{0,1:T(8,128)(2,1)}, u32[]{:S(2)}, u32[]{:S(2)}) collective-permute-start(bf16[128,1024]{0,1:T(8,128)(2,1)} %get-tuple-element.20), channel_id=1, source_target_pairs={{1,0},{2,1},{3,2},{4,3},{5,4},{6,5},{7,6},{8,7},{9,8},{10,9},{11,1... | collective-permute-start | bytes 786440 | tf_op jit(solution)/shard_map/ppermute | solution.py:24
  56.7 4.3 %copy-start.4 = (bf16[4,128,128]{2,1,0:T(8,128)(2,1)}, bf16[4,128,128]{2,1,0:T(8,128)(2,1)S(1)}, u32[]{:S(2)}) copy-start(bf16[4,128,128]{2,1,0:T(8,128)(2,1)S(1)} %convolution_convert_fusion.2) | copy-start | bytes 393220
  59.4 0.7 copy-start.1
  61.0 14.4 %all-to-all-start = ((bf16[4,128,384]{1,2,0:T(8,128)(2,1)}), bf16[4,128,384]{1,2,0:T(8,128)(2,1)S(1)}, u32[]{:S(2)}, u32[]{:S(2)}) async-start(bf16[4,128,384]{1,2,0:T(8,128)(2,1)} %bitcast.79), calls=%async_computation | async-start | bytes 786432 | tf_op jit(solution)/shard_map/all_to_all | solution.py:97
  82.0 21.8 %collective-permute-start.4 = (f32[8,16,1536]{2,1,0:T(8,128)}, f32[8,16,1536]{2,1,0:T(8,128)}, u32[]{:S(2)}, u32[]{:S(2)}) collective-permute-start(f32[8,16,1536]{2,1,0:T(8,128)} %reshape.192), channel_id=1, source_target_pairs={{0,32},{32,0},{1,33},{33,1},{2,34},{34,2},{3,35},{35,3},{4,36},{36... | collective-permute-start | bytes 2359304 | tf_op jit(solution)/shard_map/ppermute | solution.py:106
  103.8 6.6 %copy-start.7 = (f32[128]{0:T(128)S(1)}, f32[128]{0:T(128)}, u32[]{:S(2)}) copy-start(f32[128]{0:T(128)} %get-tuple-element.15) | copy-start | bytes 1540
  106.1 27.9 %all-to-all-start.2 = ((f32[8,16,1536]{2,1,0:T(8,128)}), f32[8,16,1536]{2,1,0:T(8,128)}, u32[]{:S(2)}, u32[]{:S(2)}) async-start(f32[8,16,1536]{2,1,0:T(8,128)} %add.53), calls=%async_computation.2 | async-start | bytes 1572864 | tf_op jit(solution)/shard_map/all_to_all | solution.py:107
  110.3 45.3 %copy-start.2 = (bf16[128,1024]{0,1:T(8,128)(2,1)S(1)}, bf16[128,1024]{0,1:T(8,128)(2,1)}, u32[]{:S(2)}) copy-start(bf16[128,1024]{0,1:T(8,128)(2,1)} %copy-done.1) | copy-start | bytes 786436
  110.3 45.3 %copy-start.5 = (bf16[4,128,128]{2,1,0:T(8,128)(2,1)S(1)}, bf16[4,128,128]{2,1,0:T(8,128)(2,1)}, u32[]{:S(2)}) copy-start(bf16[4,128,128]{2,1,0:T(8,128)(2,1)} %copy-done.4) | copy-start | bytes 393220
  137.4 29.6 %all-to-all-start.3 = ((f32[16,1,1536]{2,1,0:T(1,128)}), f32[16,1,1536]{2,1,0:T(1,128)}, u32[]{:S(2)}, u32[]{:S(2)}) async-start(f32[16,1,1536]{2,1,0:T(1,128)} %all_to_all.18), calls=%async_computation.3 | async-start | bytes 196608 | tf_op jit(solution)/shard_map/all_to_all | solution.py:108

commit v15 on v12

--- a/solution.py
+++ b/solution.py
@@ -90,10 +90,10 @@
     col_factor = grad_all.reshape(frame_count, ring, group, block_cols).transpose(2, 0, 1, 3)
     col_factor = col_factor.reshape(group, frame_count, ring * block_cols)
     row_factor = jnp.broadcast_to(frame_rows[None], (group, frame_count, model_width))
-    sent = jnp.concatenate([row_factor, col_factor], axis=2)
-    got = lax.all_to_all(sent, "cy", 0, 0, tiled=True)
-    row_pieces = got[..., :model_width].reshape(group, frame_count, spread, pair, block_rows)
-    col_pieces = got[..., model_width:].reshape(group, frame_count, ring, block_cols)
+    got_rows = lax.all_to_all(row_factor, "cy", 0, 0, tiled=True)
+    got_cols = lax.all_to_all(col_factor, "cy", 0, 0, tiled=True)
+    row_pieces = got_rows.reshape(group, frame_count, spread, pair, block_rows)
+    col_pieces = got_cols.reshape(group, frame_count, ring, block_cols)
     core = lax.axis_index("cc")
     keep, send = [
         jnp.einsum(

time: 192 us -> 170 us (0.89)
  waiting for transfers between devices: 65.4 us -> 35.9 us
  starting transfers between devices: 57.6 us -> 62.7 us
  local copies, waits for them, and re-layouts: 25.4 us -> 27.7 us
    all_to_all x1 -> x2, waiting for transfers between devices: 33.8 us -> 5.47 us  [the longest x1 5.47 us: weight_gradient(): got_cols = lax.all_to_all(col_factor, 'cy', 0, 0, tiled=True)]
    ppermute x1, starting transfers between devices: 3.36 us -> 15.2 us  [weight_gradient(): half = keep + lax.ppermute(send, 'cc', [(0, 1), (1, 0)])]
    all_to_all x1, starting transfers between devices: 11.7 us -> 4.2 us  [weight_gradient(): part = jnp.sum(lax.all_to_all(half, 'cx', 0, 0, tiled=True), axis=0)]
    all_to_all x1 -> x2, starting transfers between devices: 10.4 us -> 13.7 us  [the longest x1 6.98 us: weight_gradient(): got_rows = lax.all_to_all(row_factor, 'cy', 0, 0, tiled=True)]
    slice x2 -> x0, local copies, waits for them, and re-layouts: 2.32 us -> none  [the longest x1 1.3 us: weight_gradient(): got[..., :model_width].reshape(group, frame_count, spread, pair, block_rows)]
    broadcast_in_dim x1, local copies, waits for them, and re-layouts: 0.14 us -> 2.1 us  [weight_gradient(): jnp.broadcast_to(frame_rows[None], (group, frame_count, model_width))]
    unnamed x19 -> x17, local copies, waits for them, and re-layouts: 4.28 us -> 4.27 us
  transfers between devices with their start and end apart: 8 -> 9, of which waited for: 5 -> 4; matrix products, arithmetic and copies ran while one was open for 13% -> 29% of each run, Pallas kernels for 0% -> 0%
where the time goes in v15:
time: 170 us; the launch traced here: 168 us
  starting transfers between devices  62.7 us (37%)
  waiting for transfers between devices  35.9 us (21%)
  matrix products  29.2 us (17%)
  local copies, waits for them, and re-layouts  27.7 us (16%)
  other arithmetic  11.4 us (7%)
    all_to_all x1, waiting for transfers between devices, weight_gradient(): part = jnp.sum(lax.all_to_all(half, 'cx', 0, 0, tiled=True), axis=0)  19.4 us
    all_to_all x1, starting transfers between devices, weight_gradient(): summed = jnp.sum(lax.all_to_all(part, CALLS[:2], 0, 0, tiled=True), axis=0)  18.2 us
    ppermute x1, starting transfers between devices, weight_gradient(): half = keep + lax.ppermute(send, 'cc', [(0, 1), (1, 0)])  15.2 us
    all_to_all x1, waiting for transfers between devices, weight_gradient(): summed = jnp.sum(lax.all_to_all(part, CALLS[:2], 0, 0, tiled=True), axis=0)  9.48 us
    ppermute x2, starting transfers between devices, with_halo(): lax.ppermute(tail, axis, [(i, (i + 1) % count) for i in range(ends)])  8.85 us
    reshape x2, local copies, waits for them, and re-layouts, weight_gradient(): keep, send = [jnp.einsum('sfna,sfxb->xnab', lax.dynamic_index_in_dim(row_...  6.98 us
    all_to_all x1, starting transfers between devices, weight_gradient(): got_rows = lax.all_to_all(row_factor, 'cy', 0, 0, tiled=True)  6.98 us
    all_to_all x1, starting transfers between devices, weight_gradient(): got_cols = lax.all_to_all(col_factor, 'cy', 0, 0, tiled=True)  6.69 us
  transfers between devices with their start and end apart: 9, of which 4 were waited for; matrix products, arithmetic and copies ran while one was open for 29% of the time, Pallas kernels for 0%

profile of v15, /device:TPU:1, one launch (start us, length us, event | category | flops | bytes accessed | tf_op | source)
XLA Modules:
  0.0 168.5 jit_solution(229825104663649272)
XLA Ops:
  0.6 1.9 %copy-done = bf16[1024,1536]{1,0:T(8,128)(2,1)S(1)} copy-done((bf16[1024,1536]{1,0:T(8,128)(2,1)S(1)}, bf16[1024,1536]{1,0:T(8,128)(2,1)}, u32[]{:S(2)}) %copy-start) | copy-done | bytes 3145752
  6.1 5.5 %collective-permute-start = (bf16[128,1024]{1,0:T(8,128)(2,1)}, bf16[128,1024]{1,0:T(8,128)(2,1)}, u32[]{:S(2)}, u32[]{:S(2)}) collective-permute-start(bf16[128,1024]{1,0:T(8,128)(2,1)} %slice.32), channel_id=1, source_target_pairs={{0,1},{1,2},{2,3},{3,4},{4,5},{5,6},{6,7},{7,8},{8,9},{9,10},{10,1... | collective-permute-start | bytes 786440 | tf_op jit(solution)/shard_map/ppermute | solution.py:22
  13.3 2.1 %broadcast_in_dim.31 = bf16[4,128,1024]{1,2,0:T(8,128)(2,1)} broadcast(bf16[128,1024]{0,1:T(8,128)(2,1)} %copy.54), dimensions={1,2} | broadcast | bytes 1310720 | tf_op jit(solution)/shard_map/broadcast_in_dim | solution.py:92
  15.4 7.0 %all-to-all-start.1 = ((bf16[4,128,1024]{1,2,0:T(8,128)(2,1)}), bf16[4,128,1024]{1,2,0:T(8,128)(2,1)}, u32[]{:S(2)}, u32[]{:S(2)}) async-start(bf16[4,128,1024]{1,2,0:T(8,128)(2,1)} %broadcast_in_dim.31), calls=%async_computation.1 | async-start | bytes 2097152 | tf_op jit(solution)/shard_map/all_to_all | solution.py:93
  32.5 2.3 %fusion.26 = f32[4,128,384]{2,1,0:T(8,128)} fusion(bf16[48,4,8,128]{3,2,1,0:T(8,128)(2,1)} %get-tuple-element.22, bf16[128,4,128]{0,2,1:T(8,128)(2,1)} %bitcast.80, pred[128]{0:T(512)(128)(4,1)S(1)} %get-tuple-element.16), kind=kOutput, calls=%fused_computation.36 | convolution fusion | flops 50397184 | bytes 1310848 | tf_op jit(solution)/shard_map/fhd,shd->hfs/dot_general | solution.py:60
  34.8 2.3 %fusion.57 = (f32[4,128]{1,0:T(4,128)S(1)}, f32[4,128,384]{2,1,0:T(8,128)}) fusion(bf16[128,4,128]{0,2,1:T(8,128)(2,1)} %bitcast.88, bf16[384,4,128]{0,2,1:T(8,128)(2,1)} %bitcast.84, pred[128,384]{1,0:T(8,128)(4,1)} %fusion.39), kind=kOutput, calls=%fused_computation.77 | convolution fusion | flops 51118464 | bytes 1361920 | tf_op jit(solution)/shard_map/sub | solution.py:52
  37.1 5.4 %fusion.12 = f32[4,128,384]{2,1,0:T(8,128)} fusion(bf16[128,4,128]{0,2,1:T(8,128)(2,1)S(1)} %bitcast.90, f32[4,128,384]{2,1,0:T(8,128)} %fusion.26, f32[4,128,384]{2,1,0:T(8,128)} %get-tuple-element.24, f32[4,128]{1,0:T(4,128)S(1)} %get-tuple-element.23), kind=kOutput, calls=%fused_computation.22 | convolution fusion | flops 51708800 | bytes 2492416 | tf_op jit(solution)/shard_map/hfs,fhd->shd/dot_general | solution.py:68
  42.5 2.5 %fusion.34 = f32[4,128,384]{2,1,0:T(8,128)} fusion(bf16[128,4,128]{0,2,1:T(8,128)(2,1)S(1)} %bitcast.81, pred[128]{0:T(512)(128)(4,1)S(1)} %get-tuple-element.16, f32[4,128]{1,0:T(4,128)S(1)} %get-tuple-element.23, bf16[128,4,128]{0,2,1:T(8,128)(2,1)S(1)} %bitcast.91, bf16[384,4,128]{0,2,1:T(8,128)(2,1)} %bitcast.85, pred[128,384]{1,0:T(8,128)(4,1)} %fusion.39), kind=kOutput, calls=%fused_computation.47 | convolution fusion | flops 101712768 | bytes 1493120 | tf_op jit(solution)/shard_map/hfs,fhd->shd/dot_general | solution.py:71
  47.3 3.4 %collective-permute-start.2 = (bf16[128,1024]{0,1:T(8,128)(2,1)}, bf16[128,1024]{0,1:T(8,128)(2,1)S(1)}, u32[]{:S(2)}, u32[]{:S(2)}) collective-permute-start(bf16[128,1024]{0,1:T(8,128)(2,1)} %get-tuple-element.19), channel_id=1, source_target_pairs={{0,1},{1,2},{2,3},{3,4},{4,5},{5,6},{6,7},{7,8},{8,9},{9,10},{10,1... | collective-permute-start | bytes 786440 | tf_op jit(solution)/shard_map/ppermute | solution.py:22
  51.9 4.5 %convolution_convert_fusion.2 = bf16[4,128,128]{2,1,0:T(8,128)(2,1)S(1)} fusion(bf16[384,4,128]{0,2,1:T(8,128)(2,1)} %bitcast.86, f32[4,128,384]{2,1,0:T(8,128)} %fusion.26, f32[4,128,384]{2,1,0:T(8,128)} %get-tuple-element.24, f32[4,128]{1,0:T(4,128)S(1)} %get-tuple-element.23), kind=kOutput, calls=%fused_computation.21 | convolution fusion | flops 51774336 | bytes 2099200 | tf_op jit(solution)/shard_map/hfs,shd->fhd/dot_general | solution.py:65
  60.8 6.7 %all-to-all-start = ((bf16[4,128,384]{1,2,0:T(8,128)(2,1)}), bf16[4,128,384]{1,2,0:T(8,128)(2,1)S(1)}, u32[]{:S(2)}, u32[]{:S(2)}) async-start(bf16[4,128,384]{1,2,0:T(8,128)(2,1)} %bitcast.77), calls=%async_computation | async-start | bytes 786432 | tf_op jit(solution)/shard_map/all_to_all | solution.py:94
  67.5 2.3 %constant_dynamic-slice_fusion = (bf16[4,128,16,1,32]{1,4,3,2,0:T(8,128)(2,1)}, bf16[4,128,16,1,32]{1,4,3,2,0:T(8,128)(2,1)}) fusion(bf16[4,128,16,2,32]{1,4,3,2,0:T(8,128)(2,1)} %bitcast.17, s32[]{:T(128)S(6)} %select_n.19, s32[]{:T(128)S(6)} %select_n.18), kind=kLoop, calls=%fused_computation.60 | loop fusion | bytes 2097160 | tf_op jit(solution)/shard_map/jit(dynamic_index_in_dim)/dynamic_slice | solution.py:101
  69.8 5.5 %all-to-all-done = bf16[4,128,384]{1,2,0:T(8,128)(2,1)S(1)} async-done(((bf16[4,128,384]{1,2,0:T(8,128)(2,1)}), bf16[4,128,384]{1,2,0:T(8,128)(2,1)S(1)}, u32[]{:S(2)}, u32[]{:S(2)}) %all-to-all-start) | async-done | bytes 393248 | tf_op jit(solution)/shard_map/all_to_all | solution.py:94
  75.2 3.1 %convolution_bitcast_fusion = f32[8,16,32,48]{3,2,1,0:T(8,128)} fusion(bf16[4,128,16,1,32]{1,4,3,2,0:T(8,128)(2,1)} %get-tuple-element.17, bf16[4,128,8,48,1]{1,3,2,0,4:T(8,128)(2,1)S(1)} %bitcast.71), kind=kOutput, calls=%fused_computation.6 | convolution fusion | flops 201326592 | bytes 1703936 | tf_op jit(solution)/shard_map/sfna,sfxb->xnab/dot_general | solution.py:99
  78.3 3.5 %reshape.190 = f32[8,16,1536]{2,1,0:T(8,128)} reshape(f32[8,16,32,48]{3,2,1,0:T(8,128)} %convolution_bitcast_fusion) | data formatting | bytes 1572864 | tf_op jit(solution)/shard_map/reshape | solution.py:104
  81.8 15.2 %collective-permute-start.4 = (f32[8,16,1536]{2,1,0:T(8,128)}, f32[8,16,1536]{2,1,0:T(8,128)}, u32[]{:S(2)}, u32[]{:S(2)}) collective-permute-start(f32[8,16,1536]{2,1,0:T(8,128)} %reshape.190), channel_id=1, source_target_pairs={{0,32},{32,0},{1,33},{33,1},{2,34},{34,2},{3,35},{35,3},{4,36},{36... | collective-permute-start | bytes 2359304 | tf_op jit(solution)/shard_map/ppermute | solution.py:107
  97.0 3.1 %convolution_bitcast_fusion.1 = f32[8,16,32,48]{3,2,1,0:T(8,128)} fusion(bf16[4,128,16,1,32]{1,4,3,2,0:T(8,128)(2,1)} %get-tuple-element.18, bf16[4,128,8,48,1]{1,3,2,0,4:T(8,128)(2,1)S(1)} %bitcast.72), kind=kOutput, calls=%fused_computation.7 | convolution fusion | flops 201326592 | bytes 1703936 | tf_op jit(solution)/shard_map/sfna,sfxb->xnab/dot_general | solution.py:99
  100.1 3.5 %reshape.189 = f32[8,16,1536]{2,1,0:T(8,128)} reshape(f32[8,16,32,48]{3,2,1,0:T(8,128)} %convolution_bitcast_fusion.1) | data formatting | bytes 1572864 | tf_op jit(solution)/shard_map/reshape | solution.py:104
  103.6 2.3 %add.63 = f32[8,16,1536]{2,1,0:T(8,128)} add(f32[8,16,1536]{2,1,0:T(8,128)} %reshape.189, f32[8,16,1536]{2,1,0:T(8,128)} %collective-permute-done.4) | non-fusion elementwise | flops 196608 | bytes 2359296 | tf_op jit(solution)/shard_map/add | solution.py:107
  106.0 4.2 %all-to-all-start.2 = ((f32[8,16,1536]{2,1,0:T(8,128)}), f32[8,16,1536]{2,1,0:T(8,128)}, u32[]{:S(2)}, u32[]{:S(2)}) async-start(f32[8,16,1536]{2,1,0:T(8,128)} %add.63), calls=%async_computation.2 | async-start | bytes 1572864 | tf_op jit(solution)/shard_map/all_to_all | solution.py:108
  110.2 2.6 %fusion.11 = bf16[4,128,128]{2,1,0:T(8,128)(2,1)} fusion(bf16[48,4,8,128]{3,2,1,0:T(8,128)(2,1)} %get-tuple-element.22, f32[128]{0:T(128)S(1)} %copy-done.7, f32[4,128]{1,0:T(4,128)S(1)} %get-tuple-element.23, bf16[128,4,128]{0,2,1:T(8,128)(2,1)} %bitcast.89, bf16[384,4,128]{0,2,1:T(8,128)(2,1)} %bitcast.87, pred[128,384]{1,0:T(8,128)(4,1)} %fusion.39), kind=kOutput, calls=%fused_computation.20 | convolution fusion | flops 101778304 | bytes 1100288 | tf_op jit(solution)/shard_map/hfs,shd->fhd/dot_general | solution.py:56
  114.4 19.4 %all-to-all-done.2 = f32[8,16,1536]{2,1,0:T(8,128)} async-done(((f32[8,16,1536]{2,1,0:T(8,128)}), f32[8,16,1536]{2,1,0:T(8,128)}, u32[]{:S(2)}, u32[]{:S(2)}) %all-to-all-start.2) | async-done | bytes 786464 | tf_op jit(solution)/shard_map/all_to_all | solution.py:108
  137.2 18.2 %all-to-all-start.3 = ((f32[16,1,1536]{2,1,0:T(1,128)}), f32[16,1,1536]{2,1,0:T(1,128)}, u32[]{:S(2)}, u32[]{:S(2)}) async-start(f32[16,1,1536]{2,1,0:T(1,128)} %all_to_all.18), calls=%async_computation.3 | async-start | bytes 196608 | tf_op jit(solution)/shard_map/all_to_all | solution.py:109
  157.4 9.5 %all-to-all-done.3 = f32[16,1,1536]{2,1,0:T(1,128)} async-done(((f32[16,1,1536]{2,1,0:T(1,128)}), f32[16,1,1536]{2,1,0:T(1,128)}, u32[]{:S(2)}, u32[]{:S(2)}) %all-to-all-start.3) | async-done | bytes 98336 | tf_op jit(solution)/shard_map/all_to_all | solution.py:109
  (48 shorter events, 31.2 us)
Async XLA Ops:
  0.6 1.9 %copy-start = (bf16[1024,1536]{1,0:T(8,128)(2,1)S(1)}, bf16[1024,1536]{1,0:T(8,128)(2,1)}, u32[]{:S(2)}) copy-start(bf16[1024,1536]{1,0:T(8,128)(2,1)} %param.5) | copy-start | bytes 9437188
  4.8 24.7 %collective-permute-start.1 = (bf16[128,1024]{1,0:T(8,128)(2,1)}, bf16[128,1024]{1,0:T(8,128)(2,1)}, u32[]{:S(2)}, u32[]{:S(2)}) collective-permute-start(bf16[128,1024]{1,0:T(8,128)(2,1)} %slice.32), channel_id=1, source_target_pairs={{1,0},{2,1},{3,2},{4,3},{5,4},{6,5},{7,6},{8,7},{9,8},{10,9},{11,1... | collective-permute-start | bytes 786440 | tf_op jit(solution)/shard_map/ppermute | solution.py:24
  6.1 23.5 %collective-permute-start = (bf16[128,1024]{1,0:T(8,128)(2,1)}, bf16[128,1024]{1,0:T(8,128)(2,1)}, u32[]{:S(2)}, u32[]{:S(2)}) collective-permute-start(bf16[128,1024]{1,0:T(8,128)(2,1)} %slice.32), channel_id=1, source_target_pairs={{0,1},{1,2},{2,3},{3,4},{4,5},{5,6},{6,7},{7,8},{8,9},{9,10},{10,1... | collective-permute-start | bytes 786440 | tf_op jit(solution)/shard_map/ppermute | solution.py:22
  15.4 45.4 %all-to-all-start.1 = ((bf16[4,128,1024]{1,2,0:T(8,128)(2,1)}), bf16[4,128,1024]{1,2,0:T(8,128)(2,1)}, u32[]{:S(2)}, u32[]{:S(2)}) async-start(bf16[4,128,1024]{1,2,0:T(8,128)(2,1)} %broadcast_in_dim.31), calls=%async_computation.1 | async-start | bytes 2097152 | tf_op jit(solution)/shard_map/all_to_all | solution.py:93
  32.5 4.6 %copy-start.6 = (bf16[128,512]{0,1:T(8,128)(2,1)S(1)}, bf16[128,512]{0,1:T(8,128)(2,1)}, u32[]{:S(2)}) copy-start(bf16[128,512]{0,1:T(8,128)(2,1)} %copy.70) | copy-start | bytes 393220
  37.1 5.4 %copy-start.3 = (bf16[1,128,512]{1,2,0:T(8,128)(2,1)S(1)}, bf16[1,128,512]{1,2,0:T(8,128)(2,1)}, u32[]{:S(2)}) copy-start(bf16[1,128,512]{1,2,0:T(8,128)(2,1)} %copy.65) | copy-start | bytes 393220
  47.3 9.2 %collective-permute-start.2 = (bf16[128,1024]{0,1:T(8,128)(2,1)}, bf16[128,1024]{0,1:T(8,128)(2,1)S(1)}, u32[]{:S(2)}, u32[]{:S(2)}) collective-permute-start(bf16[128,1024]{0,1:T(8,128)(2,1)} %get-tuple-element.19), channel_id=1, source_target_pairs={{0,1},{1,2},{2,3},{3,4},{4,5},{5,6},{6,7},{7,8},{8,9},{9,10},{10,1... | collective-permute-start | bytes 786440 | tf_op jit(solution)/shard_map/ppermute | solution.py:22
  50.6 7.4 %collective-permute-start.3 = (bf16[128,1024]{0,1:T(8,128)(2,1)}, bf16[128,1024]{0,1:T(8,128)(2,1)}, u32[]{:S(2)}, u32[]{:S(2)}) collective-permute-start(bf16[128,1024]{0,1:T(8,128)(2,1)} %get-tuple-element.20), channel_id=1, source_target_pairs={{1,0},{2,1},{3,2},{4,3},{5,4},{6,5},{7,6},{8,7},{9,8},{10,9},{11,1... | collective-permute-start | bytes 786440 | tf_op jit(solution)/shard_map/ppermute | solution.py:24
  56.5 4.3 %copy-start.4 = (bf16[4,128,128]{2,1,0:T(8,128)(2,1)}, bf16[4,128,128]{2,1,0:T(8,128)(2,1)S(1)}, u32[]{:S(2)}) copy-start(bf16[4,128,128]{2,1,0:T(8,128)(2,1)S(1)} %convolution_convert_fusion.2) | copy-start | bytes 393220
  59.3 0.7 copy-start.1
  60.8 14.4 %all-to-all-start = ((bf16[4,128,384]{1,2,0:T(8,128)(2,1)}), bf16[4,128,384]{1,2,0:T(8,128)(2,1)S(1)}, u32[]{:S(2)}, u32[]{:S(2)}) async-start(bf16[4,128,384]{1,2,0:T(8,128)(2,1)} %bitcast.77), calls=%async_computation | async-start | bytes 786432 | tf_op jit(solution)/shard_map/all_to_all | solution.py:94
  81.8 21.8 %collective-permute-start.4 = (f32[8,16,1536]{2,1,0:T(8,128)}, f32[8,16,1536]{2,1,0:T(8,128)}, u32[]{:S(2)}, u32[]{:S(2)}) collective-permute-start(f32[8,16,1536]{2,1,0:T(8,128)} %reshape.190), channel_id=1, source_target_pairs={{0,32},{32,0},{1,33},{33,1},{2,34},{34,2},{3,35},{35,3},{4,36},{36... | collective-permute-start | bytes 2359304 | tf_op jit(solution)/shard_map/ppermute | solution.py:107
  103.6 6.6 %copy-start.7 = (f32[128]{0:T(128)S(1)}, f32[128]{0:T(128)}, u32[]{:S(2)}) copy-start(f32[128]{0:T(128)} %get-tuple-element.15) | copy-start | bytes 1540
  106.0 27.9 %all-to-all-start.2 = ((f32[8,16,1536]{2,1,0:T(8,128)}), f32[8,16,1536]{2,1,0:T(8,128)}, u32[]{:S(2)}, u32[]{:S(2)}) async-start(f32[8,16,1536]{2,1,0:T(8,128)} %add.63), calls=%async_computation.2 | async-start | bytes 1572864 | tf_op jit(solution)/shard_map/all_to_all | solution.py:108
  110.2 45.3 %copy-start.2 = (bf16[128,1024]{0,1:T(8,128)(2,1)S(1)}, bf16[128,1024]{0,1:T(8,128)(2,1)}, u32[]{:S(2)}) copy-start(bf16[128,1024]{0,1:T(8,128)(2,1)} %copy-done.1) | copy-start | bytes 786436
  110.2 45.3 %copy-start.5 = (bf16[4,128,128]{2,1,0:T(8,128)(2,1)S(1)}, bf16[4,128,128]{2,1,0:T(8,128)(2,1)}, u32[]{:S(2)}) copy-start(bf16[4,128,128]{2,1,0:T(8,128)(2,1)} %copy-done.4) | copy-start | bytes 393220
  137.2 29.6 %all-to-all-start.3 = ((f32[16,1,1536]{2,1,0:T(1,128)}), f32[16,1,1536]{2,1,0:T(1,128)}, u32[]{:S(2)}, u32[]{:S(2)}) async-start(f32[16,1,1536]{2,1,0:T(1,128)} %all_to_all.18), calls=%async_computation.3 | async-start | bytes 196608 | tf_op jit(solution)/shard_map/all_to_all | solution.py:109
